TPU v7x, 128 devices: a whole 4x4x4 slice. The times are simulated.
128 devices in a mesh: table: 4 (over y), blk: 32 (over z, x, core).
Axes of the slice: x: 4, y: 4, z: 4, core: 2. Of those that a mesh axis runs over, the one named last changes fastest.
Arguments:
- residual: bfloat16 [4, 4096, 512], P('table', 'blk'), may hold values from -6 to 6
- queries: bfloat16 [4, 4096, 512], P('table', 'blk'), may hold values from -26 to 26
- key_rows: bfloat16 [4, 4096, 512], P('table', 'blk'), may hold values from -26 to 26
- value_rows: bfloat16 [4, 4096, 512], P('table', 'blk'), may hold values from -6 to 6
- w_out: bfloat16 [512, 512], replicated, may hold values from -0.25 to 0.25
- expert_ids: int32 [4, 4096, 2], P('table', 'blk'), may hold values from 0 to 63, all different within a row; in each aligned block of 128 rows (0 to 127, 128 to 255, ..., all dimensions but the last counted through in order) at most 12 rows name the same one
- route_gates: float32 [4, 4096, 2], P('table', 'blk'), may hold values from 0.2 to 1
- cotangent: bfloat16 [4, 4096, 512], P('table', 'blk'), may hold values from -6 to 6
- w_gate: bfloat16 [128, 512, 1024], P(('table', 'blk')), may hold values from -0.25 to 0.25
- w_up: bfloat16 [128, 512, 1024], P(('table', 'blk')), may hold values from -0.25 to 0.25
- w_down: bfloat16 [128, 1024, 512], P(('table', 'blk')), may hold values from -0.125 to 0.125
Outputs:
- block_out: bfloat16 [4, 4096, 512], P('table', 'blk')
- grad_stream: bfloat16 [4, 4096, 512], P('table', 'blk')
- grad_gate: bfloat16 [128, 512, 1024], P(('table', 'blk'))
- grad_up: bfloat16 [128, 512, 1024], P(('table', 'blk'))
- grad_down: bfloat16 [128, 1024, 512], P(('table', 'blk'))
Inputs may be any that keep to these rules, and one draw needn't show every extreme that they name: `expert_ids`: each row names 2 different experts; in the rows of one device (aligned blocks of 128 rows of a table) no expert is named by more than 12 rows, a bound that some block reaches.
All inputs are finite; a program needn't handle non-finite values.
Results may differ from a plain program's by a relative error of at most 0.011.
Values may be sent and summed in bfloat16 or wider, within the bound.
No kernel may reach another device: no remote copies, remote signals or barrier semaphores. Data moves between devices by JAX's collectives and lax.ppermute only.
A program may use at most 128 MiB of HBM per device.

v0:
```python
import math

import jax
import jax.numpy as jnp
from jax import lax
from jax.experimental import pallas as pl
from jax.experimental.pallas import tpu as pltpu
from jax.sharding import PartitionSpec as P


D = 512
HEADS = 8
HEAD = 64
EXPERTS = 64
TOP = 2
PIECES = 2
CAP = 12


def silu_grad(pre):
    sig = jax.nn.sigmoid(pre)
    return sig * (1.0 + pre * (1.0 - sig))


def to_experts(buffer):
    return lax.all_to_all(buffer, ("table", "blk"), split_axis=0, concat_axis=0, tiled=True)


def to_anchor(buffer):
    return lax.all_to_all(buffer, ("table", "blk"), split_axis=0, concat_axis=0, tiled=True)


def forward_part(arrived, w_gate, w_up, w_down):
    pre_gate = jnp.einsum("svcd,vdf->svcf", arrived, w_gate, preferred_element_type=jnp.float32)
    pre_up = jnp.einsum("svcd,vdf->svcf", arrived, w_up, preferred_element_type=jnp.float32)
    activated = jax.nn.silu(pre_gate)
    hidden = (activated * pre_up).astype(jnp.bfloat16)
    outputs = jnp.einsum(
        "svcf,vfd->svcd", hidden, w_down, preferred_element_type=jnp.float32
    ).astype(jnp.bfloat16)
    return (outputs, pre_gate, pre_up, activated, hidden)


def backward_part(arrived, arrived_cots, pre_gate, pre_up, activated, hidden, w_gate, w_up, w_down):
    grad_hidden = jnp.einsum(
        "svcd,vfd->svcf", arrived_cots, w_down, preferred_element_type=jnp.float32
    )
    grad_pre_gate = (grad_hidden * pre_up * silu_grad(pre_gate)).astype(jnp.bfloat16)
    grad_pre_up = (grad_hidden * activated).astype(jnp.bfloat16)
    grad_down = jnp.einsum(
        "svcf,svcd->vfd", hidden, arrived_cots, preferred_element_type=jnp.float32
    ).astype(jnp.bfloat16)
    grad_gate = jnp.einsum(
        "svcd,svcf->vdf", arrived, grad_pre_gate, preferred_element_type=jnp.float32
    ).astype(jnp.bfloat16)
    grad_up = jnp.einsum(
        "svcd,svcf->vdf", arrived, grad_pre_up, preferred_element_type=jnp.float32
    ).astype(jnp.bfloat16)
    grad_inputs = (
        jnp.einsum("svcf,vdf->svcd", grad_pre_gate, w_gate, preferred_element_type=jnp.float32)
        + jnp.einsum("svcf,vdf->svcd", grad_pre_up, w_up, preferred_element_type=jnp.float32)
    ).astype(jnp.bfloat16)
    return (grad_inputs, grad_gate, grad_up, grad_down)


def partner_pairs():
    devices = lax.psum(1, "blk")
    return [(b, b ^ 1) for b in range(devices)]


def dispatch(slots):
    width = slots.shape[1] // PIECES
    parts = jnp.transpose(slots.reshape(EXPERTS, CAP, PIECES, width), (0, 2, 1, 3))
    got = to_experts(parts.reshape(EXPERTS * PIECES, CAP, width))
    other = lax.ppermute(got, "blk", partner_pairs())
    first = lax.axis_index("blk") % 2 == 0
    return jnp.concatenate(
        [jnp.where(first, got, other), jnp.where(first, other, got)], axis=-1
    )


def give_back(outputs, grads):
    first = lax.axis_index("blk") % 2 == 0
    keep = jnp.where(first, outputs, grads)
    other = lax.ppermute(jnp.where(first, grads, outputs), "blk", partner_pairs())
    summed = (keep.astype(jnp.float32) + other.astype(jnp.float32)).astype(jnp.bfloat16)
    back = to_anchor(summed).reshape(EXPERTS, PIECES, CAP, -1)
    return back[:, 0].reshape(EXPERTS * CAP, -1), back[:, 1].reshape(EXPERTS * CAP, -1)


def attend_heads(query_rows, key_rows, value_rows):
    rows = query_rows.shape[0]
    devices = lax.psum(1, "blk")
    groups = devices // HEADS
    part = rows // groups
    scale = 1.0 / math.sqrt(HEAD)

    def by_head(block):
        heads = jnp.transpose(block.reshape(rows, HEADS, HEAD), (1, 0, 2))
        return jnp.broadcast_to(heads[:, None], (HEADS, groups, rows, HEAD)).reshape(devices, rows, HEAD)

    pairs = jnp.concatenate([by_head(key_rows), by_head(value_rows)], axis=-1)
    asked = jnp.transpose(query_rows.reshape(groups, part, HEADS, HEAD), (2, 0, 1, 3))
    asked = asked.reshape(devices, part, HEAD)
    asked = jnp.concatenate([asked, jnp.zeros_like(asked)], axis=-1)
    parcel = jnp.concatenate([pairs, asked], axis=1)
    got = lax.all_to_all(parcel, "blk", 0, 0, tiled=True)
    steps = 4
    chunk = devices // steps

    def kernel(got_ref, out_ref):
        step = pl.program_id(0)
        pairs_all = got_ref[:, :rows, :].reshape(devices * rows, 2 * HEAD)
        asked_now = got_ref[pl.ds(step * chunk, chunk), rows:, :].reshape(chunk * part, 2 * HEAD)
        scores = lax.dot_general(
            asked_now, pairs_all, (((1,), (1,)), ((), ())), preferred_element_type=jnp.float32
        ) * scale
        highest = jnp.max(scores, axis=-1, keepdims=True)
        expo = jnp.exp(scores - highest)
        denom = jnp.sum(expo, axis=-1, keepdims=True)
        totals = jnp.dot(expo.astype(jnp.bfloat16), pairs_all, preferred_element_type=jnp.float32)
        out_ref[...] = (totals[:, HEAD:] / denom).astype(jnp.bfloat16).reshape(chunk, part, HEAD)

    queries_total = devices * part
    keys_total = devices * rows
    mixed = pl.pallas_call(
        kernel,
        grid=(steps,),
        in_specs=[pl.BlockSpec(got.shape, lambda i: (0, 0, 0))],
        out_specs=pl.BlockSpec((chunk, part, HEAD), lambda i: (i, 0, 0)),
        out_shape=jax.ShapeDtypeStruct((devices, part, HEAD), jnp.bfloat16),
        compiler_params=pltpu.CompilerParams(vmem_limit_bytes=48 * 1024 * 1024),
        cost_estimate=pl.CostEstimate(
            flops=4 * queries_total * keys_total * 2 * HEAD,
            transcendentals=queries_total * keys_total,
            bytes_accessed=got.size * 2 + queries_total * HEAD * 2,
        ),
    )(got)
    back = lax.all_to_all(mixed, "blk", 0, 0, tiled=True)
    back = jnp.transpose(back.reshape(HEADS, groups, part, HEAD), (1, 2, 0, 3))
    return back.reshape(rows, HEADS * HEAD)


def block(
    residual,
    queries,
    key_rows,
    value_rows,
    w_out,
    expert_ids,
    route_gates,
    cotangent,
    w_gate,
    w_up,
    w_down,
):
    row_count = queries.shape[1]
    route_experts = expert_ids[0].reshape(-1)
    gates = route_gates[0].reshape(-1)
    onehot = (route_experts[:, None] == jnp.arange(EXPERTS, dtype=jnp.int32)[None, :]).astype(
        jnp.int32
    )
    before = jnp.cumsum(onehot, axis=0) - onehot
    position = jnp.sum(before * onehot, axis=1)
    slot_index = route_experts * CAP + position
    grad_flat = cotangent[0].astype(jnp.float32)
    route_cots = (gates[:, None] * jnp.repeat(grad_flat, TOP, axis=0)).astype(jnp.bfloat16)
    cot_slots = jnp.zeros((EXPERTS * CAP, D), jnp.bfloat16).at[slot_index].set(route_cots)
    arrived_cots = dispatch(cot_slots).reshape(-1, w_gate.shape[0], CAP, D)
    attended = attend_heads(queries[0], key_rows[0], value_rows[0])
    stream = residual[0].astype(jnp.float32) + jnp.dot(
        attended, w_out, preferred_element_type=jnp.float32
    )
    radius = jnp.sqrt(jnp.mean(stream * stream, axis=-1, keepdims=True) + 1e-06)
    unit = stream / radius
    normed = unit.astype(jnp.bfloat16)
    local_pieces = w_gate.shape[0]
    in_slots = jnp.zeros((EXPERTS * CAP, D), jnp.bfloat16).at[slot_index].set(
        jnp.repeat(normed, TOP, axis=0)
    )
    arrived = dispatch(in_slots).reshape(-1, local_pieces, CAP, D)
    outputs, pre_gate, pre_up, activated, hidden = forward_part(arrived, w_gate, w_up, w_down)
    grad_inputs, grad_gate, grad_up, grad_down = backward_part(
        arrived, arrived_cots, pre_gate, pre_up, activated, hidden, w_gate, w_up, w_down
    )
    out_slots, grad_slots = give_back(outputs[:, 0], grad_inputs[:, 0])
    route_out = out_slots.astype(jnp.float32)[slot_index]
    route_grad = grad_slots.astype(jnp.float32)[slot_index]
    moe = jnp.sum((gates[:, None] * route_out).reshape(row_count, TOP, D), axis=1)
    block_out = (stream + moe).astype(jnp.bfloat16)[None]
    grad_unit = jnp.sum(route_grad.reshape(row_count, TOP, D), axis=1)
    grad_stream = (
        grad_flat + (grad_unit - unit * jnp.mean(grad_unit * unit, axis=-1, keepdims=True)) / radius
    )
    return (block_out, grad_stream.astype(jnp.bfloat16)[None], grad_gate, grad_up, grad_down)


def solution(mesh):
    return jax.shard_map(
        block,
        mesh=mesh,
        in_specs=(
            P("table", "blk", None),
            P("table", "blk", None),
            P("table", "blk", None),
            P("table", "blk", None),
            P(),
            P("table", "blk", None),
            P("table", "blk", None),
            P("table", "blk", None),
            P(("table", "blk"), None, None),
            P(("table", "blk"), None, None),
            P(("table", "blk"), None, None),
        ),
        out_specs=(
            P("table", "blk", None),
            P("table", "blk", None),
            P(("table", "blk"), None, None),
            P(("table", "blk"), None, None),
            P(("table", "blk"), None, None),
        ),
        check_vma=False,
    )
```

profile of v0, /device:TPU:1, one launch (start us, length us, event | category | flops | bytes accessed | tf_op | source)
XLA Modules:
  0.0 180.9 jit_solution(12880855269817031520)
XLA Ops:
  4.8 1.7 fusion.26
  6.5 9.6 %all-to-all-start = ((bf16[32,160,128]{2,1,0:T(8,128)(2,1)}), bf16[32,160,128]{2,1,0:T(8,128)(2,1)S(1)}, u32[]{:S(2)}, u32[]{:S(2)}) async-start(bf16[32,160,128]{2,1,0:T(8,128)(2,1)} %fusion.26), calls=%async_computation | async-start | bytes 2621440 | tf_op jit(solution)/shard_map/all_to_all | solution.py:107
  20.4 15.0 %all-to-all-done.got_ref = bf16[32,160,128]{2,1,0:T(8,128)(2,1)S(1)} async-done(((bf16[32,160,128]{2,1,0:T(8,128)(2,1)}), bf16[32,160,128]{2,1,0:T(8,128)(2,1)S(1)}, u32[]{:S(2)}, u32[]{:S(2)}) %all-to-all-start) | async-done | bytes 1310752 | tf_op jit(solution)/shard_map/all_to_all | solution.py:107
  35.4 8.3 %shard_map.146 = bf16[32,32,64]{2,1,0:T(8,128)(2,1)S(1)} custom-call(bf16[32,160,128]{2,1,0:T(8,128)(2,1)S(1)} %all-to-all-done.got_ref), custom_call_target="tpu_custom_call" | custom-call | flops 2147483648 | bytes 1441792 | tf_op jit(solution)/shard_map/pallas_call | solution.py:126
  44.5 5.0 %all-to-all-start.1 = ((bf16[32,2,1024]{2,1,0:T(2,128)(2,1)}), bf16[32,2,1024]{2,1,0:T(2,128)(2,1)S(1)}, u32[]{:S(2)}, u32[]{:S(2)}) async-start(bf16[32,2,1024]{2,1,0:T(2,128)(2,1)} %reshape.256), calls=%async_computation.1 | async-start | bytes 262144 | tf_op jit(solution)/shard_map/all_to_all | solution.py:139
  49.5 1.8 %scatter_custom_fusion.1 = bf16[768,512]{1,0:T(8,128)(2,1)S(1)} fusion(s32[256]{0:T(256)S(1)} %bitcast.198, bf16[]{:T(256)} %constant.35.clone.1, f32[256,512]{1,0:T(8,128)S(1)} %reshape.200, f32[256]{0:T(256)S(1)} %mul.85), kind=kCustom, calls=%fused_computation.62 | custom fusion | flops 262144 | bytes 1311746 | tf_op jit(solution)/shard_map/scatter | solution.py:168
  52.8 4.5 %all-to-all-done.1 = bf16[32,2,1024]{2,1,0:T(2,128)(2,1)S(1)} async-done(((bf16[32,2,1024]{2,1,0:T(2,128)(2,1)}), bf16[32,2,1024]{2,1,0:T(2,128)(2,1)S(1)}, u32[]{:S(2)}, u32[]{:S(2)}) %all-to-all-start.1) | async-done | bytes 131104 | tf_op jit(solution)/shard_map/all_to_all | solution.py:139
  57.2 5.9 %all-to-all-start.3 = ((bf16[128,12,256]{2,1,0:T(8,128)(2,1)}), bf16[128,12,256]{2,1,0:T(8,128)(2,1)S(1)}, u32[]{:S(2)}, u32[]{:S(2)}) async-start(bf16[128,12,256]{2,1,0:T(8,128)(2,1)} %bitcast.34), calls=%async_computation.3 | async-start | bytes 2097152 | tf_op jit(solution)/shard_map/all_to_all | solution.py:26
  65.4 2.5 %scatter_custom_fusion = bf16[768,512]{1,0:T(8,128)(2,1)} fusion(s32[256]{0:T(256)S(1)} %bitcast.199, bf16[256,512]{1,0:T(8,128)(2,1)S(1)} %reshape.233, bf16[]{:T(256)} %constant.35.clone.1), kind=kCustom, calls=%fused_computation.64 | custom fusion | bytes 786434 | tf_op jit(solution)/shard_map/scatter | solution.py:178
  67.8 2.2 %reshape.194 = bf16[64,12,2,256]{3,2,1,0:T(2,128)(2,1)S(1)} reshape(bf16[768,512]{1,0:T(8,128)(2,1)} %scatter_custom_fusion) | data formatting | bytes 1572864 | tf_op jit(solution)/shard_map/reshape | solution.py:73
  71.3 11.1 %all-to-all-done.3 = bf16[128,12,256]{2,1,0:T(8,128)(2,1)S(1)} async-done(((bf16[128,12,256]{2,1,0:T(8,128)(2,1)}), bf16[128,12,256]{2,1,0:T(8,128)(2,1)S(1)}, u32[]{:S(2)}, u32[]{:S(2)}) %all-to-all-start.3) | async-done | bytes 786464 | tf_op jit(solution)/shard_map/all_to_all | solution.py:26
  82.4 4.4 %all-to-all-start.2 = ((bf16[128,12,256]{2,1,0:T(8,128)(2,1)}), bf16[128,12,256]{2,1,0:T(8,128)(2,1)S(1)}, u32[]{:S(2)}, u32[]{:S(2)}) async-start(bf16[128,12,256]{2,1,0:T(8,128)(2,1)} %bitcast.188), calls=%async_computation.2 | async-start | bytes 2097152 | tf_op jit(solution)/shard_map/all_to_all | solution.py:26
  89.1 17.0 %all-to-all-done.2 = bf16[128,12,256]{2,1,0:T(8,128)(2,1)S(1)} async-done(((bf16[128,12,256]{2,1,0:T(8,128)(2,1)}), bf16[128,12,256]{2,1,0:T(8,128)(2,1)S(1)}, u32[]{:S(2)}, u32[]{:S(2)}) %all-to-all-start.2) | async-done | bytes 786464 | tf_op jit(solution)/shard_map/all_to_all | solution.py:26
  108.2 2.2 %collective-permute-done = bf16[128,12,256]{2,0,1:T(8,128)(2,1)} collective-permute-done((bf16[128,12,256]{2,0,1:T(8,128)(2,1)}, bf16[128,12,256]{2,0,1:T(8,128)(2,1)}, u32[]{:S(2)}, u32[]{:S(2)}) %collective-permute-start) | collective-permute-done | bytes 786464 | tf_op jit(solution)/shard_map/ppermute | solution.py:75
  110.5 2.4 %broadcast_select_fusion.2 = (bf16[128,12,256]{2,0,1:T(8,128)(2,1)S(1)}, bf16[128,12,256]{2,0,1:T(8,128)(2,1)S(1)}, bf16[128,12,256]{2,0,1:T(8,128)(2,1)S(1)}, bf16[128,12,256]{2,0,1:T(8,128)(2,1)S(1)}) fusion(bf16[128,12,256]{2,0,1:T(8,128)(2,1)} %collective-permute-done.1, pred[]{:T(512)S(6)} %eq.34, bf16[128,12,256]{2,0,1:T(8,128)(2,1)} %collective-permute-done, ...), kind=kLoop, calls=%fused_computation.57 | loop fusion | flops 1572864 | bytes 6291457 | tf_op jit(solution)/shard_map/jit(_where)/select_n | solution.py:78
  112.9 1.9 %fusion.29 = f32[128,12,1024]{2,0,1:T(8,128)S(1)} fusion(bf16[1,1024,512]{2,1,0:T(8,128)(2,1)S(1)} %copy-done.18, bf16[128,12,256]{2,0,1:T(8,128)(2,1)S(1)} %get-tuple-element.13, bf16[128,12,256]{2,0,1:T(8,128)(2,1)S(1)} %get-tuple-element.12), kind=kOutput, calls=%fused_computation.46 | convolution fusion | flops 1613758464 | bytes 8912896 | tf_op jit(solution)/shard_map/svcd,vfd->svcf/dot_general | solution.py:45
  114.9 1.8 fusion.37
  116.8 4.1 %fusion.9 = (bf16[128,12,1024]{2,0,1:T(8,128)(2,1)S(1)}, bf16[128,1,12,1024]{3,0,2,1:T(8,128)(2,1)S(1)}, bf16[128,12,1024]{2,0,1:T(8,128)(2,1)S(1)}) fusion(f32[128,12,1024]{2,0,1:T(8,128)S(1)} %fusion.37, f32[128,12,1024]{2,0,1:T(8,128)S(1)} %fusion.29, bf16[1,512,1024]{2,1,0:T(8,128)(2,1)S(1)} %copy-done, ...), kind=kOutput, calls=%fused_computation.19 | convolution fusion | flops 1637351424 | bytes 24641536 | tf_op jit(solution)/shard_map/svcd,vdf->svcf/dot_general | solution.py:35
  121.0 1.8 %fusion.32 = f32[128,12,512]{2,0,1:T(8,128)S(1)} fusion(bf16[128,12,1024]{2,0,1:T(8,128)(2,1)S(1)} %get-tuple-element.7, bf16[1,512,1024]{2,1,0:T(8,128)(2,1)S(1)} %copy-done), kind=kOutput, calls=%fused_computation.49 | convolution fusion | flops 1610612736 | bytes 7340032 | tf_op jit(solution)/shard_map/svcf,vdf->svcd/dot_general | solution.py:61
  123.5 1.8 convolution_convert_fusion
  125.3 2.0 %broadcast_select_fusion = (bf16[128,12,512]{2,0,1:T(8,128)(2,1)S(1)}, bf16[128,12,512]{2,0,1:T(8,128)(2,1)S(1)}) fusion(bf16[128,12,512]{2,0,1:T(8,128)(2,1)S(1)} %convolution_convert_fusion, pred[]{:T(512)S(6)} %eq.34, f32[128,12,512]{2,0,1:T(8,128)S(1)} %fusion.32, bf16[1,512,1024]{2,1,0:T(8,128)(2,1)S(1)} %copy-done.4, ...), kind=kOutput, calls=%fused_computation.36 | convolution fusion | flops 1612972032 | bytes 12058625 | tf_op jit(solution)/shard_map/svcf,vdf->svcd/dot_general | solution.py:60
  128.0 3.0 %collective-permute-done.2 = bf16[128,12,512]{2,0,1:T(8,128)(2,1)S(1)} collective-permute-done((bf16[128,12,512]{2,0,1:T(8,128)(2,1)S(1)}, bf16[128,12,512]{2,0,1:T(8,128)(2,1)S(1)}, u32[]{:S(2)}, u32[]{:S(2)}) %collective-permute-start.2) | collective-permute-done | bytes 1572896 | tf_op jit(solution)/shard_map/ppermute | solution.py:85
  131.7 2.2 %copy.90 = bf16[128,12,512]{2,1,0:T(8,128)(2,1)} copy(bf16[128,12,512]{2,0,1:T(8,128)(2,1)S(1)} %fusion.15) | data formatting | bytes 3145728 | tf_op jit(solution)/shard_map/convert_element_type | solution.py:86
  134.0 3.8 %all-to-all-start.4 = ((bf16[128,12,512]{2,1,0:T(8,128)(2,1)}), bf16[128,12,512]{2,1,0:T(8,128)(2,1)S(1)}, u32[]{:S(2)}, u32[]{:S(2)}) async-start(bf16[128,12,512]{2,1,0:T(8,128)(2,1)} %copy.90), calls=%async_computation.4 | async-start | bytes 4194304 | tf_op jit(solution)/shard_map/all_to_all | solution.py:30
  138.6 5.1 %fusion.24 = bf16[1,512,1024]{2,1,0:T(8,128)(2,1)} fusion(bf16[128,12,1024]{2,0,1:T(8,128)(2,1)} %copy-done.19, bf16[128,12,256]{2,0,1:T(8,128)(2,1)S(1)} %copy-done.10, bf16[128,12,256]{2,0,1:T(8,128)(2,1)} %copy-done.12), kind=kOutput, calls=%fused_computation.38 | convolution fusion | flops 1614282752 | bytes 5767168 | tf_op jit(solution)/shard_map/svcd,svcf->vdf/dot_general | solution.py:56
  143.7 2.8 %fusion.21 = bf16[1,512,1024]{2,1,0:T(8,128)(2,1)} fusion(bf16[128,1,12,1024]{3,0,2,1:T(8,128)(2,1)S(1)} %copy-done.3, bf16[128,12,256]{2,0,1:T(8,128)(2,1)S(1)} %copy-done.11, bf16[128,12,256]{2,0,1:T(8,128)(2,1)S(1)} %copy-done.13), kind=kOutput, calls=%fused_computation.37 | convolution fusion | flops 1614282752 | bytes 5767168 | tf_op jit(solution)/shard_map/svcd,svcf->vdf/dot_general | solution.py:53
  146.5 2.8 %fusion.25 = bf16[1,1024,512]{2,1,0:T(8,128)(2,1)} fusion(bf16[128,12,1024]{2,0,1:T(8,128)(2,1)S(1)} %copy-done.21, bf16[128,12,256]{2,0,1:T(8,128)(2,1)S(1)} %copy-done.8, bf16[128,12,256]{2,0,1:T(8,128)(2,1)S(1)} %copy-done.6), kind=kOutput, calls=%fused_computation.39 | convolution fusion | flops 1614282752 | bytes 5767168 | tf_op jit(solution)/shard_map/svcf,svcd->vfd/dot_general | solution.py:50
  149.3 19.1 %all-to-all-done.4 = bf16[128,12,512]{2,1,0:T(8,128)(2,1)S(1)} async-done(((bf16[128,12,512]{2,1,0:T(8,128)(2,1)}), bf16[128,12,512]{2,1,0:T(8,128)(2,1)S(1)}, u32[]{:S(2)}, u32[]{:S(2)}) %all-to-all-start.4) | async-done | bytes 1572896 | tf_op jit(solution)/shard_map/all_to_all | solution.py:30
  168.4 2.5 %fusion.27 = (f32[64,1,12,512]{3,2,0,1:T(8,128)}, f32[64,1,12,512]{3,2,0,1:T(8,128)}) fusion(bf16[64,2,12,512]{3,2,1,0:T(8,128)(2,1)S(1)} %bitcast.185), kind=kLoop, calls=%fused_computation.43 | loop fusion | flops 786432 | bytes 4718592 | tf_op jit(solution)/shard_map/convert_element_type | solution.py:188
  170.9 1.6 reshape.210
  174.6 1.6 reshape.211
  178.4 1.8 multiply_reduce_fusion
  (99 shorter events, 26.3 us)
Async XLA Ops:
  0.6 116.1 %copy-start = (bf16[1,512,1024]{2,1,0:T(8,128)(2,1)S(1)}, bf16[1,512,1024]{2,1,0:T(8,128)(2,1)}, u32[]{:S(2)}) copy-start(bf16[1,512,1024]{2,1,0:T(8,128)(2,1)} %param.20) | copy-start | bytes 3145732
  4.8 11.3 %copy-start.17 = (s32[1,128,2]{1,2,0:T(2,128)S(1)}, s32[1,128,2]{1,2,0:T(2,128)}, u32[]{:S(2)}) copy-start(s32[1,128,2]{1,2,0:T(2,128)} %param.16) | copy-start | bytes 3076
  4.8 12.8 %copy-start.15 = (bf16[1,128,512]{2,1,0:T(8,128)(2,1)S(1)}, bf16[1,128,512]{2,1,0:T(8,128)(2,1)}, u32[]{:S(2)}) copy-start(bf16[1,128,512]{2,1,0:T(8,128)(2,1)} %param.18) | copy-start | bytes 393220
  6.5 13.5 %copy-start.16 = (f32[1,128,2]{1,2,0:T(2,128)S(1)}, f32[1,128,2]{1,2,0:T(2,128)}, u32[]{:S(2)}) copy-start(f32[1,128,2]{1,2,0:T(2,128)} %param.17) | copy-start | bytes 3076
  6.5 28.8 %all-to-all-start = ((bf16[32,160,128]{2,1,0:T(8,128)(2,1)}), bf16[32,160,128]{2,1,0:T(8,128)(2,1)S(1)}, u32[]{:S(2)}, u32[]{:S(2)}) async-start(bf16[32,160,128]{2,1,0:T(8,128)(2,1)} %fusion.26), calls=%async_computation | async-start | bytes 2621440 | tf_op jit(solution)/shard_map/all_to_all | solution.py:107
  44.5 12.7 %all-to-all-start.1 = ((bf16[32,2,1024]{2,1,0:T(2,128)(2,1)}), bf16[32,2,1024]{2,1,0:T(2,128)(2,1)S(1)}, u32[]{:S(2)}, u32[]{:S(2)}) async-start(bf16[32,2,1024]{2,1,0:T(2,128)(2,1)} %reshape.256), calls=%async_computation.1 | async-start | bytes 262144 | tf_op jit(solution)/shard_map/all_to_all | solution.py:139
  51.4 12.4 %copy-start.14 = (bf16[512,512]{1,0:T(8,128)(2,1)S(1)}, bf16[512,512]{1,0:T(8,128)(2,1)}, u32[]{:S(2)}) copy-start(bf16[512,512]{1,0:T(8,128)(2,1)} %param.15) | copy-start | bytes 1572868
  57.2 25.1 %all-to-all-start.3 = ((bf16[128,12,256]{2,1,0:T(8,128)(2,1)}), bf16[128,12,256]{2,1,0:T(8,128)(2,1)S(1)}, u32[]{:S(2)}, u32[]{:S(2)}) async-start(bf16[128,12,256]{2,1,0:T(8,128)(2,1)} %bitcast.34), calls=%async_computation.3 | async-start | bytes 2097152 | tf_op jit(solution)/shard_map/all_to_all | solution.py:26
  82.4 23.8 %all-to-all-start.2 = ((bf16[128,12,256]{2,1,0:T(8,128)(2,1)}), bf16[128,12,256]{2,1,0:T(8,128)(2,1)S(1)}, u32[]{:S(2)}, u32[]{:S(2)}) async-start(bf16[128,12,256]{2,1,0:T(8,128)(2,1)} %bitcast.188), calls=%async_computation.2 | async-start | bytes 2097152 | tf_op jit(solution)/shard_map/all_to_all | solution.py:26
  87.9 20.3 %collective-permute-start.1 = (bf16[128,12,256]{2,0,1:T(8,128)(2,1)}, bf16[128,12,256]{2,0,1:T(8,128)(2,1)}, u32[]{:S(2)}, u32[]{:S(2)}) collective-permute-start(bf16[128,12,256]{2,0,1:T(8,128)(2,1)} %copy.88), channel_id=1, source_target_pairs={{0,1},{1,0},{2,3},{3,2},{4,5},{5,4},{6,7},{7,6},{8,9},{9,8},{10,11... | collective-permute-start | bytes 2359304 | tf_op jit(solution)/shard_map/ppermute | solution.py:75
  107.3 3.2 %collective-permute-start = (bf16[128,12,256]{2,0,1:T(8,128)(2,1)}, bf16[128,12,256]{2,0,1:T(8,128)(2,1)}, u32[]{:S(2)}, u32[]{:S(2)}) collective-permute-start(bf16[128,12,256]{2,0,1:T(8,128)(2,1)} %copy.82), channel_id=1, source_target_pairs={{0,1},{1,0},{2,3},{3,2},{4,5},{5,4},{6,7},{7,6},{8,9},{9,8},{10,11... | collective-permute-start | bytes 2359304 | tf_op jit(solution)/shard_map/ppermute | solution.py:75
  108.2 4.7 %copy-start.18 = (bf16[1,1024,512]{2,1,0:T(8,128)(2,1)S(1)}, bf16[1,1024,512]{2,1,0:T(8,128)(2,1)}, u32[]{:S(2)}) copy-start(bf16[1,1024,512]{2,1,0:T(8,128)(2,1)} %param.21) | copy-start | bytes 3145732
  112.9 1.9 %copy-start.5 = (bf16[128,12,256]{2,0,1:T(8,128)(2,1)}, bf16[128,12,256]{2,0,1:T(8,128)(2,1)S(1)}, u32[]{:S(2)}) copy-start(bf16[128,12,256]{2,0,1:T(8,128)(2,1)S(1)} %get-tuple-element.12) | copy-start | bytes 2359300
  112.9 1.9 %copy-start.7 = (bf16[128,12,256]{2,0,1:T(8,128)(2,1)}, bf16[128,12,256]{2,0,1:T(8,128)(2,1)S(1)}, u32[]{:S(2)}) copy-start(bf16[128,12,256]{2,0,1:T(8,128)(2,1)S(1)} %get-tuple-element.13) | copy-start | bytes 2359300
  112.9 3.9 %copy-start.9 = (bf16[128,12,256]{2,0,1:T(8,128)(2,1)}, bf16[128,12,256]{2,0,1:T(8,128)(2,1)S(1)}, u32[]{:S(2)}) copy-start(bf16[128,12,256]{2,0,1:T(8,128)(2,1)S(1)} %get-tuple-element.20) | copy-start | bytes 2359300
  112.9 3.9 %copy-start.12 = (bf16[128,12,256]{2,0,1:T(8,128)(2,1)}, bf16[128,12,256]{2,0,1:T(8,128)(2,1)S(1)}, u32[]{:S(2)}) copy-start(bf16[128,12,256]{2,0,1:T(8,128)(2,1)S(1)} %get-tuple-element.21) | copy-start | bytes 2359300
  112.9 2.0 %copy-start.4 = (bf16[1,512,1024]{2,1,0:T(8,128)(2,1)S(1)}, bf16[1,512,1024]{2,1,0:T(8,128)(2,1)}, u32[]{:S(2)}) copy-start(bf16[1,512,1024]{2,1,0:T(8,128)(2,1)} %param.19) | copy-start | bytes 3145732
  120.9 1.9 %copy-start.19 = (bf16[128,12,1024]{2,0,1:T(8,128)(2,1)}, bf16[128,12,1024]{2,0,1:T(8,128)(2,1)S(1)}, u32[]{:S(2)}) copy-start(bf16[128,12,1024]{2,0,1:T(8,128)(2,1)S(1)} %get-tuple-element.7) | copy-start | bytes 9437188
  120.9 2.6 %copy-start.20 = (bf16[128,12,1024]{2,0,1:T(8,128)(2,1)}, bf16[128,12,1024]{2,0,1:T(8,128)(2,1)S(1)}, u32[]{:S(2)}) copy-start(bf16[128,12,1024]{2,0,1:T(8,128)(2,1)S(1)} %get-tuple-element.5) | copy-start | bytes 9437188
  121.0 4.4 %copy-start.2 = (bf16[128,1,12,1024]{3,0,2,1:T(8,128)(2,1)}, bf16[128,1,12,1024]{3,0,2,1:T(8,128)(2,1)S(1)}, u32[]{:S(2)}) copy-start(bf16[128,1,12,1024]{3,0,2,1:T(8,128)(2,1)S(1)} %get-tuple-element.6) | copy-start | bytes 9437188
  127.3 3.7 %collective-permute-start.2 = (bf16[128,12,512]{2,0,1:T(8,128)(2,1)S(1)}, bf16[128,12,512]{2,0,1:T(8,128)(2,1)S(1)}, u32[]{:S(2)}, u32[]{:S(2)}) collective-permute-start(bf16[128,12,512]{2,0,1:T(8,128)(2,1)S(1)} %get-tuple-element.18), channel_id=1, source_target_pairs={{0,1},{1,0},{2,3},{3,2},{4,5},{5,4},{6,7},{7,6},{8,9},{9,8},{10,11... | collective-permute-start | bytes 4718600 | tf_op jit(solution)/shard_map/ppermute | solution.py:85
  131.7 6.8 %copy-start.10 = (bf16[128,12,256]{2,0,1:T(8,128)(2,1)S(1)}, bf16[128,12,256]{2,0,1:T(8,128)(2,1)}, u32[]{:S(2)}) copy-start(bf16[128,12,256]{2,0,1:T(8,128)(2,1)} %copy-done.9) | copy-start | bytes 2359300
  134.0 34.4 %all-to-all-start.4 = ((bf16[128,12,512]{2,1,0:T(8,128)(2,1)}), bf16[128,12,512]{2,1,0:T(8,128)(2,1)S(1)}, u32[]{:S(2)}, u32[]{:S(2)}) async-start(bf16[128,12,512]{2,1,0:T(8,128)(2,1)} %copy.90), calls=%async_computation.4 | async-start | bytes 4194304 | tf_op jit(solution)/shard_map/all_to_all | solution.py:30
  138.5 5.1 %copy-start.3 = (bf16[128,1,12,1024]{3,0,2,1:T(8,128)(2,1)S(1)}, bf16[128,1,12,1024]{3,0,2,1:T(8,128)(2,1)}, u32[]{:S(2)}) copy-start(bf16[128,1,12,1024]{3,0,2,1:T(8,128)(2,1)} %copy-done.2) | copy-start | bytes 9437188
  138.6 5.1 %copy-start.11 = (bf16[128,12,256]{2,0,1:T(8,128)(2,1)S(1)}, bf16[128,12,256]{2,0,1:T(8,128)(2,1)}, u32[]{:S(2)}) copy-start(bf16[128,12,256]{2,0,1:T(8,128)(2,1)} %copy-done.9) | copy-start | bytes 2359300
  138.6 5.1 %copy-start.13 = (bf16[128,12,256]{2,0,1:T(8,128)(2,1)S(1)}, bf16[128,12,256]{2,0,1:T(8,128)(2,1)}, u32[]{:S(2)}) copy-start(bf16[128,12,256]{2,0,1:T(8,128)(2,1)} %copy-done.12) | copy-start | bytes 2359300
  143.6 2.8 %copy-start.6 = (bf16[128,12,256]{2,0,1:T(8,128)(2,1)S(1)}, bf16[128,12,256]{2,0,1:T(8,128)(2,1)}, u32[]{:S(2)}) copy-start(bf16[128,12,256]{2,0,1:T(8,128)(2,1)} %copy-done.5) | copy-start | bytes 2359300
  143.7 2.8 %copy-start.8 = (bf16[128,12,256]{2,0,1:T(8,128)(2,1)S(1)}, bf16[128,12,256]{2,0,1:T(8,128)(2,1)}, u32[]{:S(2)}) copy-start(bf16[128,12,256]{2,0,1:T(8,128)(2,1)} %copy-done.7) | copy-start | bytes 2359300
  143.7 2.8 %copy-start.21 = (bf16[128,12,1024]{2,0,1:T(8,128)(2,1)S(1)}, bf16[128,12,1024]{2,0,1:T(8,128)(2,1)}, u32[]{:S(2)}) copy-start(bf16[128,12,1024]{2,0,1:T(8,128)(2,1)} %copy-done.20) | copy-start | bytes 9437188
  176.3 4.7 %copy-start.1 = (bf16[1,512,1024]{2,1,0:T(8,128)(2,1)S(1)}, bf16[1,512,1024]{2,1,0:T(8,128)(2,1)}, u32[]{:S(2)}) copy-start(bf16[1,512,1024]{2,1,0:T(8,128)(2,1)} %param.20) | copy-start | bytes 3145732
where the time goes:
time: 182 us; the launch traced here: 181 us
  waiting for transfers between devices  72 us (40%)
  starting transfers between devices  31.5 us (17%)
  local copies, waits for them, and re-layouts  29.2 us (16%)
  matrix products  25.3 us (14%)
  other arithmetic  13.4 us (7%)
  Pallas kernels  8.25 us (5%)
    all_to_all x2, waiting for transfers between devices, to_experts(): lax.all_to_all(buffer, ('table', 'blk'), split_axis=0, concat_axis=0, til...  28.2 us
    all_to_all x1, waiting for transfers between devices, to_anchor(): lax.all_to_all(buffer, ('table', 'blk'), split_axis=0, concat_axis=0, til...  19.1 us
    all_to_all x1, waiting for transfers between devices, attend_heads(): got = lax.all_to_all(parcel, 'blk', 0, 0, tiled=True)  15 us
    all_to_all x2, starting transfers between devices, to_experts(): lax.all_to_all(buffer, ('table', 'blk'), split_axis=0, concat_axis=0, til...  10.3 us
    all_to_all x1, starting transfers between devices, attend_heads(): got = lax.all_to_all(parcel, 'blk', 0, 0, tiled=True)  9.55 us
    pallas_call x1, Pallas kernels, attend_heads(): pl.pallas_call(kernel, grid=(steps,), in_specs=[pl.BlockSpec(got.shape, l...  8.25 us
    dot_general x1, matrix products, backward_part(): jnp.einsum('svcd,svcf->vdf', arrived, grad_pre_up, preferred_element_type...  5.06 us
    all_to_all x1, starting transfers between devices, attend_heads(): back = lax.all_to_all(mixed, 'blk', 0, 0, tiled=True)  5.02 us
  transfers between devices with their start and end apart: 8, of which 7 were waited for; matrix products, arithmetic and copies ran while one was open for 16% of the time, Pallas kernels for 0%

commit v1 on v0

--- a/solution.py
+++ b/solution.py
@@ -30,62 +30,35 @@
     return lax.all_to_all(buffer, ("table", "blk"), split_axis=0, concat_axis=0, tiled=True)
 
 
-def forward_part(arrived, w_gate, w_up, w_down):
-    pre_gate = jnp.einsum("svcd,vdf->svcf", arrived, w_gate, preferred_element_type=jnp.float32)
-    pre_up = jnp.einsum("svcd,vdf->svcf", arrived, w_up, preferred_element_type=jnp.float32)
-    activated = jax.nn.silu(pre_gate)
-    hidden = (activated * pre_up).astype(jnp.bfloat16)
-    outputs = jnp.einsum(
-        "svcf,vfd->svcd", hidden, w_down, preferred_element_type=jnp.float32
-    ).astype(jnp.bfloat16)
-    return (outputs, pre_gate, pre_up, activated, hidden)
-
-
-def backward_part(arrived, arrived_cots, pre_gate, pre_up, activated, hidden, w_gate, w_up, w_down):
-    grad_hidden = jnp.einsum(
-        "svcd,vfd->svcf", arrived_cots, w_down, preferred_element_type=jnp.float32
-    )
-    grad_pre_gate = (grad_hidden * pre_up * silu_grad(pre_gate)).astype(jnp.bfloat16)
-    grad_pre_up = (grad_hidden * activated).astype(jnp.bfloat16)
-    grad_down = jnp.einsum(
-        "svcf,svcd->vfd", hidden, arrived_cots, preferred_element_type=jnp.float32
-    ).astype(jnp.bfloat16)
-    grad_gate = jnp.einsum(
-        "svcd,svcf->vdf", arrived, grad_pre_gate, preferred_element_type=jnp.float32
-    ).astype(jnp.bfloat16)
-    grad_up = jnp.einsum(
-        "svcd,svcf->vdf", arrived, grad_pre_up, preferred_element_type=jnp.float32
-    ).astype(jnp.bfloat16)
-    grad_inputs = (
-        jnp.einsum("svcf,vdf->svcd", grad_pre_gate, w_gate, preferred_element_type=jnp.float32)
-        + jnp.einsum("svcf,vdf->svcd", grad_pre_up, w_up, preferred_element_type=jnp.float32)
-    ).astype(jnp.bfloat16)
-    return (grad_inputs, grad_gate, grad_up, grad_down)
-
-
 def partner_pairs():
     devices = lax.psum(1, "blk")
     return [(b, b ^ 1) for b in range(devices)]
 
 
-def dispatch(slots):
-    width = slots.shape[1] // PIECES
-    parts = jnp.transpose(slots.reshape(EXPERTS, CAP, PIECES, width), (0, 2, 1, 3))
-    got = to_experts(parts.reshape(EXPERTS * PIECES, CAP, width))
+def spread(slots):
+    half = CAP // PIECES
+    got = to_experts(slots.reshape(EXPERTS * PIECES, half, slots.shape[1]))
     other = lax.ppermute(got, "blk", partner_pairs())
-    first = lax.axis_index("blk") % 2 == 0
-    return jnp.concatenate(
-        [jnp.where(first, got, other), jnp.where(first, other, got)], axis=-1
-    )
-
-
-def give_back(outputs, grads):
-    first = lax.axis_index("blk") % 2 == 0
-    keep = jnp.where(first, outputs, grads)
-    other = lax.ppermute(jnp.where(first, grads, outputs), "blk", partner_pairs())
-    summed = (keep.astype(jnp.float32) + other.astype(jnp.float32)).astype(jnp.bfloat16)
-    back = to_anchor(summed).reshape(EXPERTS, PIECES, CAP, -1)
-    return back[:, 0].reshape(EXPERTS * CAP, -1), back[:, 1].reshape(EXPERTS * CAP, -1)
+    return got.reshape(-1, slots.shape[1]), other.reshape(-1, slots.shape[1])
+
+
+def piece_pass(inputs, cots, gate_mat, up_mat, down_mat):
+    pre_gate = jnp.dot(inputs, gate_mat, preferred_element_type=jnp.float32)
+    pre_up = jnp.dot(inputs, up_mat, preferred_element_type=jnp.float32)
+    activated = jax.nn.silu(pre_gate)
+    hidden = (activated * pre_up).astype(jnp.bfloat16)
+    output = jnp.dot(hidden, down_mat, preferred_element_type=jnp.float32).astype(jnp.bfloat16)
+    grad_hidden = jnp.dot(cots, down_mat.T, preferred_element_type=jnp.float32)
+    grad_pre_gate = (grad_hidden * pre_up * silu_grad(pre_gate)).astype(jnp.bfloat16)
+    grad_pre_up = (grad_hidden * activated).astype(jnp.bfloat16)
+    grad_inputs = (
+        jnp.dot(grad_pre_gate, gate_mat.T, preferred_element_type=jnp.float32)
+        + jnp.dot(grad_pre_up, up_mat.T, preferred_element_type=jnp.float32)
+    ).astype(jnp.bfloat16)
+    grad_down = jnp.dot(hidden.T, cots, preferred_element_type=jnp.float32)
+    grad_gate = jnp.dot(inputs.T, grad_pre_gate, preferred_element_type=jnp.float32)
+    grad_up = jnp.dot(inputs.T, grad_pre_up, preferred_element_type=jnp.float32)
+    return (jnp.concatenate([output, grad_inputs], axis=-1), grad_gate, grad_up, grad_down)
 
 
 def attend_heads(query_rows, key_rows, value_rows):
@@ -165,8 +138,10 @@
     slot_index = route_experts * CAP + position
     grad_flat = cotangent[0].astype(jnp.float32)
     route_cots = (gates[:, None] * jnp.repeat(grad_flat, TOP, axis=0)).astype(jnp.bfloat16)
-    cot_slots = jnp.zeros((EXPERTS * CAP, D), jnp.bfloat16).at[slot_index].set(route_cots)
-    arrived_cots = dispatch(cot_slots).reshape(-1, w_gate.shape[0], CAP, D)
+    slot_ids = jnp.arange(EXPERTS * CAP, dtype=jnp.int32)
+    placing = (slot_ids[:, None] == slot_index[None, :]).astype(jnp.bfloat16)
+    cot_slots = jnp.dot(placing, route_cots, preferred_element_type=jnp.float32).astype(jnp.bfloat16)
+    cot_own, cot_other = spread(cot_slots)
     attended = attend_heads(queries[0], key_rows[0], value_rows[0])
     stream = residual[0].astype(jnp.float32) + jnp.dot(
         attended, w_out, preferred_element_type=jnp.float32
@@ -174,18 +149,23 @@
     radius = jnp.sqrt(jnp.mean(stream * stream, axis=-1, keepdims=True) + 1e-06)
     unit = stream / radius
     normed = unit.astype(jnp.bfloat16)
-    local_pieces = w_gate.shape[0]
-    in_slots = jnp.zeros((EXPERTS * CAP, D), jnp.bfloat16).at[slot_index].set(
-        jnp.repeat(normed, TOP, axis=0)
-    )
-    arrived = dispatch(in_slots).reshape(-1, local_pieces, CAP, D)
-    outputs, pre_gate, pre_up, activated, hidden = forward_part(arrived, w_gate, w_up, w_down)
-    grad_inputs, grad_gate, grad_up, grad_down = backward_part(
-        arrived, arrived_cots, pre_gate, pre_up, activated, hidden, w_gate, w_up, w_down
-    )
-    out_slots, grad_slots = give_back(outputs[:, 0], grad_inputs[:, 0])
-    route_out = out_slots.astype(jnp.float32)[slot_index]
-    route_grad = grad_slots.astype(jnp.float32)[slot_index]
+    in_slots = jnp.dot(
+        placing, jnp.repeat(normed, TOP, axis=0), preferred_element_type=jnp.float32
+    ).astype(jnp.bfloat16)
+    in_own, in_other = spread(in_slots)
+    mats = (w_gate[0], w_up[0], w_down[0])
+    own, gate_a, up_a, down_a = piece_pass(in_own, cot_own, *mats)
+    other, gate_b, up_b, down_b = piece_pass(in_other, cot_other, *mats)
+    theirs = lax.ppermute(other, "blk", partner_pairs())
+    summed = (own.astype(jnp.float32) + theirs.astype(jnp.float32)).astype(jnp.bfloat16)
+    back = to_anchor(summed.reshape(EXPERTS * PIECES, CAP // PIECES, 2 * D))
+    picking = (slot_index[:, None] == slot_ids[None, :]).astype(jnp.bfloat16)
+    picked = jnp.dot(picking, back.reshape(EXPERTS * CAP, 2 * D), preferred_element_type=jnp.float32)
+    route_out = picked[:, :D]
+    route_grad = picked[:, D:]
+    grad_gate = (gate_a + gate_b).astype(jnp.bfloat16)[None]
+    grad_up = (up_a + up_b).astype(jnp.bfloat16)[None]
+    grad_down = (down_a + down_b).astype(jnp.bfloat16)[None]
     moe = jnp.sum((gates[:, None] * route_out).reshape(row_count, TOP, D), axis=1)
     block_out = (stream + moe).astype(jnp.bfloat16)[None]
     grad_unit = jnp.sum(route_grad.reshape(row_count, TOP, D), axis=1)

time: 182 us -> 191 us (1.049)
  matrix products: 25.3 us -> 40.1 us
  other arithmetic: 13.4 us -> 6.66 us
  local copies, waits for them, and re-layouts: 29.2 us -> 31.4 us
    dot_general x9 -> x21, matrix products: 24.1 us -> 38.9 us  [the longest x2 6.64 us: piece_pass(): pre_gate = jnp.dot(inputs, gate_mat, preferred_element_type=jnp.float32)]
    ppermute x3, waiting for transfers between devices: 5.29 us -> 0.01 us  [the longest x2 0.01 us: spread(): other = lax.ppermute(got, 'blk', partner_pairs())]
    reshape x4 -> x9, local copies, waits for them, and re-layouts: 4.76 us -> 9.64 us  [the longest x4 3.77 us: spread(): return (got.reshape(-1, slots.shape[1]), other.reshape(-1, slots.shape[1]))]
    ppermute x0 -> x2, local copies, waits for them, and re-layouts: none -> 4.12 us  [spread(): other = lax.ppermute(got, 'blk', partner_pairs())]
    convert_element_type x3 -> x1, local copies, waits for them, and re-layouts: 5.45 us -> 1.71 us  [block(): (own.astype(jnp.float32) + theirs.astype(jnp.float32)).astype(jnp.bfloat16)]
    unnamed x50 -> x64, local copies, waits for them, and re-layouts: 4.37 us -> 7.78 us
    all_to_all x2, waiting for transfers between devices: 28.2 us -> 31.3 us  [to_experts(): lax.all_to_all(buffer, ('table', 'blk'), split_axis=0, concat_axis=0, til...]
    gather x3 -> x0, local copies, waits for them, and re-layouts: 3.05 us -> none  [the longest x2 2.08 us: block(): route_out = out_slots.astype(jnp.float32)[slot_index]]
  transfers between devices with their start and end apart: 8 -> 8, of which waited for: 7 -> 5; matrix products, arithmetic and copies ran while one was open for 16% -> 24% of each run, Pallas kernels for 0% -> 0%
where the time goes in v1:
time: 191 us
  waiting for transfers between devices  71.7 us (38%)
  matrix products  40.1 us (21%)
  local copies, waits for them, and re-layouts  31.4 us (16%)
  starting transfers between devices  31.2 us (16%)
  Pallas kernels  8.25 us (4%)
  other arithmetic  6.66 us (3%)
    all_to_all x2, waiting for transfers between devices, to_experts(): lax.all_to_all(buffer, ('table', 'blk'), split_axis=0, concat_axis=0, til...  31.3 us
    all_to_all x1, waiting for transfers between devices, to_anchor(): lax.all_to_all(buffer, ('table', 'blk'), split_axis=0, concat_axis=0, til...  19.2 us
    all_to_all x1, waiting for transfers between devices, attend_heads(): got = lax.all_to_all(parcel, 'blk', 0, 0, tiled=True)  15.2 us
    all_to_all x2, starting transfers between devices, to_experts(): lax.all_to_all(buffer, ('table', 'blk'), split_axis=0, concat_axis=0, til...  10.3 us
    all_to_all x1, starting transfers between devices, attend_heads(): got = lax.all_to_all(parcel, 'blk', 0, 0, tiled=True)  9.55 us
    pallas_call x1, Pallas kernels, attend_heads(): pl.pallas_call(kernel, grid=(steps,), in_specs=[pl.BlockSpec(got.shape, l...  8.25 us
    unnamed x64, local copies, waits for them, and re-layouts  7.78 us
    dot_general x2, matrix products, piece_pass(): pre_gate = jnp.dot(inputs, gate_mat, preferred_element_type=jnp.float32)  6.64 us
  transfers between devices with their start and end apart: 8, of which 5 were waited for; matrix products, arithmetic and copies ran while one was open for 24% of the time, Pallas kernels for 0%

profile of v1, /device:TPU:1, one launch (start us, length us, event | category | flops | bytes accessed | tf_op | source)
XLA Modules:
  0.0 190.5 jit_solution(8190454637682757890)
XLA Ops:
  4.8 1.7 fusion.6
  6.5 9.6 %all-to-all-start = ((bf16[32,160,128]{2,1,0:T(8,128)(2,1)}), bf16[32,160,128]{2,1,0:T(8,128)(2,1)S(1)}, u32[]{:S(2)}, u32[]{:S(2)}) async-start(bf16[32,160,128]{2,1,0:T(8,128)(2,1)} %fusion.6), calls=%async_computation | async-start | bytes 2621440 | tf_op jit(solution)/shard_map/all_to_all | solution.py:80
  18.6 1.4 reshape.122
  20.1 15.2 %all-to-all-done.got_ref = bf16[32,160,128]{2,1,0:T(8,128)(2,1)S(1)} async-done(((bf16[32,160,128]{2,1,0:T(8,128)(2,1)}), bf16[32,160,128]{2,1,0:T(8,128)(2,1)S(1)}, u32[]{:S(2)}, u32[]{:S(2)}) %all-to-all-start) | async-done | bytes 1310752 | tf_op jit(solution)/shard_map/all_to_all | solution.py:80
  35.4 8.2 %shard_map.146 = bf16[32,32,64]{2,1,0:T(8,128)(2,1)S(1)} custom-call(bf16[32,160,128]{2,1,0:T(8,128)(2,1)S(1)} %all-to-all-done.got_ref), custom_call_target="tpu_custom_call" | custom-call | flops 2147483648 | bytes 1441792 | tf_op jit(solution)/shard_map/pallas_call | solution.py:99
  44.5 5.0 %all-to-all-start.1 = ((bf16[32,2,1024]{2,1,0:T(2,128)(2,1)}), bf16[32,2,1024]{2,1,0:T(2,128)(2,1)S(1)}, u32[]{:S(2)}, u32[]{:S(2)}) async-start(bf16[32,2,1024]{2,1,0:T(2,128)(2,1)} %reshape.134), calls=%async_computation.1 | async-start | bytes 262144 | tf_op jit(solution)/shard_map/all_to_all | solution.py:112
  51.2 6.0 %all-to-all-done.1 = bf16[32,2,1024]{2,1,0:T(2,128)(2,1)S(1)} async-done(((bf16[32,2,1024]{2,1,0:T(2,128)(2,1)}), bf16[32,2,1024]{2,1,0:T(2,128)(2,1)S(1)}, u32[]{:S(2)}, u32[]{:S(2)}) %all-to-all-start.1) | async-done | bytes 131104 | tf_op jit(solution)/shard_map/all_to_all | solution.py:112
  57.2 5.9 %all-to-all-start.3 = ((bf16[128,6,512]{2,1,0:T(8,128)(2,1)}), bf16[128,6,512]{2,1,0:T(8,128)(2,1)S(1)}, u32[]{:S(2)}, u32[]{:S(2)}) async-start(bf16[128,6,512]{2,1,0:T(8,128)(2,1)} %reshape.123), calls=%async_computation.3 | async-start | bytes 2097152 | tf_op jit(solution)/shard_map/all_to_all | solution.py:26
  67.0 15.4 %all-to-all-done.3 = bf16[128,6,512]{2,1,0:T(8,128)(2,1)S(1)} async-done(((bf16[128,6,512]{2,1,0:T(8,128)(2,1)}), bf16[128,6,512]{2,1,0:T(8,128)(2,1)S(1)}, u32[]{:S(2)}, u32[]{:S(2)}) %all-to-all-start.3) | async-done | bytes 786464 | tf_op jit(solution)/shard_map/all_to_all | solution.py:26
  82.3 4.4 %all-to-all-start.2 = ((bf16[128,6,512]{2,1,0:T(8,128)(2,1)}), bf16[128,6,512]{2,1,0:T(8,128)(2,1)S(1)}, u32[]{:S(2)}, u32[]{:S(2)}) async-start(bf16[128,6,512]{2,1,0:T(8,128)(2,1)} %reshape.120), calls=%async_computation.2 | async-start | bytes 2097152 | tf_op jit(solution)/shard_map/all_to_all | solution.py:26
  90.2 15.9 %all-to-all-done.2 = bf16[128,6,512]{2,1,0:T(8,128)(2,1)S(1)} async-done(((bf16[128,6,512]{2,1,0:T(8,128)(2,1)}), bf16[128,6,512]{2,1,0:T(8,128)(2,1)S(1)}, u32[]{:S(2)}, u32[]{:S(2)}) %all-to-all-start.2) | async-done | bytes 786464 | tf_op jit(solution)/shard_map/all_to_all | solution.py:26
  108.2 2.7 %fusion.10 = f32[768,1024]{1,0:T(8,128)} fusion(bf16[768,512]{1,0:T(8,128)(2,1)S(1)} %copy-done.11, bf16[1,1024,512]{2,1,0:T(8,128)(2,1)S(1)} %copy-done.7), kind=kOutput, calls=%fused_computation.31 | convolution fusion | flops 805306368 | bytes 4980736 | tf_op jit(solution)/shard_map/dot_general | solution.py:51
  110.9 2.5 %copy.43 = bf16[128,6,512]{2,1,0:T(8,128)(2,1)} copy(bf16[128,6,512]{2,0,1:T(8,128)(2,1)} %collective-permute-done.1) | data formatting | bytes 1572864 | tf_op jit(solution)/shard_map/ppermute | solution.py:41
  113.5 2.1 %reshape.126 = bf16[768,512]{1,0:T(8,128)(2,1)} reshape(bf16[128,6,512]{2,1,0:T(8,128)(2,1)} %copy.43) | data formatting | bytes 1572864 | tf_op jit(solution)/shard_map/reshape | solution.py:42
  115.6 3.8 %fusion.7 = f32[768,1024]{1,0:T(8,128)} fusion(bf16[768,512]{1,0:T(8,128)(2,1)} %reshape.126, bf16[1,1024,512]{2,1,0:T(8,128)(2,1)S(1)} %copy-done.7), kind=kOutput, calls=%fused_computation.28 | convolution fusion | flops 805306368 | bytes 4980736 | tf_op jit(solution)/shard_map/dot_general | solution.py:51
  119.7 4.1 %fusion.25 = f32[768,1024]{1,0:T(8,128)} fusion(bf16[768,512]{1,0:T(8,128)(2,1)S(1)} %reshape.121, bf16[1,512,1024]{2,1,0:T(8,128)(2,1)} %param.19), kind=kOutput, calls=%fused_computation.46 | convolution fusion | flops 805306368 | bytes 4980736 | tf_op jit(solution)/shard_map/dot_general | solution.py:46
  123.8 1.6 copy.41
  125.7 2.5 %fusion.21 = f32[768,1024]{1,0:T(8,128)S(1)} fusion(bf16[768,512]{1,0:T(8,128)(2,1)S(1)} %reshape.125, bf16[1,512,1024]{2,1,0:T(8,128)(2,1)} %param.19), kind=kOutput, calls=%fused_computation.42 | convolution fusion | flops 805306368 | bytes 4980736 | tf_op jit(solution)/shard_map/dot_general | solution.py:46
  128.3 2.3 %multiply_convert_fusion.2 = (bf16[768,1024]{1,0:T(8,128)(2,1)S(1)}, bf16[768,1024]{1,0:T(8,128)(2,1)S(1)}, bf16[768,1024]{1,0:T(8,128)(2,1)S(1)}) fusion(f32[768,1024]{1,0:T(8,128)S(1)} %fusion.21, f32[768,1024]{1,0:T(8,128)S(1)} %copy-done.14, bf16[768,512]{1,0:T(8,128)(2,1)S(1)} %reshape.125, bf16[1,512,1024]{2,1,0:T(8,128)(2,1)S(1)} %copy-done), kind=kOutput, calls=%fused_computation.3 | convolution fusion | flops 817102848 | bytes 12845056 | tf_op jit(solution)/shard_map/dot_general | solution.py:47
  137.0 2.3 %multiply_convert_fusion.5 = (bf16[768,1024]{1,0:T(8,128)(2,1)S(1)}, bf16[768,1024]{1,0:T(8,128)(2,1)S(1)}, bf16[768,1024]{1,0:T(8,128)(2,1)S(1)}) fusion(f32[768,1024]{1,0:T(8,128)S(1)} %copy-done.1, f32[768,1024]{1,0:T(8,128)S(1)} %copy-done.13, bf16[768,512]{1,0:T(8,128)(2,1)S(1)} %copy-done.5, bf16[1,512,1024]{2,1,0:T(8,128)(2,1)S(1)} %copy-done), kind=kOutput, calls=%fused_computation.8 | convolution fusion | flops 817102848 | bytes 12845056 | tf_op jit(solution)/shard_map/dot_general | solution.py:47
  141.6 2.3 %fusion.42 = f32[1024,512]{1,0:T(8,128)} fusion(bf16[768,1024]{1,0:T(8,128)(2,1)S(1)} %get-tuple-element.5, bf16[768,512]{1,0:T(8,128)(2,1)S(1)} %copy-done.12), kind=kOutput, calls=%fused_computation.82 | convolution fusion | flops 805306368 | bytes 4456448 | tf_op jit(solution)/shard_map/dot_general | solution.py:58
  145.0 1.6 add_convert_fusion
  146.6 1.7 copy.44
  148.3 1.7 reshape.127
  150.0 3.8 %all-to-all-start.4 = ((bf16[128,6,1024]{2,1,0:T(8,128)(2,1)}), bf16[128,6,1024]{2,1,0:T(8,128)(2,1)S(1)}, u32[]{:S(2)}, u32[]{:S(2)}) async-start(bf16[128,6,1024]{2,1,0:T(8,128)(2,1)} %reshape.127), calls=%async_computation.4 | async-start | bytes 4194304 | tf_op jit(solution)/shard_map/all_to_all | solution.py:30
  153.9 2.8 %fusion.41 = f32[512,1024]{1,0:T(8,128)S(1)} fusion(bf16[768,512]{1,0:T(8,128)(2,1)} %copy-done.4, bf16[768,1024]{1,0:T(8,128)(2,1)} %copy-done.28), kind=kOutput, calls=%fused_computation.81 | convolution fusion | flops 805306368 | bytes 4456448 | tf_op jit(solution)/shard_map/dot_general | solution.py:60
  159.0 2.0 %fusion.5 = bf16[1,1024,512]{2,1,0:T(8,128)(2,1)} fusion(f32[1024,512]{1,0:T(8,128)S(1)} %copy-done.19, bf16[768,1024]{1,0:T(8,128)(2,1)S(1)} %copy-done.25, bf16[768,512]{1,0:T(8,128)(2,1)S(1)} %copy-done.10), kind=kOutput, calls=%fused_computation.25 | convolution fusion | flops 806354944 | bytes 5505024 | tf_op jit(solution)/shard_map/dot_general | solution.py:58
  160.9 2.0 %fusion.4 = bf16[1,512,1024]{2,1,0:T(8,128)(2,1)} fusion(f32[512,1024]{1,0:T(8,128)S(1)} %fusion.41, bf16[768,512]{1,0:T(8,128)(2,1)S(1)} %copy-done.3, bf16[768,1024]{1,0:T(8,128)(2,1)S(1)} %copy-done.23), kind=kOutput, calls=%fused_computation.24 | convolution fusion | flops 806354944 | bytes 5505024 | tf_op jit(solution)/shard_map/dot_general | solution.py:60
  162.9 2.0 %fusion.3 = bf16[1,512,1024]{2,1,0:T(8,128)(2,1)} fusion(f32[512,1024]{1,0:T(8,128)S(1)} %fusion.40, bf16[768,512]{1,0:T(8,128)(2,1)S(1)} %copy-done.3, bf16[768,1024]{1,0:T(8,128)(2,1)S(1)} %copy-done.21), kind=kOutput, calls=%fused_computation.23 | convolution fusion | flops 806354944 | bytes 5505024 | tf_op jit(solution)/shard_map/dot_general | solution.py:59
  164.9 19.2 %all-to-all-done.4 = bf16[128,6,1024]{2,1,0:T(8,128)(2,1)S(1)} async-done(((bf16[128,6,1024]{2,1,0:T(8,128)(2,1)}), bf16[128,6,1024]{2,1,0:T(8,128)(2,1)S(1)}, u32[]{:S(2)}, u32[]{:S(2)}) %all-to-all-start.4) | async-done | bytes 1572896 | tf_op jit(solution)/shard_map/all_to_all | solution.py:30
  184.1 1.4 reshape.128
  185.5 2.0 %fusion.27 = f32[256,1024]{1,0:T(8,128)S(1)} fusion(bf16[768,1024]{1,0:T(8,128)(2,1)} %reshape.128, s32[256]{0:T(256)S(1)} %multiply_add_fusion), kind=kOutput, calls=%fused_computation.50 | convolution fusion | flops 402849792 | bytes 2622464 | tf_op jit(solution)/shard_map/dot_general | solution.py:163
  (120 shorter events, 33.9 us)
Async XLA Ops:
  0.6 127.6 %copy-start = (bf16[1,512,1024]{2,1,0:T(8,128)(2,1)S(1)}, bf16[1,512,1024]{2,1,0:T(8,128)(2,1)}, u32[]{:S(2)}) copy-start(bf16[1,512,1024]{2,1,0:T(8,128)(2,1)} %param.20) | copy-start | bytes 3145732
  6.5 9.6 %copy-start.17 = (s32[1,128,2]{1,2,0:T(2,128)S(1)}, s32[1,128,2]{1,2,0:T(2,128)}, u32[]{:S(2)}) copy-start(s32[1,128,2]{1,2,0:T(2,128)} %param.16) | copy-start | bytes 3076
  6.5 10.8 %copy-start.18 = (f32[1,128,2]{1,2,0:T(2,128)S(1)}, f32[1,128,2]{1,2,0:T(2,128)}, u32[]{:S(2)}) copy-start(f32[1,128,2]{1,2,0:T(2,128)} %param.17) | copy-start | bytes 3076
  6.5 11.1 %copy-start.16 = (bf16[1,128,512]{2,1,0:T(8,128)(2,1)S(1)}, bf16[1,128,512]{2,1,0:T(8,128)(2,1)}, u32[]{:S(2)}) copy-start(bf16[1,128,512]{2,1,0:T(8,128)(2,1)} %param.18) | copy-start | bytes 393220
  6.5 28.8 %all-to-all-start = ((bf16[32,160,128]{2,1,0:T(8,128)(2,1)}), bf16[32,160,128]{2,1,0:T(8,128)(2,1)S(1)}, u32[]{:S(2)}, u32[]{:S(2)}) async-start(bf16[32,160,128]{2,1,0:T(8,128)(2,1)} %fusion.6), calls=%async_computation | async-start | bytes 2621440 | tf_op jit(solution)/shard_map/all_to_all | solution.py:80
  44.5 12.7 %all-to-all-start.1 = ((bf16[32,2,1024]{2,1,0:T(2,128)(2,1)}), bf16[32,2,1024]{2,1,0:T(2,128)(2,1)S(1)}, u32[]{:S(2)}, u32[]{:S(2)}) async-start(bf16[32,2,1024]{2,1,0:T(2,128)(2,1)} %reshape.134), calls=%async_computation.1 | async-start | bytes 262144 | tf_op jit(solution)/shard_map/all_to_all | solution.py:112
  51.2 12.6 %copy-start.15 = (bf16[512,512]{1,0:T(8,128)(2,1)S(1)}, bf16[512,512]{1,0:T(8,128)(2,1)}, u32[]{:S(2)}) copy-start(bf16[512,512]{1,0:T(8,128)(2,1)} %param.15) | copy-start | bytes 1572868
  57.2 25.1 %all-to-all-start.3 = ((bf16[128,6,512]{2,1,0:T(8,128)(2,1)}), bf16[128,6,512]{2,1,0:T(8,128)(2,1)S(1)}, u32[]{:S(2)}, u32[]{:S(2)}) async-start(bf16[128,6,512]{2,1,0:T(8,128)(2,1)} %reshape.123), calls=%async_computation.3 | async-start | bytes 2097152 | tf_op jit(solution)/shard_map/all_to_all | solution.py:26
  82.3 23.8 %all-to-all-start.2 = ((bf16[128,6,512]{2,1,0:T(8,128)(2,1)}), bf16[128,6,512]{2,1,0:T(8,128)(2,1)S(1)}, u32[]{:S(2)}, u32[]{:S(2)}) async-start(bf16[128,6,512]{2,1,0:T(8,128)(2,1)} %reshape.120), calls=%async_computation.2 | async-start | bytes 2097152 | tf_op jit(solution)/shard_map/all_to_all | solution.py:26
  87.9 23.0 %collective-permute-start.1 = (bf16[128,6,512]{2,0,1:T(8,128)(2,1)}, bf16[128,6,512]{2,0,1:T(8,128)(2,1)}, u32[]{:S(2)}, u32[]{:S(2)}) collective-permute-start(bf16[128,6,512]{2,0,1:T(8,128)(2,1)} %copy.42), channel_id=1, source_target_pairs={{0,1},{1,0},{2,3},{3,2},{4,5},{5,4},{6,7},{7,6},{8,9},{9,8},{10,11... | collective-permute-start | bytes 2359304 | tf_op jit(solution)/shard_map/ppermute | solution.py:41
  90.2 18.0 %copy-start.7 = (bf16[1,1024,512]{2,1,0:T(8,128)(2,1)S(1)}, bf16[1,1024,512]{2,1,0:T(8,128)(2,1)}, u32[]{:S(2)}) copy-start(bf16[1,1024,512]{2,1,0:T(8,128)(2,1)} %param.21) | copy-start | bytes 3145732
  106.1 2.1 %copy-start.11 = (bf16[768,512]{1,0:T(8,128)(2,1)S(1)}, bf16[768,512]{1,0:T(8,128)(2,1)}, u32[]{:S(2)}) copy-start(bf16[768,512]{1,0:T(8,128)(2,1)} %reshape.124) | copy-start | bytes 2359300
  107.2 16.6 %collective-permute-start = (bf16[128,6,512]{2,0,1:T(8,128)(2,1)}, bf16[128,6,512]{2,0,1:T(8,128)(2,1)}, u32[]{:S(2)}, u32[]{:S(2)}) collective-permute-start(bf16[128,6,512]{2,0,1:T(8,128)(2,1)} %copy.40), channel_id=1, source_target_pairs={{0,1},{1,0},{2,3},{3,2},{4,5},{5,4},{6,7},{7,6},{8,9},{9,8},{10,11... | collective-permute-start | bytes 2359304 | tf_op jit(solution)/shard_map/ppermute | solution.py:41
  119.7 4.1 %copy-start.4 = (bf16[768,512]{1,0:T(8,128)(2,1)}, bf16[768,512]{1,0:T(8,128)(2,1)S(1)}, u32[]{:S(2)}) copy-start(bf16[768,512]{1,0:T(8,128)(2,1)S(1)} %reshape.121) | copy-start | bytes 2359300
  125.7 2.6 %copy-start.2 = (bf16[768,512]{1,0:T(8,128)(2,1)}, bf16[768,512]{1,0:T(8,128)(2,1)S(1)}, u32[]{:S(2)}) copy-start(bf16[768,512]{1,0:T(8,128)(2,1)S(1)} %reshape.125) | copy-start | bytes 2359300
  125.7 2.6 %copy-start.14 = (f32[768,1024]{1,0:T(8,128)S(1)}, f32[768,1024]{1,0:T(8,128)}, u32[]{:S(2)}) copy-start(f32[768,1024]{1,0:T(8,128)} %fusion.7) | copy-start | bytes 9437188
  128.3 2.4 %copy-start.9 = (bf16[1,512,1024]{2,1,0:T(8,128)(2,1)S(1)}, bf16[1,512,1024]{2,1,0:T(8,128)(2,1)}, u32[]{:S(2)}) copy-start(bf16[1,512,1024]{2,1,0:T(8,128)(2,1)} %param.19) | copy-start | bytes 3145732
  130.6 1.6 copy-start.24
  130.6 3.1 %copy-start.22 = (bf16[768,1024]{1,0:T(8,128)(2,1)}, bf16[768,1024]{1,0:T(8,128)(2,1)S(1)}, u32[]{:S(2)}) copy-start(bf16[768,1024]{1,0:T(8,128)(2,1)S(1)} %get-tuple-element.10) | copy-start | bytes 4718596
  130.6 2.0 %copy-start.8 = (bf16[1,1024,512]{2,1,0:T(8,128)(2,1)S(1)}, bf16[1,1024,512]{2,1,0:T(8,128)(2,1)}, u32[]{:S(2)}) copy-start(bf16[1,1024,512]{2,1,0:T(8,128)(2,1)} %param.21) | copy-start | bytes 3145732
  133.7 2.1 %copy-start.13 = (f32[768,1024]{1,0:T(8,128)S(1)}, f32[768,1024]{1,0:T(8,128)}, u32[]{:S(2)}) copy-start(f32[768,1024]{1,0:T(8,128)} %fusion.10) | copy-start | bytes 9437188
  134.8 2.2 %copy-start.1 = (f32[768,1024]{1,0:T(8,128)S(1)}, f32[768,1024]{1,0:T(8,128)}, u32[]{:S(2)}) copy-start(f32[768,1024]{1,0:T(8,128)} %fusion.25) | copy-start | bytes 9437188
  134.9 10.1 %collective-permute-start.2 = (bf16[768,1024]{0,1:T(8,128)(2,1)S(1)}, bf16[768,1024]{0,1:T(8,128)(2,1)S(1)}, u32[]{:S(2)}, u32[]{:S(2)}) collective-permute-start(bf16[768,1024]{0,1:T(8,128)(2,1)S(1)} %pad_maximum_fusion), channel_id=1, source_target_pairs={{0,1},{1,0},{2,3},{3,2},{4,5},{5,4},{6,7},{7,6},{8,9},{9,8},{10,11... | collective-permute-start | bytes 4718600 | tf_op jit(solution)/shard_map/ppermute | solution.py:159
  139.3 4.6 %copy-start.28 = (bf16[768,1024]{1,0:T(8,128)(2,1)}, bf16[768,1024]{1,0:T(8,128)(2,1)S(1)}, u32[]{:S(2)}) copy-start(bf16[768,1024]{1,0:T(8,128)(2,1)S(1)} %get-tuple-element.7) | copy-start | bytes 4718596
  150.0 34.1 %all-to-all-start.4 = ((bf16[128,6,1024]{2,1,0:T(8,128)(2,1)}), bf16[128,6,1024]{2,1,0:T(8,128)(2,1)S(1)}, u32[]{:S(2)}, u32[]{:S(2)}) async-start(bf16[128,6,1024]{2,1,0:T(8,128)(2,1)} %reshape.127), calls=%async_computation.4 | async-start | bytes 4194304 | tf_op jit(solution)/shard_map/all_to_all | solution.py:30
  153.8 2.8 %copy-start.6 = (bf16[768,512]{1,0:T(8,128)(2,1)S(1)}, bf16[768,512]{1,0:T(8,128)(2,1)}, u32[]{:S(2)}) copy-start(bf16[768,512]{1,0:T(8,128)(2,1)} %copy-done.4) | copy-start | bytes 2359300
  153.8 2.8 %copy-start.27 = (bf16[768,1024]{1,0:T(8,128)(2,1)S(1)}, bf16[768,1024]{1,0:T(8,128)(2,1)}, u32[]{:S(2)}) copy-start(bf16[768,1024]{1,0:T(8,128)(2,1)} %copy-done.26) | copy-start | bytes 4718596
  156.7 1.8 copy-start.19
  156.7 2.3 %copy-start.25 = (bf16[768,1024]{1,0:T(8,128)(2,1)S(1)}, bf16[768,1024]{1,0:T(8,128)(2,1)}, u32[]{:S(2)}) copy-start(bf16[768,1024]{1,0:T(8,128)(2,1)} %copy-done.24) | copy-start | bytes 4718596
  159.0 2.0 %copy-start.3 = (bf16[768,512]{1,0:T(8,128)(2,1)S(1)}, bf16[768,512]{1,0:T(8,128)(2,1)}, u32[]{:S(2)}) copy-start(bf16[768,512]{1,0:T(8,128)(2,1)} %copy-done.2) | copy-start | bytes 2359300
  159.0 2.0 %copy-start.23 = (bf16[768,1024]{1,0:T(8,128)(2,1)S(1)}, bf16[768,1024]{1,0:T(8,128)(2,1)}, u32[]{:S(2)}) copy-start(bf16[768,1024]{1,0:T(8,128)(2,1)} %copy-done.22) | copy-start | bytes 4718596
  160.9 2.0 %copy-start.21 = (bf16[768,1024]{1,0:T(8,128)(2,1)S(1)}, bf16[768,1024]{1,0:T(8,128)(2,1)}, u32[]{:S(2)}) copy-start(bf16[768,1024]{1,0:T(8,128)(2,1)} %copy-done.20) | copy-start | bytes 4718596
  (5 other events, 6.1 us)

commit v2 on v1

--- a/solution.py
+++ b/solution.py
@@ -36,28 +36,29 @@
 
 
 def spread(slots):
-    half = CAP // PIECES
-    got = to_experts(slots.reshape(EXPERTS * PIECES, half, slots.shape[1]))
+    got = to_experts(slots)
     other = lax.ppermute(got, "blk", partner_pairs())
-    return got.reshape(-1, slots.shape[1]), other.reshape(-1, slots.shape[1])
+    return got, other
 
 
 def piece_pass(inputs, cots, gate_mat, up_mat, down_mat):
-    pre_gate = jnp.dot(inputs, gate_mat, preferred_element_type=jnp.float32)
-    pre_up = jnp.dot(inputs, up_mat, preferred_element_type=jnp.float32)
+    pre_gate = jnp.einsum("scd,df->scf", inputs, gate_mat, preferred_element_type=jnp.float32)
+    pre_up = jnp.einsum("scd,df->scf", inputs, up_mat, preferred_element_type=jnp.float32)
     activated = jax.nn.silu(pre_gate)
     hidden = (activated * pre_up).astype(jnp.bfloat16)
-    output = jnp.dot(hidden, down_mat, preferred_element_type=jnp.float32).astype(jnp.bfloat16)
-    grad_hidden = jnp.dot(cots, down_mat.T, preferred_element_type=jnp.float32)
+    output = jnp.einsum(
+        "scf,fd->scd", hidden, down_mat, preferred_element_type=jnp.float32
+    ).astype(jnp.bfloat16)
+    grad_hidden = jnp.einsum("scd,fd->scf", cots, down_mat, preferred_element_type=jnp.float32)
     grad_pre_gate = (grad_hidden * pre_up * silu_grad(pre_gate)).astype(jnp.bfloat16)
     grad_pre_up = (grad_hidden * activated).astype(jnp.bfloat16)
     grad_inputs = (
-        jnp.dot(grad_pre_gate, gate_mat.T, preferred_element_type=jnp.float32)
-        + jnp.dot(grad_pre_up, up_mat.T, preferred_element_type=jnp.float32)
-    ).astype(jnp.bfloat16)
-    grad_down = jnp.dot(hidden.T, cots, preferred_element_type=jnp.float32)
-    grad_gate = jnp.dot(inputs.T, grad_pre_gate, preferred_element_type=jnp.float32)
-    grad_up = jnp.dot(inputs.T, grad_pre_up, preferred_element_type=jnp.float32)
+        jnp.einsum("scf,df->scd", grad_pre_gate, gate_mat, preferred_element_type=jnp.float32)
+        + jnp.einsum("scf,df->scd", grad_pre_up, up_mat, preferred_element_type=jnp.float32)
+    ).astype(jnp.bfloat16)
+    grad_down = jnp.einsum("scf,scd->fd", hidden, cots, preferred_element_type=jnp.float32)
+    grad_gate = jnp.einsum("scd,scf->df", inputs, grad_pre_gate, preferred_element_type=jnp.float32)
+    grad_up = jnp.einsum("scd,scf->df", inputs, grad_pre_up, preferred_element_type=jnp.float32)
     return (jnp.concatenate([output, grad_inputs], axis=-1), grad_gate, grad_up, grad_down)
 
 
@@ -138,9 +139,12 @@
     slot_index = route_experts * CAP + position
     grad_flat = cotangent[0].astype(jnp.float32)
     route_cots = (gates[:, None] * jnp.repeat(grad_flat, TOP, axis=0)).astype(jnp.bfloat16)
-    slot_ids = jnp.arange(EXPERTS * CAP, dtype=jnp.int32)
-    placing = (slot_ids[:, None] == slot_index[None, :]).astype(jnp.bfloat16)
-    cot_slots = jnp.dot(placing, route_cots, preferred_element_type=jnp.float32).astype(jnp.bfloat16)
+    half = CAP // PIECES
+    slot_ids = jnp.arange(EXPERTS * CAP, dtype=jnp.int32).reshape(EXPERTS * PIECES, half)
+    placing = (slot_ids[:, :, None] == slot_index[None, None, :]).astype(jnp.bfloat16)
+    cot_slots = jnp.einsum(
+        "jcr,rw->jcw", placing, route_cots, preferred_element_type=jnp.float32
+    ).astype(jnp.bfloat16)
     cot_own, cot_other = spread(cot_slots)
     attended = attend_heads(queries[0], key_rows[0], value_rows[0])
     stream = residual[0].astype(jnp.float32) + jnp.dot(
@@ -149,8 +153,8 @@
     radius = jnp.sqrt(jnp.mean(stream * stream, axis=-1, keepdims=True) + 1e-06)
     unit = stream / radius
     normed = unit.astype(jnp.bfloat16)
-    in_slots = jnp.dot(
-        placing, jnp.repeat(normed, TOP, axis=0), preferred_element_type=jnp.float32
+    in_slots = jnp.einsum(
+        "jcr,rw->jcw", placing, jnp.repeat(normed, TOP, axis=0), preferred_element_type=jnp.float32
     ).astype(jnp.bfloat16)
     in_own, in_other = spread(in_slots)
     mats = (w_gate[0], w_up[0], w_down[0])
@@ -158,9 +162,9 @@
     other, gate_b, up_b, down_b = piece_pass(in_other, cot_other, *mats)
     theirs = lax.ppermute(other, "blk", partner_pairs())
     summed = (own.astype(jnp.float32) + theirs.astype(jnp.float32)).astype(jnp.bfloat16)
-    back = to_anchor(summed.reshape(EXPERTS * PIECES, CAP // PIECES, 2 * D))
-    picking = (slot_index[:, None] == slot_ids[None, :]).astype(jnp.bfloat16)
-    picked = jnp.dot(picking, back.reshape(EXPERTS * CAP, 2 * D), preferred_element_type=jnp.float32)
+    back = to_anchor(summed)
+    picking = (slot_index[:, None, None] == slot_ids[None, :, :]).astype(jnp.bfloat16)
+    picked = jnp.einsum("rjc,jcw->rw", picking, back, preferred_element_type=jnp.float32)
     route_out = picked[:, :D]
     route_grad = picked[:, D:]
     grad_gate = (gate_a + gate_b).astype(jnp.bfloat16)[None]

time: 191 us -> 177 us (0.927)
  local copies, waits for them, and re-layouts: 31.4 us -> 19 us
  matrix products: 40.1 us -> 36.9 us
  starting transfers between devices: 31.2 us -> 33.7 us
    reshape x8 -> x0, local copies, waits for them, and re-layouts: 9.34 us -> none  [the longest x4 3.77 us: spread(): return (got.reshape(-1, slots.shape[1]), other.reshape(-1, slots.shape[1]))]
    ppermute x2 -> x0, local copies, waits for them, and re-layouts: 4.12 us -> none  [spread(): other = lax.ppermute(got, 'blk', partner_pairs())]
    dot_general x21, matrix products: 38.9 us -> 35.6 us  [the longest x2 6.76 us: piece_pass(): jnp.einsum('scf,scd->fd', hidden, cots, preferred_element_type=jnp.float32)]
    convert_element_type x0 -> x2, local copies, waits for them, and re-layouts: none -> 2.83 us  [the longest x1 1.41 us: block(): cot_slots = jnp.einsum('jcr,rw->jcw', placing, route_cots, preferred_elem...]
    unnamed x64 -> x44, local copies, waits for them, and re-layouts: 7.78 us -> 5.27 us
  transfers between devices with their start and end apart: 8 -> 8, of which waited for: 5 -> 5; matrix products, arithmetic and copies ran while one was open for 24% -> 21% of each run, Pallas kernels for 0% -> 0%
where the time goes in v2:
time: 177 us; the launch traced here: 176 us
  waiting for transfers between devices  71.2 us (40%)
  matrix products  36.9 us (21%)
  starting transfers between devices  33.7 us (19%)
  local copies, waits for them, and re-layouts  19 us (11%)
  Pallas kernels  8.26 us (5%)
  other arithmetic  5.71 us (3%)
    all_to_all x2, waiting for transfers between devices, to_experts(): lax.all_to_all(buffer, ('table', 'blk'), split_axis=0, concat_axis=0, til...  31.8 us
    all_to_all x1, waiting for transfers between devices, to_anchor(): lax.all_to_all(buffer, ('table', 'blk'), split_axis=0, concat_axis=0, til...  18.4 us
    all_to_all x1, waiting for transfers between devices, attend_heads(): got = lax.all_to_all(parcel, 'blk', 0, 0, tiled=True)  15.2 us
    all_to_all x2, starting transfers between devices, to_experts(): lax.all_to_all(buffer, ('table', 'blk'), split_axis=0, concat_axis=0, til...  11.4 us
    all_to_all x1, starting transfers between devices, attend_heads(): got = lax.all_to_all(parcel, 'blk', 0, 0, tiled=True)  9.55 us
    pallas_call x1, Pallas kernels, attend_heads(): pl.pallas_call(kernel, grid=(steps,), in_specs=[pl.BlockSpec(got.shape, l...  8.26 us
    dot_general x2, matrix products, piece_pass(): jnp.einsum('scf,scd->fd', hidden, cots, preferred_element_type=jnp.float32)  6.76 us
    all_to_all x1, waiting for transfers between devices, attend_heads(): back = lax.all_to_all(mixed, 'blk', 0, 0, tiled=True)  5.84 us
  transfers between devices with their start and end apart: 8, of which 5 were waited for; matrix products, arithmetic and copies ran while one was open for 21% of the time, Pallas kernels for 0%

profile of v2, /device:TPU:1, one launch (start us, length us, event | category | flops | bytes accessed | tf_op | source)
XLA Modules:
  0.0 176.0 jit_solution(9148336705352756023)
XLA Ops:
  0.6 1.1 copy.41
  4.8 1.7 fusion.14
  6.5 9.6 %all-to-all-start = ((bf16[32,160,128]{2,1,0:T(8,128)(2,1)}), bf16[32,160,128]{2,1,0:T(8,128)(2,1)S(1)}, u32[]{:S(2)}, u32[]{:S(2)}) async-start(bf16[32,160,128]{2,1,0:T(8,128)(2,1)} %fusion.14), calls=%async_computation | async-start | bytes 2621440 | tf_op jit(solution)/shard_map/all_to_all | solution.py:81
  18.6 1.4 reshape.116
  20.2 15.2 %all-to-all-done.got_ref = bf16[32,160,128]{2,1,0:T(8,128)(2,1)S(1)} async-done(((bf16[32,160,128]{2,1,0:T(8,128)(2,1)}), bf16[32,160,128]{2,1,0:T(8,128)(2,1)S(1)}, u32[]{:S(2)}, u32[]{:S(2)}) %all-to-all-start) | async-done | bytes 1310752 | tf_op jit(solution)/shard_map/all_to_all | solution.py:81
  35.4 8.3 %shard_map.146 = bf16[32,32,64]{2,1,0:T(8,128)(2,1)S(1)} custom-call(bf16[32,160,128]{2,1,0:T(8,128)(2,1)S(1)} %all-to-all-done.got_ref), custom_call_target="tpu_custom_call" | custom-call | flops 2147483648 | bytes 1441792 | tf_op jit(solution)/shard_map/pallas_call | solution.py:100
  44.5 5.0 %all-to-all-start.1 = ((bf16[32,2,1024]{2,1,0:T(2,128)(2,1)}), bf16[32,2,1024]{2,1,0:T(2,128)(2,1)S(1)}, u32[]{:S(2)}, u32[]{:S(2)}) async-start(bf16[32,2,1024]{2,1,0:T(2,128)(2,1)} %reshape.135), calls=%async_computation.1 | async-start | bytes 262144 | tf_op jit(solution)/shard_map/all_to_all | solution.py:113
  50.0 1.4 copy.54
  51.4 5.8 %all-to-all-done.1 = bf16[32,2,1024]{2,1,0:T(2,128)(2,1)S(1)} async-done(((bf16[32,2,1024]{2,1,0:T(2,128)(2,1)}), bf16[32,2,1024]{2,1,0:T(2,128)(2,1)S(1)}, u32[]{:S(2)}, u32[]{:S(2)}) %all-to-all-start.1) | async-done | bytes 131104 | tf_op jit(solution)/shard_map/all_to_all | solution.py:113
  57.2 5.9 %all-to-all-start.3 = ((bf16[128,6,512]{2,1,0:T(8,128)(2,1)}), bf16[128,6,512]{2,1,0:T(8,128)(2,1)S(1)}, u32[]{:S(2)}, u32[]{:S(2)}) async-start(bf16[128,6,512]{2,1,0:T(8,128)(2,1)} %copy.54), calls=%async_computation.3 | async-start | bytes 2097152 | tf_op jit(solution)/shard_map/all_to_all | solution.py:26
  63.8 1.2 multiply_reduce_fusion.1
  65.8 1.4 copy.51
  67.2 15.2 %all-to-all-done.3 = bf16[128,6,512]{2,1,0:T(8,128)(2,1)S(1)} async-done(((bf16[128,6,512]{2,1,0:T(8,128)(2,1)}), bf16[128,6,512]{2,1,0:T(8,128)(2,1)S(1)}, u32[]{:S(2)}, u32[]{:S(2)}) %all-to-all-start.3) | async-done | bytes 786464 | tf_op jit(solution)/shard_map/all_to_all | solution.py:26
  82.4 5.4 %all-to-all-start.2 = ((bf16[128,6,512]{2,1,0:T(8,128)(2,1)}), bf16[128,6,512]{2,1,0:T(8,128)(2,1)}, u32[]{:S(2)}, u32[]{:S(2)}) async-start(bf16[128,6,512]{2,1,0:T(8,128)(2,1)} %copy.51), calls=%async_computation.2 | async-start | bytes 2097152 | tf_op jit(solution)/shard_map/all_to_all | solution.py:26
  87.8 1.1 copy.55
  88.9 1.3 collective-permute-start.1
  90.2 16.6 %all-to-all-done.2 = bf16[128,6,512]{2,1,0:T(8,128)(2,1)} async-done(((bf16[128,6,512]{2,1,0:T(8,128)(2,1)}), bf16[128,6,512]{2,1,0:T(8,128)(2,1)}, u32[]{:S(2)}, u32[]{:S(2)}) %all-to-all-start.2) | async-done | bytes 786464 | tf_op jit(solution)/shard_map/all_to_all | solution.py:26
  106.8 1.5 copy.52
  108.3 1.2 collective-permute-start
  109.5 2.1 %fusion.18 = f32[128,6,1024]{2,0,1:T(8,128)S(1)} fusion(bf16[128,6,512]{2,0,1:T(8,128)(2,1)} %copy.55, bf16[1,1024,512]{2,1,0:T(8,128)(2,1)S(1)} %copy-done.1), kind=kOutput, calls=%fused_computation.37 | convolution fusion | flops 805306368 | bytes 4980736 | tf_op jit(solution)/shard_map/scd,fd->scf/dot_general | solution.py:52
  111.7 2.2 %fusion.15 = f32[128,6,1024]{2,0,1:T(8,128)S(1)} fusion(bf16[128,6,512]{2,0,1:T(8,128)(2,1)} %collective-permute-done.1, bf16[1,1024,512]{2,1,0:T(8,128)(2,1)S(1)} %copy-done.1), kind=kOutput, calls=%fused_computation.34 | convolution fusion | flops 805306368 | bytes 4980736 | tf_op jit(solution)/shard_map/scd,fd->scf/dot_general | solution.py:52
  115.9 2.3 %multiply_convert_fusion.2 = (bf16[128,6,1024]{2,0,1:T(8,128)(2,1)S(1)}, bf16[128,6,1024]{2,0,1:T(8,128)(2,1)S(1)}, bf16[128,6,1024]{2,0,1:T(8,128)(2,1)S(1)}) fusion(f32[128,6,1024]{2,0,1:T(8,128)S(1)} %fusion.29, f32[128,6,1024]{2,0,1:T(8,128)S(1)} %fusion.15, bf16[128,6,512]{2,0,1:T(8,128)(2,1)S(1)} %collective-permute-done, ...), kind=kOutput, calls=%fused_computation.3 | convolution fusion | flops 817102848 | bytes 12845056 | tf_op jit(solution)/shard_map/scd,df->scf/dot_general | solution.py:46
  122.4 2.3 %multiply_convert_fusion.5 = (bf16[128,6,1024]{2,0,1:T(8,128)(2,1)S(1)}, bf16[128,6,1024]{2,0,1:T(8,128)(2,1)S(1)}, bf16[128,6,1024]{2,0,1:T(8,128)(2,1)S(1)}) fusion(f32[128,6,1024]{2,0,1:T(8,128)S(1)} %fusion.33, f32[128,6,1024]{2,0,1:T(8,128)S(1)} %fusion.18, bf16[128,6,512]{2,0,1:T(8,128)(2,1)S(1)} %copy.52, bf16[1,512,1024]{2,1,0:T(8,128)(2,1)S(1)} %copy-done), kind=kOutput, calls=%fused_computation.8 | convolution fusion | flops 817102848 | bytes 12845056 | tf_op jit(solution)/shard_map/scd,df->scf/dot_general | solution.py:46
  127.0 3.5 %fusion.57 = f32[1024,512,1]{1,0,2:T(8,128)} fusion(bf16[128,6,1024]{2,0,1:T(8,128)(2,1)S(1)} %get-tuple-element.5, bf16[128,6,512]{2,0,1:T(8,128)(2,1)} %copy.55), kind=kOutput, calls=%fused_computation.93 | convolution fusion | flops 805306368 | bytes 4456448 | tf_op jit(solution)/shard_map/scf,scd->fd/dot_general | solution.py:59
  132.0 2.2 %copy.58 = bf16[128,6,1024]{2,1,0:T(8,128)(2,1)} copy(bf16[128,6,1024]{2,0,1:T(8,128)(2,1)S(1)} %add_convert_fusion) | data formatting | bytes 3145728 | tf_op jit(solution)/shard_map/convert_element_type | solution.py:164
  134.2 5.0 %all-to-all-start.4 = ((bf16[128,6,1024]{2,1,0:T(8,128)(2,1)}), bf16[128,6,1024]{2,1,0:T(8,128)(2,1)}, u32[]{:S(2)}, u32[]{:S(2)}) async-start(bf16[128,6,1024]{2,1,0:T(8,128)(2,1)} %copy.58), calls=%async_computation.4 | async-start | bytes 4194304 | tf_op jit(solution)/shard_map/all_to_all | solution.py:30
  139.2 2.5 %fusion.56 = f32[512,1024,1]{1,0,2:T(8,128)S(1)} fusion(bf16[128,6,512]{2,0,1:T(8,128)(2,1)S(1)} %copy.52, bf16[128,6,1024]{2,0,1:T(8,128)(2,1)} %copy-done.18), kind=kOutput, calls=%fused_computation.92 | convolution fusion | flops 805306368 | bytes 4456448 | tf_op jit(solution)/shard_map/scd,scf->df/dot_general | solution.py:61
  143.8 3.3 %fusion.13 = bf16[1,1024,512]{2,1,0:T(8,128)(2,1)} fusion(bf16[128,6,1024]{2,0,1:T(8,128)(2,1)S(1)} %copy-done.15, bf16[128,6,512]{2,0,1:T(8,128)(2,1)} %collective-permute-done.1, f32[1024,512,1]{1,0,2:T(8,128)S(1)} %copy-done.9), kind=kOutput, calls=%fused_computation.31 | convolution fusion | flops 806354944 | bytes 5505024 | tf_op jit(solution)/shard_map/scf,scd->fd/dot_general | solution.py:59
  147.1 2.0 %fusion.12 = bf16[1,512,1024]{2,1,0:T(8,128)(2,1)} fusion(bf16[128,6,512]{2,0,1:T(8,128)(2,1)S(1)} %copy-done.4, bf16[128,6,1024]{2,0,1:T(8,128)(2,1)S(1)} %copy-done.13, f32[512,1024,1]{1,0,2:T(8,128)S(1)} %fusion.56), kind=kOutput, calls=%fused_computation.30 | convolution fusion | flops 806354944 | bytes 5505024 | tf_op jit(solution)/shard_map/scd,scf->df/dot_general | solution.py:61
  149.1 2.0 %fusion.11 = bf16[1,512,1024]{2,1,0:T(8,128)(2,1)} fusion(bf16[128,6,512]{2,0,1:T(8,128)(2,1)S(1)} %copy-done.4, bf16[128,6,1024]{2,0,1:T(8,128)(2,1)S(1)} %copy-done.11, f32[512,1024,1]{1,0,2:T(8,128)S(1)} %fusion.55), kind=kOutput, calls=%fused_computation.29 | convolution fusion | flops 806354944 | bytes 5505024 | tf_op jit(solution)/shard_map/scd,scf->df/dot_general | solution.py:60
  151.1 18.4 %all-to-all-done.4 = bf16[128,6,1024]{2,1,0:T(8,128)(2,1)} async-done(((bf16[128,6,1024]{2,1,0:T(8,128)(2,1)}), bf16[128,6,1024]{2,1,0:T(8,128)(2,1)}, u32[]{:S(2)}, u32[]{:S(2)}) %all-to-all-start.4) | async-done | bytes 1572896 | tf_op jit(solution)/shard_map/all_to_all | solution.py:30
  169.5 3.6 %fusion.8 = f32[256,1024]{1,0:T(8,128)S(1)} fusion(bf16[128,6,1024]{2,1,0:T(8,128)(2,1)} %all-to-all-done.4, s32[128,6]{0,1:T(8,128)S(1)} %multiply_add_fusion, s32[256]{0:T(256)S(1)} %multiply_add_fusion.1), kind=kOutput, calls=%fused_computation.28 | convolution fusion | flops 402849792 | bytes 2625536 | tf_op jit(solution)/shard_map/rjc,jcw->rw/dot_general | solution.py:167
  (93 shorter events, 23.1 us)
Async XLA Ops:
  0.6 115.3 %copy-start = (bf16[1,512,1024]{2,1,0:T(8,128)(2,1)S(1)}, bf16[1,512,1024]{2,1,0:T(8,128)(2,1)}, u32[]{:S(2)}) copy-start(bf16[1,512,1024]{2,1,0:T(8,128)(2,1)} %param.20) | copy-start | bytes 3145732
  6.5 9.6 %copy-start.7 = (s32[1,128,2]{1,2,0:T(2,128)S(1)}, s32[1,128,2]{1,2,0:T(2,128)}, u32[]{:S(2)}) copy-start(s32[1,128,2]{1,2,0:T(2,128)} %param.16) | copy-start | bytes 3076
  6.5 10.8 %copy-start.8 = (f32[1,128,2]{1,2,0:T(2,128)S(1)}, f32[1,128,2]{1,2,0:T(2,128)}, u32[]{:S(2)}) copy-start(f32[1,128,2]{1,2,0:T(2,128)} %param.17) | copy-start | bytes 3076
  6.5 11.1 %copy-start.6 = (bf16[1,128,512]{2,1,0:T(8,128)(2,1)S(1)}, bf16[1,128,512]{2,1,0:T(8,128)(2,1)}, u32[]{:S(2)}) copy-start(bf16[1,128,512]{2,1,0:T(8,128)(2,1)} %param.18) | copy-start | bytes 393220
  6.5 28.8 %all-to-all-start = ((bf16[32,160,128]{2,1,0:T(8,128)(2,1)}), bf16[32,160,128]{2,1,0:T(8,128)(2,1)S(1)}, u32[]{:S(2)}, u32[]{:S(2)}) async-start(bf16[32,160,128]{2,1,0:T(8,128)(2,1)} %fusion.14), calls=%async_computation | async-start | bytes 2621440 | tf_op jit(solution)/shard_map/all_to_all | solution.py:81
  44.5 12.7 %all-to-all-start.1 = ((bf16[32,2,1024]{2,1,0:T(2,128)(2,1)}), bf16[32,2,1024]{2,1,0:T(2,128)(2,1)S(1)}, u32[]{:S(2)}, u32[]{:S(2)}) async-start(bf16[32,2,1024]{2,1,0:T(2,128)(2,1)} %reshape.135), calls=%async_computation.1 | async-start | bytes 262144 | tf_op jit(solution)/shard_map/all_to_all | solution.py:113
  51.4 12.4 %copy-start.5 = (bf16[512,512]{1,0:T(8,128)(2,1)S(1)}, bf16[512,512]{1,0:T(8,128)(2,1)}, u32[]{:S(2)}) copy-start(bf16[512,512]{1,0:T(8,128)(2,1)} %param.15) | copy-start | bytes 1572868
  57.2 25.1 %all-to-all-start.3 = ((bf16[128,6,512]{2,1,0:T(8,128)(2,1)}), bf16[128,6,512]{2,1,0:T(8,128)(2,1)S(1)}, u32[]{:S(2)}, u32[]{:S(2)}) async-start(bf16[128,6,512]{2,1,0:T(8,128)(2,1)} %copy.54), calls=%async_computation.3 | async-start | bytes 2097152 | tf_op jit(solution)/shard_map/all_to_all | solution.py:26
  82.4 24.5 %all-to-all-start.2 = ((bf16[128,6,512]{2,1,0:T(8,128)(2,1)}), bf16[128,6,512]{2,1,0:T(8,128)(2,1)}, u32[]{:S(2)}, u32[]{:S(2)}) async-start(bf16[128,6,512]{2,1,0:T(8,128)(2,1)} %copy.51), calls=%async_computation.2 | async-start | bytes 2097152 | tf_op jit(solution)/shard_map/all_to_all | solution.py:26
  87.8 21.7 %copy-start.1 = (bf16[1,1024,512]{2,1,0:T(8,128)(2,1)S(1)}, bf16[1,1024,512]{2,1,0:T(8,128)(2,1)}, u32[]{:S(2)}) copy-start(bf16[1,1024,512]{2,1,0:T(8,128)(2,1)} %param.21) | copy-start | bytes 3145732
  88.9 22.7 %collective-permute-start.1 = (bf16[128,6,512]{2,0,1:T(8,128)(2,1)}, bf16[128,6,512]{2,0,1:T(8,128)(2,1)}, u32[]{:S(2)}, u32[]{:S(2)}) collective-permute-start(bf16[128,6,512]{2,0,1:T(8,128)(2,1)} %copy.55), channel_id=1, source_target_pairs={{0,1},{1,0},{2,3},{3,2},{4,5},{5,4},{6,7},{7,6},{8,9},{9,8},{10,11... | collective-permute-start | bytes 2359304 | tf_op jit(solution)/shard_map/ppermute | solution.py:40
  108.3 6.6 %collective-permute-start = (bf16[128,6,512]{2,0,1:T(8,128)(2,1)S(1)}, bf16[128,6,512]{2,0,1:T(8,128)(2,1)S(1)}, u32[]{:S(2)}, u32[]{:S(2)}) collective-permute-start(bf16[128,6,512]{2,0,1:T(8,128)(2,1)S(1)} %copy.52), channel_id=1, source_target_pairs={{0,1},{1,0},{2,3},{3,2},{4,5},{5,4},{6,7},{7,6},{8,9},{9,8},{10,11... | collective-permute-start | bytes 2359304 | tf_op jit(solution)/shard_map/ppermute | solution.py:40
  111.7 2.3 %copy-start.2 = (bf16[1,512,1024]{2,1,0:T(8,128)(2,1)S(1)}, bf16[1,512,1024]{2,1,0:T(8,128)(2,1)}, u32[]{:S(2)}) copy-start(bf16[1,512,1024]{2,1,0:T(8,128)(2,1)} %param.19) | copy-start | bytes 3145732
  114.9 1.0 copy-start.3
  118.3 1.1 copy-start.10
  118.3 1.6 copy-start.14
  118.3 2.6 %copy-start.12 = (bf16[128,6,1024]{2,0,1:T(8,128)(2,1)}, bf16[128,6,1024]{2,0,1:T(8,128)(2,1)S(1)}, u32[]{:S(2)}) copy-start(bf16[128,6,1024]{2,0,1:T(8,128)(2,1)S(1)} %get-tuple-element.10) | copy-start | bytes 4718596
  122.1 9.3 %collective-permute-start.2 = (bf16[128,6,1024]{2,0,1:T(8,128)(2,1)S(1)}, bf16[128,6,1024]{2,0,1:T(8,128)(2,1)S(1)}, u32[]{:S(2)}, u32[]{:S(2)}) collective-permute-start(bf16[128,6,1024]{2,0,1:T(8,128)(2,1)S(1)} %pad_maximum_fusion), channel_id=1, source_target_pairs={{0,1},{1,0},{2,3},{3,2},{4,5},{5,4},{6,7},{7,6},{8,9},{9,8},{10,11... | collective-permute-start | bytes 4718600 | tf_op jit(solution)/shard_map/ppermute | solution.py:163
  124.8 1.2 copy-start.16
  124.8 5.7 %copy-start.18 = (bf16[128,6,1024]{2,0,1:T(8,128)(2,1)}, bf16[128,6,1024]{2,0,1:T(8,128)(2,1)S(1)}, u32[]{:S(2)}) copy-start(bf16[128,6,1024]{2,0,1:T(8,128)(2,1)S(1)} %get-tuple-element.7) | copy-start | bytes 4718596
  134.2 35.2 %all-to-all-start.4 = ((bf16[128,6,1024]{2,1,0:T(8,128)(2,1)}), bf16[128,6,1024]{2,1,0:T(8,128)(2,1)}, u32[]{:S(2)}, u32[]{:S(2)}) async-start(bf16[128,6,1024]{2,1,0:T(8,128)(2,1)} %copy.58), calls=%async_computation.4 | async-start | bytes 4194304 | tf_op jit(solution)/shard_map/all_to_all | solution.py:30
  139.2 2.5 %copy-start.17 = (bf16[128,6,1024]{2,0,1:T(8,128)(2,1)S(1)}, bf16[128,6,1024]{2,0,1:T(8,128)(2,1)}, u32[]{:S(2)}) copy-start(bf16[128,6,1024]{2,0,1:T(8,128)(2,1)} %copy-done.16) | copy-start | bytes 4718596
  141.8 1.6 copy-start.9
  141.8 2.0 %copy-start.15 = (bf16[128,6,1024]{2,0,1:T(8,128)(2,1)S(1)}, bf16[128,6,1024]{2,0,1:T(8,128)(2,1)}, u32[]{:S(2)}) copy-start(bf16[128,6,1024]{2,0,1:T(8,128)(2,1)} %copy-done.14) | copy-start | bytes 4718596
  143.8 3.3 %copy-start.4 = (bf16[128,6,512]{2,0,1:T(8,128)(2,1)S(1)}, bf16[128,6,512]{2,0,1:T(8,128)(2,1)}, u32[]{:S(2)}) copy-start(bf16[128,6,512]{2,0,1:T(8,128)(2,1)} %copy-done.3) | copy-start | bytes 2359300
  143.8 3.3 %copy-start.13 = (bf16[128,6,1024]{2,0,1:T(8,128)(2,1)S(1)}, bf16[128,6,1024]{2,0,1:T(8,128)(2,1)}, u32[]{:S(2)}) copy-start(bf16[128,6,1024]{2,0,1:T(8,128)(2,1)} %copy-done.12) | copy-start | bytes 4718596
  147.1 2.0 %copy-start.11 = (bf16[128,6,1024]{2,0,1:T(8,128)(2,1)S(1)}, bf16[128,6,1024]{2,0,1:T(8,128)(2,1)}, u32[]{:S(2)}) copy-start(bf16[128,6,1024]{2,0,1:T(8,128)(2,1)} %copy-done.10) | copy-start | bytes 4718596

commit v3 on v2

--- a/solution.py
+++ b/solution.py
@@ -142,10 +142,6 @@
     half = CAP // PIECES
     slot_ids = jnp.arange(EXPERTS * CAP, dtype=jnp.int32).reshape(EXPERTS * PIECES, half)
     placing = (slot_ids[:, :, None] == slot_index[None, None, :]).astype(jnp.bfloat16)
-    cot_slots = jnp.einsum(
-        "jcr,rw->jcw", placing, route_cots, preferred_element_type=jnp.float32
-    ).astype(jnp.bfloat16)
-    cot_own, cot_other = spread(cot_slots)
     attended = attend_heads(queries[0], key_rows[0], value_rows[0])
     stream = residual[0].astype(jnp.float32) + jnp.dot(
         attended, w_out, preferred_element_type=jnp.float32
@@ -153,10 +149,13 @@
     radius = jnp.sqrt(jnp.mean(stream * stream, axis=-1, keepdims=True) + 1e-06)
     unit = stream / radius
     normed = unit.astype(jnp.bfloat16)
+    route_rows = jnp.concatenate([jnp.repeat(normed, TOP, axis=0), route_cots], axis=1)
     in_slots = jnp.einsum(
-        "jcr,rw->jcw", placing, jnp.repeat(normed, TOP, axis=0), preferred_element_type=jnp.float32
+        "jcr,rw->jcw", placing, route_rows, preferred_element_type=jnp.float32
     ).astype(jnp.bfloat16)
-    in_own, in_other = spread(in_slots)
+    both_own, both_other = spread(in_slots)
+    in_own, cot_own = both_own[..., :D], both_own[..., D:]
+    in_other, cot_other = both_other[..., :D], both_other[..., D:]
     mats = (w_gate[0], w_up[0], w_down[0])
     own, gate_a, up_a, down_a = piece_pass(in_own, cot_own, *mats)
     other, gate_b, up_b, down_b = piece_pass(in_other, cot_other, *mats)

time: 177 us -> 163 us (0.921)
  blocking collectives: 0 us -> 36.2 us
  waiting for transfers between devices: 71.2 us -> 44.9 us
  starting transfers between devices: 33.7 us -> 21.4 us
  matrix products: 36.9 us -> 30.6 us
  local copies, waits for them, and re-layouts: 19 us -> 13.7 us
    all_to_all x0 -> x1, blocking collectives: none -> 36.2 us  [to_experts(): lax.all_to_all(buffer, ('table', 'blk'), split_axis=0, concat_axis=0, til...]
    all_to_all x2 -> x0, waiting for transfers between devices: 31.8 us -> none  [to_experts(): lax.all_to_all(buffer, ('table', 'blk'), split_axis=0, concat_axis=0, til...]
    all_to_all x2 -> x0, starting transfers between devices: 11.4 us -> none  [to_experts(): lax.all_to_all(buffer, ('table', 'blk'), split_axis=0, concat_axis=0, til...]
    dot_general x2, matrix products: 6.76 us -> 4.32 us  [piece_pass(): jnp.einsum('scf,scd->fd', hidden, cots, preferred_element_type=jnp.float32)]
    dot_general x2, matrix products: 4.37 us -> 2.02 us  [piece_pass(): jnp.einsum('scd,fd->scf', cots, down_mat, preferred_element_type=jnp.floa...]
    convert_element_type x2 -> x1, local copies, waits for them, and re-layouts: 2.83 us -> 0.88 us  [block(): in_slots = jnp.einsum('jcr,rw->jcw', placing, route_rows, preferred_eleme...]
    all_to_all x1, waiting for transfers between devices: 5.84 us -> 7.69 us  [attend_heads(): back = lax.all_to_all(mixed, 'blk', 0, 0, tiled=True)]
    unnamed x44 -> x48, local copies, waits for them, and re-layouts: 5.27 us -> 5.35 us
  transfers between devices with their start and end apart: 8 -> 5, of which waited for: 5 -> 4; matrix products, arithmetic and copies ran while one was open for 21% -> 13% of each run, Pallas kernels for 0% -> 0%
where the time goes in v3:
time: 163 us; the launch traced here: 162 us
  waiting for transfers between devices  44.9 us (28%)
  blocking collectives  36.2 us (22%)
  matrix products  30.6 us (19%)
  starting transfers between devices  21.4 us (13%)
  local copies, waits for them, and re-layouts  13.7 us (8%)
  Pallas kernels  8.26 us (5%)
  other arithmetic  5.83 us (4%)
    all_to_all x1, blocking collectives, to_experts(): lax.all_to_all(buffer, ('table', 'blk'), split_axis=0, concat_axis=0, til...  36.2 us
    all_to_all x1, waiting for transfers between devices, to_anchor(): lax.all_to_all(buffer, ('table', 'blk'), split_axis=0, concat_axis=0, til...  19.3 us
    all_to_all x1, waiting for transfers between devices, attend_heads(): got = lax.all_to_all(parcel, 'blk', 0, 0, tiled=True)  16.9 us
    all_to_all x1, starting transfers between devices, attend_heads(): got = lax.all_to_all(parcel, 'blk', 0, 0, tiled=True)  9.55 us
    pallas_call x1, Pallas kernels, attend_heads(): pl.pallas_call(kernel, grid=(steps,), in_specs=[pl.BlockSpec(got.shape, l...  8.26 us
    all_to_all x1, waiting for transfers between devices, attend_heads(): back = lax.all_to_all(mixed, 'blk', 0, 0, tiled=True)  7.69 us
    unnamed x48, local copies, waits for them, and re-layouts  5.35 us
    all_to_all x1, starting transfers between devices, attend_heads(): back = lax.all_to_all(mixed, 'blk', 0, 0, tiled=True)  5.02 us
  transfers between devices with their start and end apart: 5, of which 4 were waited for; matrix products, arithmetic and copies ran while one was open for 13% of the time, Pallas kernels for 0%

profile of v3, /device:TPU:1, one launch (start us, length us, event | category | flops | bytes accessed | tf_op | source)
XLA Modules:
  0.0 162.1 jit_solution(14622403806133234522)
XLA Ops:
  0.6 1.1 copy.41
  1.9 1.0 copy.43
  3.2 1.1 reshape_squeeze.14
  4.8 1.7 %fusion.14 = bf16[32,160,128]{2,1,0:T(8,128)(2,1)} fusion(bf16[32,32,64]{2,1,0:T(8,128)(2,1)S(1)} %bitcast.139, bf16[32,128,64]{2,1,0:T(8,128)(2,1)S(1)} %bitcast.137, bf16[32,128,64]{2,1,0:T(8,128)(2,1)S(1)} %bitcast.138), kind=kLoop, calls=%fused_computation.31 | loop fusion | flops 5242880 | bytes 2490368 | tf_op jit(solution)/shard_map/concatenate | solution.py:80
  6.5 9.6 %all-to-all-start = ((bf16[32,160,128]{2,1,0:T(8,128)(2,1)}), bf16[32,160,128]{2,1,0:T(8,128)(2,1)S(1)}, u32[]{:S(2)}, u32[]{:S(2)}) async-start(bf16[32,160,128]{2,1,0:T(8,128)(2,1)} %fusion.14), calls=%async_computation | async-start | bytes 2621440 | tf_op jit(solution)/shard_map/all_to_all | solution.py:81
  18.4 16.9 %all-to-all-done.got_ref = bf16[32,160,128]{2,1,0:T(8,128)(2,1)S(1)} async-done(((bf16[32,160,128]{2,1,0:T(8,128)(2,1)}), bf16[32,160,128]{2,1,0:T(8,128)(2,1)S(1)}, u32[]{:S(2)}, u32[]{:S(2)}) %all-to-all-start) | async-done | bytes 1310752 | tf_op jit(solution)/shard_map/all_to_all | solution.py:81
  35.4 8.3 %shard_map.146 = bf16[32,32,64]{2,1,0:T(8,128)(2,1)S(1)} custom-call(bf16[32,160,128]{2,1,0:T(8,128)(2,1)S(1)} %all-to-all-done.got_ref), custom_call_target="tpu_custom_call" | custom-call | flops 2147483648 | bytes 1441792 | tf_op jit(solution)/shard_map/pallas_call | solution.py:100
  44.5 5.0 %all-to-all-start.1 = ((bf16[32,2,1024]{2,1,0:T(2,128)(2,1)}), bf16[32,2,1024]{2,1,0:T(2,128)(2,1)S(1)}, u32[]{:S(2)}, u32[]{:S(2)}) async-start(bf16[32,2,1024]{2,1,0:T(2,128)(2,1)} %reshape.133), calls=%async_computation.1 | async-start | bytes 262144 | tf_op jit(solution)/shard_map/all_to_all | solution.py:113
  49.6 7.7 %all-to-all-done.1 = bf16[32,2,1024]{2,1,0:T(2,128)(2,1)S(1)} async-done(((bf16[32,2,1024]{2,1,0:T(2,128)(2,1)}), bf16[32,2,1024]{2,1,0:T(2,128)(2,1)S(1)}, u32[]{:S(2)}, u32[]{:S(2)}) %all-to-all-start.1) | async-done | bytes 131104 | tf_op jit(solution)/shard_map/all_to_all | solution.py:113
  60.1 36.2 %all_to_all.20 = bf16[128,6,1024]{2,1,0:T(8,128)(2,1)S(1)} all-to-all(bf16[128,6,1024]{2,1,0:T(8,128)(2,1)S(1)} %copy.51), channel_id=1, replica_groups=mesh['table'=4,'blk'=32] {'table','blk'}, dimensions={0} | all-to-all | bytes 3145728 | tf_op jit(solution)/shard_map/all_to_all | solution.py:26
  97.2 1.2 collective-permute-start
  98.4 1.0 fusion.18
  99.4 1.0 fusion.33
  100.4 1.0 collective-permute-done
  101.4 1.0 fusion.15
  102.4 1.0 fusion.29
  103.4 2.1 %multiply_convert_fusion.2 = (bf16[128,6,1024]{2,0,1:T(8,128)(2,1)S(1)}, bf16[128,6,1024]{2,0,1:T(8,128)(2,1)S(1)}, bf16[128,6,1024]{2,0,1:T(8,128)(2,1)S(1)}) fusion(f32[128,6,1024]{2,0,1:T(8,128)S(1)} %fusion.29, f32[128,6,1024]{2,0,1:T(8,128)S(1)} %fusion.15, bf16[1,512,1024]{2,1,0:T(8,128)(2,1)S(1)} %copy-done, ...), kind=kOutput, calls=%fused_computation.3 | convolution fusion | flops 817102848 | bytes 12845056 | tf_op jit(solution)/shard_map/scd,df->scf/dot_general | solution.py:46
  107.3 1.0 fusion.27
  108.3 1.0 add_convert_fusion.1
  110.2 2.1 %multiply_convert_fusion.5 = (bf16[128,6,1024]{2,0,1:T(8,128)(2,1)S(1)}, bf16[128,6,1024]{2,0,1:T(8,128)(2,1)S(1)}, bf16[128,6,1024]{2,0,1:T(8,128)(2,1)S(1)}) fusion(f32[128,6,1024]{2,0,1:T(8,128)S(1)} %fusion.33, f32[128,6,1024]{2,0,1:T(8,128)S(1)} %fusion.18, bf16[1,512,1024]{2,1,0:T(8,128)(2,1)S(1)} %copy-done, bf16[128,6,1024]{2,0,1:T(8,128)(2,1)S(1)} %copy.52), kind=kOutput, calls=%fused_computation.8 | convolution fusion | flops 817102848 | bytes 12845056 | tf_op jit(solution)/shard_map/scd,df->scf/dot_general | solution.py:46
  113.5 1.0 fusion.31
  114.5 2.3 %fusion.39 = f32[1024,512,1]{1,0,2:T(8,128)} fusion(bf16[128,6,1024]{2,0,1:T(8,128)(2,1)S(1)} %get-tuple-element.5, bf16[128,6,1024]{2,0,1:T(8,128)(2,1)S(1)} %copy.52), kind=kOutput, calls=%fused_computation.57 | convolution fusion | flops 805306368 | bytes 4456448 | tf_op jit(solution)/shard_map/scf,scd->fd/dot_general | solution.py:59
  116.9 1.0 add_convert_fusion.2
  118.5 2.2 %copy.55 = bf16[128,6,1024]{2,1,0:T(8,128)(2,1)} copy(bf16[128,6,1024]{2,0,1:T(8,128)(2,1)S(1)} %add_convert_fusion) | data formatting | bytes 3145728 | tf_op jit(solution)/shard_map/convert_element_type | solution.py:163
  120.7 5.0 %all-to-all-start.3 = ((bf16[128,6,1024]{2,1,0:T(8,128)(2,1)}), bf16[128,6,1024]{2,1,0:T(8,128)(2,1)}, u32[]{:S(2)}, u32[]{:S(2)}) async-start(bf16[128,6,1024]{2,1,0:T(8,128)(2,1)} %copy.55), calls=%async_computation.3 | async-start | bytes 4194304 | tf_op jit(solution)/shard_map/all_to_all | solution.py:30
  125.7 2.6 %fusion.48 = f32[512,1024,1]{1,0,2:T(8,128)S(1)} fusion(bf16[128,6,1024]{2,0,1:T(8,128)(2,1)} %copy-done.20, bf16[128,6,1024]{2,0,1:T(8,128)(2,1)S(1)} %copy.52), kind=kOutput, calls=%fused_computation.69 | convolution fusion | flops 805306368 | bytes 4456448 | tf_op jit(solution)/shard_map/scd,scf->df/dot_general | solution.py:61
  128.3 1.0 fusion.50
  130.3 2.0 %fusion.13 = bf16[1,1024,512]{2,1,0:T(8,128)(2,1)} fusion(bf16[128,6,1024]{2,0,1:T(8,128)(2,1)S(1)} %copy-done.17, f32[1024,512,1]{1,0,2:T(8,128)S(1)} %copy-done.11, bf16[128,6,1024]{2,0,1:T(8,128)(2,1)S(1)} %copy-done.4), kind=kOutput, calls=%fused_computation.30 | convolution fusion | flops 806354944 | bytes 5505024 | tf_op jit(solution)/shard_map/scf,scd->fd/dot_general | solution.py:59
  132.3 2.0 %fusion.12 = bf16[1,512,1024]{2,1,0:T(8,128)(2,1)} fusion(bf16[128,6,1024]{2,0,1:T(8,128)(2,1)S(1)} %copy-done.15, f32[512,1024,1]{1,0,2:T(8,128)S(1)} %fusion.48, bf16[128,6,1024]{2,0,1:T(8,128)(2,1)S(1)} %copy-done.4), kind=kOutput, calls=%fused_computation.29 | convolution fusion | flops 806354944 | bytes 5505024 | tf_op jit(solution)/shard_map/scd,scf->df/dot_general | solution.py:61
  134.3 2.0 %fusion.11 = bf16[1,512,1024]{2,1,0:T(8,128)(2,1)} fusion(bf16[128,6,1024]{2,0,1:T(8,128)(2,1)S(1)} %copy-done.13, f32[512,1024,1]{1,0,2:T(8,128)S(1)} %fusion.50, bf16[128,6,1024]{2,0,1:T(8,128)(2,1)S(1)} %copy-done.4), kind=kOutput, calls=%fused_computation.28 | convolution fusion | flops 806354944 | bytes 5505024 | tf_op jit(solution)/shard_map/scd,scf->df/dot_general | solution.py:60
  136.3 19.3 %all-to-all-done.3 = bf16[128,6,1024]{2,1,0:T(8,128)(2,1)} async-done(((bf16[128,6,1024]{2,1,0:T(8,128)(2,1)}), bf16[128,6,1024]{2,1,0:T(8,128)(2,1)}, u32[]{:S(2)}, u32[]{:S(2)}) %all-to-all-start.3) | async-done | bytes 1572896 | tf_op jit(solution)/shard_map/all_to_all | solution.py:30
  155.6 3.6 %fusion.8 = f32[256,1024]{1,0:T(8,128)S(1)} fusion(bf16[128,6,1024]{2,1,0:T(8,128)(2,1)} %all-to-all-done.3, s32[128,6]{0,1:T(8,128)S(1)} %multiply_add_fusion, s32[256]{0:T(256)S(1)} %multiply_add_fusion.1), kind=kOutput, calls=%fused_computation.27 | convolution fusion | flops 402849792 | bytes 2625536 | tf_op jit(solution)/shard_map/rjc,jcw->rw/dot_general | solution.py:166
  (90 shorter events, 15.9 us)
Async XLA Ops:
  0.6 102.8 %copy-start = (bf16[1,512,1024]{2,1,0:T(8,128)(2,1)S(1)}, bf16[1,512,1024]{2,1,0:T(8,128)(2,1)}, u32[]{:S(2)}) copy-start(bf16[1,512,1024]{2,1,0:T(8,128)(2,1)} %param.20) | copy-start | bytes 3145732
  6.5 9.6 %copy-start.9 = (s32[1,128,2]{1,2,0:T(2,128)S(1)}, s32[1,128,2]{1,2,0:T(2,128)}, u32[]{:S(2)}) copy-start(s32[1,128,2]{1,2,0:T(2,128)} %param.16) | copy-start | bytes 3076
  6.5 10.8 %copy-start.10 = (f32[1,128,2]{1,2,0:T(2,128)S(1)}, f32[1,128,2]{1,2,0:T(2,128)}, u32[]{:S(2)}) copy-start(f32[1,128,2]{1,2,0:T(2,128)} %param.17) | copy-start | bytes 3076
  6.5 11.1 %copy-start.6 = (bf16[1,128,512]{2,1,0:T(8,128)(2,1)S(1)}, bf16[1,128,512]{2,1,0:T(8,128)(2,1)}, u32[]{:S(2)}) copy-start(bf16[1,128,512]{2,1,0:T(8,128)(2,1)} %param.18) | copy-start | bytes 393220
  6.5 28.8 %all-to-all-start = ((bf16[32,160,128]{2,1,0:T(8,128)(2,1)}), bf16[32,160,128]{2,1,0:T(8,128)(2,1)S(1)}, u32[]{:S(2)}, u32[]{:S(2)}) async-start(bf16[32,160,128]{2,1,0:T(8,128)(2,1)} %fusion.14), calls=%async_computation | async-start | bytes 2621440 | tf_op jit(solution)/shard_map/all_to_all | solution.py:81
  43.6 14.2 %copy-start.5 = (bf16[512,512]{1,0:T(8,128)(2,1)S(1)}, bf16[512,512]{1,0:T(8,128)(2,1)}, u32[]{:S(2)}) copy-start(bf16[512,512]{1,0:T(8,128)(2,1)} %param.15) | copy-start | bytes 1572868
  43.7 14.2 %copy-start.8 = (bf16[1,128,512]{2,1,0:T(8,128)(2,1)S(1)}, bf16[1,128,512]{2,1,0:T(8,128)(2,1)}, u32[]{:S(2)}) copy-start(bf16[1,128,512]{2,1,0:T(8,128)(2,1)} %param.11) | copy-start | bytes 393220
  44.5 12.7 %all-to-all-start.1 = ((bf16[32,2,1024]{2,1,0:T(2,128)(2,1)}), bf16[32,2,1024]{2,1,0:T(2,128)(2,1)S(1)}, u32[]{:S(2)}, u32[]{:S(2)}) async-start(bf16[32,2,1024]{2,1,0:T(2,128)(2,1)} %reshape.133), calls=%async_computation.1 | async-start | bytes 262144 | tf_op jit(solution)/shard_map/all_to_all | solution.py:113
  96.3 2.1 %copy-start.1 = (bf16[1,1024,512]{2,1,0:T(8,128)(2,1)S(1)}, bf16[1,1024,512]{2,1,0:T(8,128)(2,1)}, u32[]{:S(2)}) copy-start(bf16[1,1024,512]{2,1,0:T(8,128)(2,1)} %param.21) | copy-start | bytes 3145732
  97.2 2.3 %copy-start.2 = (bf16[1,512,1024]{2,1,0:T(8,128)(2,1)S(1)}, bf16[1,512,1024]{2,1,0:T(8,128)(2,1)}, u32[]{:S(2)}) copy-start(bf16[1,512,1024]{2,1,0:T(8,128)(2,1)} %param.19) | copy-start | bytes 3145732
  97.2 4.3 %collective-permute-start = (bf16[128,6,1024]{2,0,1:T(8,128)(2,1)S(1)}, bf16[128,6,1024]{2,0,1:T(8,128)(2,1)S(1)}, u32[]{:S(2)}, u32[]{:S(2)}) collective-permute-start(bf16[128,6,1024]{2,0,1:T(8,128)(2,1)S(1)} %copy.52), channel_id=1, source_target_pairs={{0,1},{1,0},{2,3},{3,2},{4,5},{5,4},{6,7},{7,6},{8,9},{9,8},{10,11... | collective-permute-start | bytes 4718600 | tf_op jit(solution)/shard_map/ppermute | solution.py:40
  101.4 2.0 %copy-start.3 = (bf16[128,6,1024]{2,0,1:T(8,128)(2,1)}, bf16[128,6,1024]{2,0,1:T(8,128)(2,1)S(1)}, u32[]{:S(2)}) copy-start(bf16[128,6,1024]{2,0,1:T(8,128)(2,1)S(1)} %collective-permute-done) | copy-start | bytes 4718596
  105.6 1.2 copy-start.16
  105.6 1.7 %copy-start.12 = (bf16[128,6,1024]{2,0,1:T(8,128)(2,1)}, bf16[128,6,1024]{2,0,1:T(8,128)(2,1)S(1)}, u32[]{:S(2)}) copy-start(bf16[128,6,1024]{2,0,1:T(8,128)(2,1)S(1)} %get-tuple-element.9) | copy-start | bytes 4718596
  105.6 2.7 %copy-start.14 = (bf16[128,6,1024]{2,0,1:T(8,128)(2,1)}, bf16[128,6,1024]{2,0,1:T(8,128)(2,1)S(1)}, u32[]{:S(2)}) copy-start(bf16[128,6,1024]{2,0,1:T(8,128)(2,1)S(1)} %get-tuple-element.10) | copy-start | bytes 4718596
  109.5 8.3 %collective-permute-start.1 = (bf16[128,6,1024]{2,0,1:T(8,128)(2,1)S(1)}, bf16[128,6,1024]{2,0,1:T(8,128)(2,1)S(1)}, u32[]{:S(2)}, u32[]{:S(2)}) collective-permute-start(bf16[128,6,1024]{2,0,1:T(8,128)(2,1)S(1)} %pad_maximum_fusion), channel_id=1, source_target_pairs={{0,1},{1,0},{2,3},{3,2},{4,5},{5,4},{6,7},{7,6},{8,9},{9,8},{10,11... | collective-permute-start | bytes 4718600 | tf_op jit(solution)/shard_map/ppermute | solution.py:162
  112.3 1.2 copy-start.18
  112.3 4.5 %copy-start.20 = (bf16[128,6,1024]{2,0,1:T(8,128)(2,1)}, bf16[128,6,1024]{2,0,1:T(8,128)(2,1)S(1)}, u32[]{:S(2)}) copy-start(bf16[128,6,1024]{2,0,1:T(8,128)(2,1)S(1)} %get-tuple-element.7) | copy-start | bytes 4718596
  120.7 34.9 %all-to-all-start.3 = ((bf16[128,6,1024]{2,1,0:T(8,128)(2,1)}), bf16[128,6,1024]{2,1,0:T(8,128)(2,1)}, u32[]{:S(2)}, u32[]{:S(2)}) async-start(bf16[128,6,1024]{2,1,0:T(8,128)(2,1)} %copy.55), calls=%async_computation.3 | async-start | bytes 4194304 | tf_op jit(solution)/shard_map/all_to_all | solution.py:30
  125.6 2.6 %copy-start.19 = (bf16[128,6,1024]{2,0,1:T(8,128)(2,1)S(1)}, bf16[128,6,1024]{2,0,1:T(8,128)(2,1)}, u32[]{:S(2)}) copy-start(bf16[128,6,1024]{2,0,1:T(8,128)(2,1)} %copy-done.18) | copy-start | bytes 4718596
  125.7 3.7 %copy-start.17 = (bf16[128,6,1024]{2,0,1:T(8,128)(2,1)S(1)}, bf16[128,6,1024]{2,0,1:T(8,128)(2,1)}, u32[]{:S(2)}) copy-start(bf16[128,6,1024]{2,0,1:T(8,128)(2,1)} %copy-done.16) | copy-start | bytes 4718596
  128.2 1.4 copy-start.4
  128.2 2.1 %copy-start.11 = (f32[1024,512,1]{1,0,2:T(8,128)S(1)}, f32[1024,512,1]{1,0,2:T(8,128)}, u32[]{:S(2)}) copy-start(f32[1024,512,1]{1,0,2:T(8,128)} %fusion.39) | copy-start | bytes 6291460
  130.3 2.0 %copy-start.15 = (bf16[128,6,1024]{2,0,1:T(8,128)(2,1)S(1)}, bf16[128,6,1024]{2,0,1:T(8,128)(2,1)}, u32[]{:S(2)}) copy-start(bf16[128,6,1024]{2,0,1:T(8,128)(2,1)} %copy-done.14) | copy-start | bytes 4718596
  132.3 2.0 %copy-start.13 = (bf16[128,6,1024]{2,0,1:T(8,128)(2,1)S(1)}, bf16[128,6,1024]{2,0,1:T(8,128)(2,1)}, u32[]{:S(2)}) copy-start(bf16[128,6,1024]{2,0,1:T(8,128)(2,1)} %copy-done.12) | copy-start | bytes 4718596
  159.6 1.8 %copy-start.7 = (bf16[1,128,512]{2,1,0:T(8,128)(2,1)S(1)}, bf16[1,128,512]{2,1,0:T(8,128)(2,1)}, u32[]{:S(2)}) copy-start(bf16[1,128,512]{2,1,0:T(8,128)(2,1)} %param.18) | copy-start | bytes 393220

commit v4 on v3

--- a/solution.py
+++ b/solution.py
@@ -67,32 +67,42 @@
     devices = lax.psum(1, "blk")
     groups = devices // HEADS
     part = rows // groups
+    kept = rows // 2
     scale = 1.0 / math.sqrt(HEAD)
 
     def by_head(block):
-        heads = jnp.transpose(block.reshape(rows, HEADS, HEAD), (1, 0, 2))
-        return jnp.broadcast_to(heads[:, None], (HEADS, groups, rows, HEAD)).reshape(devices, rows, HEAD)
+        return jnp.transpose(block.reshape(rows, HEADS, HEAD), (1, 0, 2))
 
     pairs = jnp.concatenate([by_head(key_rows), by_head(value_rows)], axis=-1)
+    pairs = pairs.reshape(HEADS, 1, 2, kept, 2 * HEAD)
+    pairs = jnp.broadcast_to(pairs, (HEADS, groups // 2, 2, kept, 2 * HEAD))
+    pairs = pairs.reshape(devices, kept, 2 * HEAD)
     asked = jnp.transpose(query_rows.reshape(groups, part, HEADS, HEAD), (2, 0, 1, 3))
     asked = asked.reshape(devices, part, HEAD)
     asked = jnp.concatenate([asked, jnp.zeros_like(asked)], axis=-1)
     parcel = jnp.concatenate([pairs, asked], axis=1)
     got = lax.all_to_all(parcel, "blk", 0, 0, tiled=True)
+    other = lax.ppermute(got[:, :kept, :], "blk", partner_pairs())
     steps = 4
     chunk = devices // steps
 
-    def kernel(got_ref, out_ref):
+    def kernel(got_ref, other_ref, out_ref):
         step = pl.program_id(0)
-        pairs_all = got_ref[:, :rows, :].reshape(devices * rows, 2 * HEAD)
-        asked_now = got_ref[pl.ds(step * chunk, chunk), rows:, :].reshape(chunk * part, 2 * HEAD)
-        scores = lax.dot_general(
-            asked_now, pairs_all, (((1,), (1,)), ((), ())), preferred_element_type=jnp.float32
-        ) * scale
-        highest = jnp.max(scores, axis=-1, keepdims=True)
-        expo = jnp.exp(scores - highest)
-        denom = jnp.sum(expo, axis=-1, keepdims=True)
-        totals = jnp.dot(expo.astype(jnp.bfloat16), pairs_all, preferred_element_type=jnp.float32)
+        near = got_ref[:, :kept, :].reshape(devices * kept, 2 * HEAD)
+        far = other_ref[...].reshape(devices * kept, 2 * HEAD)
+        asked_now = got_ref[pl.ds(step * chunk, chunk), kept:, :].reshape(chunk * part, 2 * HEAD)
+        dims = (((1,), (1,)), ((), ()))
+        near_scores = lax.dot_general(asked_now, near, dims, preferred_element_type=jnp.float32) * scale
+        far_scores = lax.dot_general(asked_now, far, dims, preferred_element_type=jnp.float32) * scale
+        highest = jnp.maximum(
+            jnp.max(near_scores, axis=-1, keepdims=True), jnp.max(far_scores, axis=-1, keepdims=True)
+        )
+        near_expo = jnp.exp(near_scores - highest)
+        far_expo = jnp.exp(far_scores - highest)
+        denom = jnp.sum(near_expo, axis=-1, keepdims=True) + jnp.sum(far_expo, axis=-1, keepdims=True)
+        totals = jnp.dot(
+            near_expo.astype(jnp.bfloat16), near, preferred_element_type=jnp.float32
+        ) + jnp.dot(far_expo.astype(jnp.bfloat16), far, preferred_element_type=jnp.float32)
         out_ref[...] = (totals[:, HEAD:] / denom).astype(jnp.bfloat16).reshape(chunk, part, HEAD)
 
     queries_total = devices * part
@@ -100,16 +110,19 @@
     mixed = pl.pallas_call(
         kernel,
         grid=(steps,),
-        in_specs=[pl.BlockSpec(got.shape, lambda i: (0, 0, 0))],
+        in_specs=[
+            pl.BlockSpec(got.shape, lambda i: (0, 0, 0)),
+            pl.BlockSpec(other.shape, lambda i: (0, 0, 0)),
+        ],
         out_specs=pl.BlockSpec((chunk, part, HEAD), lambda i: (i, 0, 0)),
         out_shape=jax.ShapeDtypeStruct((devices, part, HEAD), jnp.bfloat16),
         compiler_params=pltpu.CompilerParams(vmem_limit_bytes=48 * 1024 * 1024),
         cost_estimate=pl.CostEstimate(
             flops=4 * queries_total * keys_total * 2 * HEAD,
             transcendentals=queries_total * keys_total,
-            bytes_accessed=got.size * 2 + queries_total * HEAD * 2,
+            bytes_accessed=(got.size + other.size) * 2 + queries_total * HEAD * 2,
         ),
-    )(got)
+    )(got, other)
     back = lax.all_to_all(mixed, "blk", 0, 0, tiled=True)
     back = jnp.transpose(back.reshape(HEADS, groups, part, HEAD), (1, 2, 0, 3))
     return back.reshape(rows, HEADS * HEAD)

time: 163 us -> 158 us (0.969)
  waiting for transfers between devices: 44.9 us -> 41.7 us
    all_to_all x1, waiting for transfers between devices: 16.9 us -> 12.7 us  [attend_heads(): got = lax.all_to_all(parcel, 'blk', 0, 0, tiled=True)]
    unnamed x48 -> x50, local copies, waits for them, and re-layouts: 5.35 us -> 5.36 us
  transfers between devices with their start and end apart: 5 -> 6, of which waited for: 4 -> 5; matrix products, arithmetic and copies ran while one was open for 13% -> 13% of each run, Pallas kernels for 0% -> 0%
where the time goes in v4:
time: 158 us; the launch traced here: 157 us
  waiting for transfers between devices  41.7 us (26%)
  blocking collectives  36.2 us (23%)
  matrix products  30.6 us (19%)
  starting transfers between devices  20.8 us (13%)
  local copies, waits for them, and re-layouts  13.1 us (8%)
  Pallas kernels  8.8 us (6%)
  other arithmetic  5.08 us (3%)
    all_to_all x1, blocking collectives, to_experts(): lax.all_to_all(buffer, ('table', 'blk'), split_axis=0, concat_axis=0, til...  36.2 us
    all_to_all x1, waiting for transfers between devices, to_anchor(): lax.all_to_all(buffer, ('table', 'blk'), split_axis=0, concat_axis=0, til...  19.3 us
    all_to_all x1, waiting for transfers between devices, attend_heads(): got = lax.all_to_all(parcel, 'blk', 0, 0, tiled=True)  12.7 us
    all_to_all x1, starting transfers between devices, attend_heads(): got = lax.all_to_all(parcel, 'blk', 0, 0, tiled=True)  9.55 us
    pallas_call x1, Pallas kernels, attend_heads(): pl.pallas_call(kernel, grid=(steps,), in_specs=[pl.BlockSpec(got.shape, l...  8.8 us
    all_to_all x1, waiting for transfers between devices, attend_heads(): back = lax.all_to_all(mixed, 'blk', 0, 0, tiled=True)  7.69 us
    unnamed x50, local copies, waits for them, and re-layouts  5.36 us
    all_to_all x1, starting transfers between devices, to_anchor(): lax.all_to_all(buffer, ('table', 'blk'), split_axis=0, concat_axis=0, til...  4.98 us
  transfers between devices with their start and end apart: 6, of which 5 were waited for; matrix products, arithmetic and copies ran while one was open for 13% of the time, Pallas kernels for 0%

profile of v4, /device:TPU:1, one launch (start us, length us, event | category | flops | bytes accessed | tf_op | source)
XLA Modules:
  0.0 157.5 jit_solution(5703614135422292401)
XLA Ops:
  0.7 1.1 copy.54
  1.8 1.0 copy.55
  4.4 9.6 %all-to-all-start = ((bf16[32,96,128]{2,1,0:T(8,128)(2,1)}), bf16[32,96,128]{2,1,0:T(8,128)(2,1)S(1)}, u32[]{:S(2)}, u32[]{:S(2)}) async-start(bf16[32,96,128]{2,1,0:T(8,128)(2,1)} %fusion.34), calls=%async_computation | async-start | bytes 1572864 | tf_op jit(solution)/shard_map/all_to_all | solution.py:84
  15.5 12.7 %all-to-all-done.got_ref = bf16[32,96,128]{2,1,0:T(8,128)(2,1)S(1)} async-done(((bf16[32,96,128]{2,1,0:T(8,128)(2,1)}), bf16[32,96,128]{2,1,0:T(8,128)(2,1)S(1)}, u32[]{:S(2)}, u32[]{:S(2)}) %all-to-all-start) | async-done | bytes 786464 | tf_op jit(solution)/shard_map/all_to_all | solution.py:84
  31.3 8.8 %shard_map.146 = bf16[32,32,64]{2,1,0:T(8,128)(2,1)S(1)} custom-call(bf16[32,96,128]{2,1,0:T(8,128)(2,1)S(1)} %all-to-all-done.got_ref, bf16[32,64,128]{2,1,0:T(8,128)(2,1)S(1)} %collective-permute-done.other_ref), custom_call_target="tpu_custom_call" | custom-call | flops 2147483648 | bytes 1441792 | tf_op jit(solution)/shard_map/pallas_call | solution.py:110
  41.0 3.9 %all-to-all-start.1 = ((bf16[32,2,1024]{2,1,0:T(2,128)(2,1)}), bf16[32,2,1024]{2,1,0:T(2,128)(2,1)S(1)}, u32[]{:S(2)}, u32[]{:S(2)}) async-start(bf16[32,2,1024]{2,1,0:T(2,128)(2,1)} %reshape.129), calls=%async_computation.1 | async-start | bytes 262144 | tf_op jit(solution)/shard_map/all_to_all | solution.py:126
  44.9 7.7 %all-to-all-done.1 = bf16[32,2,1024]{2,1,0:T(2,128)(2,1)S(1)} async-done(((bf16[32,2,1024]{2,1,0:T(2,128)(2,1)}), bf16[32,2,1024]{2,1,0:T(2,128)(2,1)S(1)}, u32[]{:S(2)}, u32[]{:S(2)}) %all-to-all-start.1) | async-done | bytes 131104 | tf_op jit(solution)/shard_map/all_to_all | solution.py:126
  55.5 36.2 %all_to_all.20 = bf16[128,6,1024]{2,1,0:T(8,128)(2,1)S(1)} all-to-all(bf16[128,6,1024]{2,1,0:T(8,128)(2,1)S(1)} %copy.63), channel_id=1, replica_groups=mesh['table'=4,'blk'=32] {'table','blk'}, dimensions={0} | all-to-all | bytes 3145728 | tf_op jit(solution)/shard_map/all_to_all | solution.py:26
  92.5 1.2 collective-permute-start.1
  93.7 1.0 fusion.17
  94.8 1.0 fusion.32
  95.8 1.0 collective-permute-done.1
  96.8 1.0 fusion.14
  97.8 1.0 fusion.28
  98.8 2.1 %multiply_convert_fusion.2 = (bf16[128,6,1024]{2,0,1:T(8,128)(2,1)S(1)}, bf16[128,6,1024]{2,0,1:T(8,128)(2,1)S(1)}, bf16[128,6,1024]{2,0,1:T(8,128)(2,1)S(1)}) fusion(f32[128,6,1024]{2,0,1:T(8,128)S(1)} %fusion.28, f32[128,6,1024]{2,0,1:T(8,128)S(1)} %fusion.14, bf16[1,512,1024]{2,1,0:T(8,128)(2,1)S(1)} %copy-done, ...), kind=kOutput, calls=%fused_computation.3 | convolution fusion | flops 817102848 | bytes 12845056 | tf_op jit(solution)/shard_map/scd,df->scf/dot_general | solution.py:46
  101.0 1.0 convolution_convert_fusion.1
  102.6 1.0 fusion.26
  103.6 1.0 add_convert_fusion.1
  105.5 2.1 %multiply_convert_fusion.5 = (bf16[128,6,1024]{2,0,1:T(8,128)(2,1)S(1)}, bf16[128,6,1024]{2,0,1:T(8,128)(2,1)S(1)}, bf16[128,6,1024]{2,0,1:T(8,128)(2,1)S(1)}) fusion(f32[128,6,1024]{2,0,1:T(8,128)S(1)} %fusion.32, f32[128,6,1024]{2,0,1:T(8,128)S(1)} %fusion.17, bf16[1,512,1024]{2,1,0:T(8,128)(2,1)S(1)} %copy-done, bf16[128,6,1024]{2,0,1:T(8,128)(2,1)S(1)} %copy.64), kind=kOutput, calls=%fused_computation.8 | convolution fusion | flops 817102848 | bytes 12845056 | tf_op jit(solution)/shard_map/scd,df->scf/dot_general | solution.py:46
  107.7 1.0 convolution_convert_fusion.2
  108.8 1.0 fusion.30
  109.8 2.3 %fusion.39 = f32[1024,512,1]{1,0,2:T(8,128)} fusion(bf16[128,6,1024]{2,0,1:T(8,128)(2,1)S(1)} %get-tuple-element.5, bf16[128,6,1024]{2,0,1:T(8,128)(2,1)S(1)} %copy.64), kind=kOutput, calls=%fused_computation.57 | convolution fusion | flops 805306368 | bytes 4456448 | tf_op jit(solution)/shard_map/scf,scd->fd/dot_general | solution.py:59
  112.2 1.0 add_convert_fusion.2
  113.8 2.2 %copy.67 = bf16[128,6,1024]{2,1,0:T(8,128)(2,1)} copy(bf16[128,6,1024]{2,0,1:T(8,128)(2,1)S(1)} %add_convert_fusion) | data formatting | bytes 3145728 | tf_op jit(solution)/shard_map/convert_element_type | solution.py:176
  116.0 5.0 %all-to-all-start.3 = ((bf16[128,6,1024]{2,1,0:T(8,128)(2,1)}), bf16[128,6,1024]{2,1,0:T(8,128)(2,1)}, u32[]{:S(2)}, u32[]{:S(2)}) async-start(bf16[128,6,1024]{2,1,0:T(8,128)(2,1)} %copy.67), calls=%async_computation.3 | async-start | bytes 4194304 | tf_op jit(solution)/shard_map/all_to_all | solution.py:30
  121.0 2.6 %fusion.48 = f32[512,1024,1]{1,0,2:T(8,128)S(1)} fusion(bf16[128,6,1024]{2,0,1:T(8,128)(2,1)} %copy-done.21, bf16[128,6,1024]{2,0,1:T(8,128)(2,1)S(1)} %copy.64), kind=kOutput, calls=%fused_computation.69 | convolution fusion | flops 805306368 | bytes 4456448 | tf_op jit(solution)/shard_map/scd,scf->df/dot_general | solution.py:61
  123.6 1.0 fusion.50
  125.6 2.0 %fusion.13 = bf16[1,1024,512]{2,1,0:T(8,128)(2,1)} fusion(bf16[128,6,1024]{2,0,1:T(8,128)(2,1)S(1)} %copy-done.18, f32[1024,512,1]{1,0,2:T(8,128)S(1)} %copy-done.12, bf16[128,6,1024]{2,0,1:T(8,128)(2,1)S(1)} %copy-done.4), kind=kOutput, calls=%fused_computation.30 | convolution fusion | flops 806354944 | bytes 5505024 | tf_op jit(solution)/shard_map/scf,scd->fd/dot_general | solution.py:59
  127.6 2.0 %fusion.12 = bf16[1,512,1024]{2,1,0:T(8,128)(2,1)} fusion(bf16[128,6,1024]{2,0,1:T(8,128)(2,1)S(1)} %copy-done.16, f32[512,1024,1]{1,0,2:T(8,128)S(1)} %fusion.48, bf16[128,6,1024]{2,0,1:T(8,128)(2,1)S(1)} %copy-done.4), kind=kOutput, calls=%fused_computation.29 | convolution fusion | flops 806354944 | bytes 5505024 | tf_op jit(solution)/shard_map/scd,scf->df/dot_general | solution.py:61
  129.6 2.0 %fusion.11 = bf16[1,512,1024]{2,1,0:T(8,128)(2,1)} fusion(bf16[128,6,1024]{2,0,1:T(8,128)(2,1)S(1)} %copy-done.14, f32[512,1024,1]{1,0,2:T(8,128)S(1)} %fusion.50, bf16[128,6,1024]{2,0,1:T(8,128)(2,1)S(1)} %copy-done.4), kind=kOutput, calls=%fused_computation.28 | convolution fusion | flops 806354944 | bytes 5505024 | tf_op jit(solution)/shard_map/scd,scf->df/dot_general | solution.py:60
  131.6 19.3 %all-to-all-done.3 = bf16[128,6,1024]{2,1,0:T(8,128)(2,1)} async-done(((bf16[128,6,1024]{2,1,0:T(8,128)(2,1)}), bf16[128,6,1024]{2,1,0:T(8,128)(2,1)}, u32[]{:S(2)}, u32[]{:S(2)}) %all-to-all-start.3) | async-done | bytes 1572896 | tf_op jit(solution)/shard_map/all_to_all | solution.py:30
  150.9 3.6 %fusion.8 = f32[256,1024]{1,0:T(8,128)S(1)} fusion(bf16[128,6,1024]{2,1,0:T(8,128)(2,1)} %all-to-all-done.3, s32[128,6]{0,1:T(8,128)S(1)} %multiply_add_fusion, s32[256]{0:T(256)S(1)} %multiply_add_fusion.1), kind=kOutput, calls=%fused_computation.27 | convolution fusion | flops 402849792 | bytes 2625536 | tf_op jit(solution)/shard_map/rjc,jcw->rw/dot_general | solution.py:179
  (94 shorter events, 16.9 us)
Async XLA Ops:
  0.6 98.2 %copy-start = (bf16[1,512,1024]{2,1,0:T(8,128)(2,1)S(1)}, bf16[1,512,1024]{2,1,0:T(8,128)(2,1)}, u32[]{:S(2)}) copy-start(bf16[1,512,1024]{2,1,0:T(8,128)(2,1)} %param.20) | copy-start | bytes 3145732
  0.6 2.4 %copy-start.8 = (bf16[1,128,512]{2,1,0:T(8,128)(2,1)S(1)}, bf16[1,128,512]{2,1,0:T(8,128)(2,1)}, u32[]{:S(2)}) copy-start(bf16[1,128,512]{2,1,0:T(8,128)(2,1)} %param.12) | copy-start | bytes 393220
  3.4 10.6 %copy-start.10 = (s32[1,128,2]{1,2,0:T(2,128)S(1)}, s32[1,128,2]{1,2,0:T(2,128)}, u32[]{:S(2)}) copy-start(s32[1,128,2]{1,2,0:T(2,128)} %param.16) | copy-start | bytes 3076
  3.4 11.8 %copy-start.11 = (f32[1,128,2]{1,2,0:T(2,128)S(1)}, f32[1,128,2]{1,2,0:T(2,128)}, u32[]{:S(2)}) copy-start(f32[1,128,2]{1,2,0:T(2,128)} %param.17) | copy-start | bytes 3076
  4.4 25.2 %copy-start.6 = (bf16[1,128,512]{2,1,0:T(8,128)(2,1)S(1)}, bf16[1,128,512]{2,1,0:T(8,128)(2,1)}, u32[]{:S(2)}) copy-start(bf16[1,128,512]{2,1,0:T(8,128)(2,1)} %param.18) | copy-start | bytes 393220
  4.4 23.8 %all-to-all-start = ((bf16[32,96,128]{2,1,0:T(8,128)(2,1)}), bf16[32,96,128]{2,1,0:T(8,128)(2,1)S(1)}, u32[]{:S(2)}, u32[]{:S(2)}) async-start(bf16[32,96,128]{2,1,0:T(8,128)(2,1)} %fusion.34), calls=%async_computation | async-start | bytes 1572864 | tf_op jit(solution)/shard_map/all_to_all | solution.py:84
  29.1 2.3 %collective-permute-start = (bf16[32,64,128]{2,1,0:T(8,128)(2,1)}, bf16[32,64,128]{2,1,0:T(8,128)(2,1)S(1)}, u32[]{:S(2)}, u32[]{:S(2)}) collective-permute-start(bf16[32,64,128]{2,1,0:T(8,128)(2,1)} %slice.36), channel_id=1, source_target_pairs={{0,1},{1,0},{2,3},{3,2},{4,5},{5,4},{6,7},{7,6},{8,9},{9,8},{10,11... | collective-permute-start | bytes 1572872 | tf_op jit(solution)/shard_map/ppermute | solution.py:85
  40.1 13.1 %copy-start.5 = (bf16[512,512]{1,0:T(8,128)(2,1)S(1)}, bf16[512,512]{1,0:T(8,128)(2,1)}, u32[]{:S(2)}) copy-start(bf16[512,512]{1,0:T(8,128)(2,1)} %param.15) | copy-start | bytes 1572868
  40.1 13.1 %copy-start.9 = (bf16[1,128,512]{2,1,0:T(8,128)(2,1)S(1)}, bf16[1,128,512]{2,1,0:T(8,128)(2,1)}, u32[]{:S(2)}) copy-start(bf16[1,128,512]{2,1,0:T(8,128)(2,1)} %param.11) | copy-start | bytes 393220
  41.0 11.6 %all-to-all-start.1 = ((bf16[32,2,1024]{2,1,0:T(2,128)(2,1)}), bf16[32,2,1024]{2,1,0:T(2,128)(2,1)S(1)}, u32[]{:S(2)}, u32[]{:S(2)}) async-start(bf16[32,2,1024]{2,1,0:T(2,128)(2,1)} %reshape.129), calls=%async_computation.1 | async-start | bytes 262144 | tf_op jit(solution)/shard_map/all_to_all | solution.py:126
  91.6 2.1 %copy-start.1 = (bf16[1,1024,512]{2,1,0:T(8,128)(2,1)S(1)}, bf16[1,1024,512]{2,1,0:T(8,128)(2,1)}, u32[]{:S(2)}) copy-start(bf16[1,1024,512]{2,1,0:T(8,128)(2,1)} %param.21) | copy-start | bytes 3145732
  92.5 2.3 %copy-start.2 = (bf16[1,512,1024]{2,1,0:T(8,128)(2,1)S(1)}, bf16[1,512,1024]{2,1,0:T(8,128)(2,1)}, u32[]{:S(2)}) copy-start(bf16[1,512,1024]{2,1,0:T(8,128)(2,1)} %param.19) | copy-start | bytes 3145732
  92.5 4.3 %collective-permute-start.1 = (bf16[128,6,1024]{2,0,1:T(8,128)(2,1)S(1)}, bf16[128,6,1024]{2,0,1:T(8,128)(2,1)S(1)}, u32[]{:S(2)}, u32[]{:S(2)}) collective-permute-start(bf16[128,6,1024]{2,0,1:T(8,128)(2,1)S(1)} %copy.64), channel_id=1, source_target_pairs={{0,1},{1,0},{2,3},{3,2},{4,5},{5,4},{6,7},{7,6},{8,9},{9,8},{10,11... | collective-permute-start | bytes 4718600 | tf_op jit(solution)/shard_map/ppermute | solution.py:40
  96.8 2.0 %copy-start.3 = (bf16[128,6,1024]{2,0,1:T(8,128)(2,1)}, bf16[128,6,1024]{2,0,1:T(8,128)(2,1)S(1)}, u32[]{:S(2)}) copy-start(bf16[128,6,1024]{2,0,1:T(8,128)(2,1)S(1)} %collective-permute-done.1) | copy-start | bytes 4718596
  100.9 1.2 copy-start.17
  101.0 1.6 %copy-start.13 = (bf16[128,6,1024]{2,0,1:T(8,128)(2,1)}, bf16[128,6,1024]{2,0,1:T(8,128)(2,1)S(1)}, u32[]{:S(2)}) copy-start(bf16[128,6,1024]{2,0,1:T(8,128)(2,1)S(1)} %get-tuple-element.9) | copy-start | bytes 4718596
  101.0 2.7 %copy-start.15 = (bf16[128,6,1024]{2,0,1:T(8,128)(2,1)}, bf16[128,6,1024]{2,0,1:T(8,128)(2,1)S(1)}, u32[]{:S(2)}) copy-start(bf16[128,6,1024]{2,0,1:T(8,128)(2,1)S(1)} %get-tuple-element.10) | copy-start | bytes 4718596
  104.9 8.3 %collective-permute-start.2 = (bf16[128,6,1024]{2,0,1:T(8,128)(2,1)S(1)}, bf16[128,6,1024]{2,0,1:T(8,128)(2,1)S(1)}, u32[]{:S(2)}, u32[]{:S(2)}) collective-permute-start(bf16[128,6,1024]{2,0,1:T(8,128)(2,1)S(1)} %pad_maximum_fusion), channel_id=1, source_target_pairs={{0,1},{1,0},{2,3},{3,2},{4,5},{5,4},{6,7},{7,6},{8,9},{9,8},{10,11... | collective-permute-start | bytes 4718600 | tf_op jit(solution)/shard_map/ppermute | solution.py:175
  107.7 1.2 copy-start.19
  107.7 4.5 %copy-start.21 = (bf16[128,6,1024]{2,0,1:T(8,128)(2,1)}, bf16[128,6,1024]{2,0,1:T(8,128)(2,1)S(1)}, u32[]{:S(2)}) copy-start(bf16[128,6,1024]{2,0,1:T(8,128)(2,1)S(1)} %get-tuple-element.7) | copy-start | bytes 4718596
  116.0 34.9 %all-to-all-start.3 = ((bf16[128,6,1024]{2,1,0:T(8,128)(2,1)}), bf16[128,6,1024]{2,1,0:T(8,128)(2,1)}, u32[]{:S(2)}, u32[]{:S(2)}) async-start(bf16[128,6,1024]{2,1,0:T(8,128)(2,1)} %copy.67), calls=%async_computation.3 | async-start | bytes 4194304 | tf_op jit(solution)/shard_map/all_to_all | solution.py:30
  121.0 2.6 %copy-start.20 = (bf16[128,6,1024]{2,0,1:T(8,128)(2,1)S(1)}, bf16[128,6,1024]{2,0,1:T(8,128)(2,1)}, u32[]{:S(2)}) copy-start(bf16[128,6,1024]{2,0,1:T(8,128)(2,1)} %copy-done.19) | copy-start | bytes 4718596
  121.0 3.7 %copy-start.18 = (bf16[128,6,1024]{2,0,1:T(8,128)(2,1)S(1)}, bf16[128,6,1024]{2,0,1:T(8,128)(2,1)}, u32[]{:S(2)}) copy-start(bf16[128,6,1024]{2,0,1:T(8,128)(2,1)} %copy-done.17) | copy-start | bytes 4718596
  123.6 1.4 copy-start.4
  123.6 2.1 %copy-start.12 = (f32[1024,512,1]{1,0,2:T(8,128)S(1)}, f32[1024,512,1]{1,0,2:T(8,128)}, u32[]{:S(2)}) copy-start(f32[1024,512,1]{1,0,2:T(8,128)} %fusion.39) | copy-start | bytes 6291460
  125.6 2.0 %copy-start.16 = (bf16[128,6,1024]{2,0,1:T(8,128)(2,1)S(1)}, bf16[128,6,1024]{2,0,1:T(8,128)(2,1)}, u32[]{:S(2)}) copy-start(bf16[128,6,1024]{2,0,1:T(8,128)(2,1)} %copy-done.15) | copy-start | bytes 4718596
  127.6 2.0 %copy-start.14 = (bf16[128,6,1024]{2,0,1:T(8,128)(2,1)S(1)}, bf16[128,6,1024]{2,0,1:T(8,128)(2,1)}, u32[]{:S(2)}) copy-start(bf16[128,6,1024]{2,0,1:T(8,128)(2,1)} %copy-done.13) | copy-start | bytes 4718596
  154.9 1.8 %copy-start.7 = (bf16[1,128,512]{2,1,0:T(8,128)(2,1)S(1)}, bf16[1,128,512]{2,1,0:T(8,128)(2,1)}, u32[]{:S(2)}) copy-start(bf16[1,128,512]{2,1,0:T(8,128)(2,1)} %param.18) | copy-start | bytes 393220

commit v5 on v4

--- a/solution.py
+++ b/solution.py
@@ -167,11 +167,10 @@
         "jcr,rw->jcw", placing, route_rows, preferred_element_type=jnp.float32
     ).astype(jnp.bfloat16)
     both_own, both_other = spread(in_slots)
-    in_own, cot_own = both_own[..., :D], both_own[..., D:]
-    in_other, cot_other = both_other[..., :D], both_other[..., D:]
+    both = jnp.concatenate([both_own, both_other], axis=0)
     mats = (w_gate[0], w_up[0], w_down[0])
-    own, gate_a, up_a, down_a = piece_pass(in_own, cot_own, *mats)
-    other, gate_b, up_b, down_b = piece_pass(in_other, cot_other, *mats)
+    done, gate_sum, up_sum, down_sum = piece_pass(both[..., :D], both[..., D:], *mats)
+    own, other = done[: both_own.shape[0]], done[both_own.shape[0] :]
     theirs = lax.ppermute(other, "blk", partner_pairs())
     summed = (own.astype(jnp.float32) + theirs.astype(jnp.float32)).astype(jnp.bfloat16)
     back = to_anchor(summed)
@@ -179,9 +178,9 @@
     picked = jnp.einsum("rjc,jcw->rw", picking, back, preferred_element_type=jnp.float32)
     route_out = picked[:, :D]
     route_grad = picked[:, D:]
-    grad_gate = (gate_a + gate_b).astype(jnp.bfloat16)[None]
-    grad_up = (up_a + up_b).astype(jnp.bfloat16)[None]
-    grad_down = (down_a + down_b).astype(jnp.bfloat16)[None]
+    grad_gate = gate_sum.astype(jnp.bfloat16)[None]
+    grad_up = up_sum.astype(jnp.bfloat16)[None]
+    grad_down = down_sum.astype(jnp.bfloat16)[None]
     moe = jnp.sum((gates[:, None] * route_out).reshape(row_count, TOP, D), axis=1)
     block_out = (stream + moe).astype(jnp.bfloat16)[None]
     grad_unit = jnp.sum(route_grad.reshape(row_count, TOP, D), axis=1)

time: 158 us -> 163 us (1.032)
  waiting for transfers between devices: 41.7 us -> 47.1 us
  matrix products: 30.6 us -> 32.5 us
    dot_general x2 -> x1, matrix products: 1.94 us -> 5.96 us  [piece_pass(): jnp.einsum('scf,fd->scd', hidden, down_mat, preferred_element_type=jnp.fl...]
    ppermute x1, waiting for transfers between devices: 0.01 us -> 3.04 us  [block(): theirs = lax.ppermute(other, 'blk', partner_pairs())]
    ppermute x1, waiting for transfers between devices: 1.02 us -> 3.04 us  [spread(): other = lax.ppermute(got, 'blk', partner_pairs())]
    dot_general x2 -> x1, matrix products: 4.54 us -> 2.79 us  [piece_pass(): jnp.einsum('scd,scf->df', inputs, grad_pre_up, preferred_element_type=jnp...]
    dot_general x2 -> x1, matrix products: 4.31 us -> 5.3 us  [piece_pass(): jnp.einsum('scf,scd->fd', hidden, cots, preferred_element_type=jnp.float32)]
    dot_general x2 -> x1, matrix products: 4.24 us -> 5.19 us  [piece_pass(): jnp.einsum('scd,df->scf', inputs, up_mat, preferred_element_type=jnp.floa...]
    unnamed x50 -> x37, local copies, waits for them, and re-layouts: 5.36 us -> 4.58 us
  transfers between devices with their start and end apart: 6 -> 6, of which waited for: 5 -> 6; matrix products, arithmetic and copies ran while one was open for 13% -> 8% of each run, Pallas kernels for 0% -> 0%
where the time goes in v5:
time: 163 us
  waiting for transfers between devices  47.1 us (29%)
  blocking collectives  36.2 us (22%)
  matrix products  32.5 us (20%)
  starting transfers between devices  19.3 us (12%)
  local copies, waits for them, and re-layouts  12.5 us (8%)
  Pallas kernels  8.79 us (5%)
  other arithmetic  5.09 us (3%)
    all_to_all x1, blocking collectives, to_experts(): lax.all_to_all(buffer, ('table', 'blk'), split_axis=0, concat_axis=0, til...  36.2 us
    all_to_all x1, waiting for transfers between devices, to_anchor(): lax.all_to_all(buffer, ('table', 'blk'), split_axis=0, concat_axis=0, til...  19.7 us
    all_to_all x1, waiting for transfers between devices, attend_heads(): got = lax.all_to_all(parcel, 'blk', 0, 0, tiled=True)  12.7 us
    all_to_all x1, starting transfers between devices, attend_heads(): got = lax.all_to_all(parcel, 'blk', 0, 0, tiled=True)  9.42 us
    pallas_call x1, Pallas kernels, attend_heads(): pl.pallas_call(kernel, grid=(steps,), in_specs=[pl.BlockSpec(got.shape, l...  8.79 us
    all_to_all x1, waiting for transfers between devices, attend_heads(): back = lax.all_to_all(mixed, 'blk', 0, 0, tiled=True)  7.69 us
    dot_general x1, matrix products, piece_pass(): jnp.einsum('scf,fd->scd', hidden, down_mat, preferred_element_type=jnp.fl...  5.96 us
    dot_general x1, matrix products, piece_pass(): jnp.einsum('scf,scd->fd', hidden, cots, preferred_element_type=jnp.float32)  5.3 us
  transfers between devices with their start and end apart: 6, of which 6 were waited for; matrix products, arithmetic and copies ran while one was open for 8% of the time, Pallas kernels for 0%

profile of v5, /device:TPU:1, one launch (start us, length us, event | category | flops | bytes accessed | tf_op | source)
XLA Modules:
  0.0 162.5 jit_solution(3927630434846851792)
XLA Ops:
  0.6 1.1 copy.45
  1.8 1.0 copy.46
  3.0 1.1 reshape_squeeze.14
  4.3 1.0 fusion.29
  5.3 9.4 %all-to-all-start = ((bf16[32,96,128]{2,1,0:T(8,128)(2,1)}), bf16[32,96,128]{2,1,0:T(8,128)(2,1)S(1)}, u32[]{:S(2)}, u32[]{:S(2)}) async-start(bf16[32,96,128]{2,1,0:T(8,128)(2,1)} %fusion.29), calls=%async_computation | async-start | bytes 1572864 | tf_op jit(solution)/shard_map/all_to_all | solution.py:84
  16.2 12.7 %all-to-all-done.got_ref = bf16[32,96,128]{2,1,0:T(8,128)(2,1)S(1)} async-done(((bf16[32,96,128]{2,1,0:T(8,128)(2,1)}), bf16[32,96,128]{2,1,0:T(8,128)(2,1)S(1)}, u32[]{:S(2)}, u32[]{:S(2)}) %all-to-all-start) | async-done | bytes 786464 | tf_op jit(solution)/shard_map/all_to_all | solution.py:84
  29.0 0.9 slice.36
  31.2 0.9 collective-permute-done.other_ref
  32.1 8.8 %shard_map.146 = bf16[32,32,64]{2,1,0:T(8,128)(2,1)S(1)} custom-call(bf16[32,96,128]{2,1,0:T(8,128)(2,1)S(1)} %all-to-all-done.got_ref, bf16[32,64,128]{2,1,0:T(8,128)(2,1)S(1)} %collective-permute-done.other_ref), custom_call_target="tpu_custom_call" | custom-call | flops 2147483648 | bytes 1441792 | tf_op jit(solution)/shard_map/pallas_call | solution.py:110
  40.9 0.8 reshape.126
  41.7 3.9 %all-to-all-start.1 = ((bf16[32,2,1024]{2,1,0:T(2,128)(2,1)}), bf16[32,2,1024]{2,1,0:T(2,128)(2,1)S(1)}, u32[]{:S(2)}, u32[]{:S(2)}) async-start(bf16[32,2,1024]{2,1,0:T(2,128)(2,1)} %reshape.126), calls=%async_computation.1 | async-start | bytes 262144 | tf_op jit(solution)/shard_map/all_to_all | solution.py:126
  45.7 7.7 %all-to-all-done.1 = bf16[32,2,1024]{2,1,0:T(2,128)(2,1)S(1)} async-done(((bf16[32,2,1024]{2,1,0:T(2,128)(2,1)}), bf16[32,2,1024]{2,1,0:T(2,128)(2,1)S(1)}, u32[]{:S(2)}, u32[]{:S(2)}) %all-to-all-start.1) | async-done | bytes 131104 | tf_op jit(solution)/shard_map/all_to_all | solution.py:126
  55.3 0.9 copy.54
  56.2 36.2 %all_to_all.20 = bf16[128,6,1024]{2,1,0:T(8,128)(2,1)S(1)} all-to-all(bf16[128,6,1024]{2,1,0:T(8,128)(2,1)S(1)} %copy.54), channel_id=1, replica_groups=mesh['table'=4,'blk'=32] {'table','blk'}, dimensions={0} | all-to-all | bytes 3145728 | tf_op jit(solution)/shard_map/all_to_all | solution.py:26
  92.4 0.9 constant_dynamic-update-slice_fusion.1
  93.3 1.2 collective-permute-start.1
  94.5 3.0 %collective-permute-done.1 = bf16[128,6,1024]{2,0,1:T(8,128)(2,1)S(1)} collective-permute-done((bf16[128,6,1024]{2,0,1:T(8,128)(2,1)S(1)}, bf16[128,6,1024]{2,0,1:T(8,128)(2,1)S(1)}, u32[]{:S(2)}, u32[]{:S(2)}) %collective-permute-start.1) | collective-permute-done | bytes 1572896 | tf_op jit(solution)/shard_map/ppermute | solution.py:40
  97.7 1.8 %fusion.6 = f32[256,6,1024]{2,0,1:T(8,128)S(1)} fusion(bf16[256,6,1024]{2,0,1:T(8,128)(2,1)S(1)} %constant_dynamic-update-slice_fusion, bf16[1,1024,512]{2,1,0:T(8,128)(2,1)S(1)} %copy-done.9), kind=kOutput, calls=%fused_computation.21 | convolution fusion | flops 1610612736 | bytes 8912896 | tf_op jit(solution)/shard_map/scd,fd->scf/dot_general | solution.py:52
  99.7 1.8 %fusion.23 = f32[256,6,1024]{2,0,1:T(8,128)S(1)} fusion(bf16[1,512,1024]{2,1,0:T(8,128)(2,1)S(1)} %copy-done.10, bf16[256,6,1024]{2,0,1:T(8,128)(2,1)S(1)} %constant_dynamic-update-slice_fusion), kind=kOutput, calls=%fused_computation.35 | convolution fusion | flops 1610612736 | bytes 8912896 | tf_op jit(solution)/shard_map/scd,df->scf/dot_general | solution.py:45
  101.6 5.2 %multiply_convert_fusion.2 = (bf16[256,6,1024]{2,0,1:T(8,128)(2,1)}, bf16[256,6,1024]{2,0,1:T(8,128)(2,1)S(1)}, bf16[256,6,1024]{2,0,1:T(8,128)(2,1)S(1)}) fusion(f32[256,6,1024]{2,0,1:T(8,128)S(1)} %fusion.23, f32[256,6,1024]{2,0,1:T(8,128)S(1)} %fusion.6, bf16[1,512,1024]{2,1,0:T(8,128)(2,1)S(1)} %copy-done, ...), kind=kOutput, calls=%fused_computation.2 | convolution fusion | flops 1634205696 | bytes 24641536 | tf_op jit(solution)/shard_map/scd,df->scf/dot_general | solution.py:46
  106.8 6.0 %convolution_convert_fusion = bf16[256,6,512]{2,0,1:T(8,128)(2,1)S(1)} fusion(bf16[256,6,1024]{2,0,1:T(8,128)(2,1)} %get-tuple-element.7, bf16[1,1024,512]{2,1,0:T(8,128)(2,1)S(1)} %copy-done.9), kind=kOutput, calls=%fused_computation.12 | convolution fusion | flops 1611399168 | bytes 5767168 | tf_op jit(solution)/shard_map/scf,fd->scd/dot_general | solution.py:49
  112.7 1.9 %fusion.21 = f32[256,6,512]{2,0,1:T(8,128)S(1)} fusion(bf16[256,6,1024]{2,0,1:T(8,128)(2,1)S(1)} %get-tuple-element.8, bf16[1,512,1024]{2,1,0:T(8,128)(2,1)S(1)} %copy-done.10), kind=kOutput, calls=%fused_computation.33 | convolution fusion | flops 1610612736 | bytes 7340032 | tf_op jit(solution)/shard_map/scf,df->scd/dot_general | solution.py:56
  114.6 2.0 %add_convert_fusion.1 = bf16[256,6,512]{2,0,1:T(8,128)(2,1)S(1)} fusion(f32[256,6,512]{2,0,1:T(8,128)S(1)} %fusion.21, bf16[256,6,1024]{2,0,1:T(8,128)(2,1)S(1)} %get-tuple-element.9, bf16[1,512,1024]{2,1,0:T(8,128)(2,1)S(1)} %copy-done), kind=kOutput, calls=%fused_computation.8 | convolution fusion | flops 1612185600 | bytes 8912896 | tf_op jit(solution)/shard_map/scf,df->scd/dot_general | solution.py:57
  117.3 3.0 %collective-permute-done.2 = bf16[128,6,1024]{2,0,1:T(8,128)(2,1)S(1)} collective-permute-done((bf16[128,6,1024]{2,0,1:T(8,128)(2,1)S(1)}, bf16[128,6,1024]{2,0,1:T(8,128)(2,1)S(1)}, u32[]{:S(2)}, u32[]{:S(2)}) %collective-permute-start.2) | collective-permute-done | bytes 1572896 | tf_op jit(solution)/shard_map/ppermute | solution.py:174
  120.9 2.2 %copy.57 = bf16[128,6,1024]{2,1,0:T(8,128)(2,1)} copy(bf16[128,6,1024]{2,0,1:T(8,128)(2,1)S(1)} %add_convert_fusion) | data formatting | bytes 3145728 | tf_op jit(solution)/shard_map/convert_element_type | solution.py:175
  123.1 3.8 %all-to-all-start.3 = ((bf16[128,6,1024]{2,1,0:T(8,128)(2,1)}), bf16[128,6,1024]{2,1,0:T(8,128)(2,1)S(1)}, u32[]{:S(2)}, u32[]{:S(2)}) async-start(bf16[128,6,1024]{2,1,0:T(8,128)(2,1)} %copy.57), calls=%async_computation.3 | async-start | bytes 4194304 | tf_op jit(solution)/shard_map/all_to_all | solution.py:30
  127.0 5.3 %fusion.13 = bf16[1,1024,512]{2,1,0:T(8,128)(2,1)} fusion(bf16[256,6,1024]{2,0,1:T(8,128)(2,1)} %get-tuple-element.7, bf16[256,6,1024]{2,0,1:T(8,128)(2,1)} %copy-done.1), kind=kOutput, calls=%fused_computation.26 | convolution fusion | flops 1611137024 | bytes 5767168 | tf_op jit(solution)/shard_map/scf,scd->fd/dot_general | solution.py:59
  132.3 2.8 %fusion.11 = bf16[1,512,1024]{2,1,0:T(8,128)(2,1)} fusion(bf16[256,6,1024]{2,0,1:T(8,128)(2,1)S(1)} %copy-done.14, bf16[256,6,1024]{2,0,1:T(8,128)(2,1)S(1)} %copy-done.2), kind=kOutput, calls=%fused_computation.24 | convolution fusion | flops 1611137024 | bytes 5767168 | tf_op jit(solution)/shard_map/scd,scf->df/dot_general | solution.py:60
  135.1 2.8 %fusion.12 = bf16[1,512,1024]{2,1,0:T(8,128)(2,1)} fusion(bf16[256,6,1024]{2,0,1:T(8,128)(2,1)S(1)} %copy-done.12, bf16[256,6,1024]{2,0,1:T(8,128)(2,1)S(1)} %copy-done.2), kind=kOutput, calls=%fused_computation.25 | convolution fusion | flops 1611137024 | bytes 5767168 | tf_op jit(solution)/shard_map/scd,scf->df/dot_general | solution.py:61
  137.9 19.7 %all-to-all-done.3 = bf16[128,6,1024]{2,1,0:T(8,128)(2,1)S(1)} async-done(((bf16[128,6,1024]{2,1,0:T(8,128)(2,1)}), bf16[128,6,1024]{2,1,0:T(8,128)(2,1)S(1)}, u32[]{:S(2)}, u32[]{:S(2)}) %all-to-all-start.3) | async-done | bytes 1572896 | tf_op jit(solution)/shard_map/all_to_all | solution.py:30
  157.5 2.0 %fusion.8 = f32[256,1024]{1,0:T(8,128)S(1)} fusion(bf16[128,6,1024]{2,1,0:T(8,128)(2,1)S(1)} %all-to-all-done.3, s32[128,6]{0,1:T(8,128)S(1)} %multiply_add_fusion, s32[256]{0:T(256)S(1)} %multiply_add_fusion.1), kind=kOutput, calls=%fused_computation.23 | convolution fusion | flops 402849792 | bytes 2625536 | tf_op jit(solution)/shard_map/rjc,jcw->rw/dot_general | solution.py:178
  161.7 0.8 fusion.39
  (72 shorter events, 8.8 us)
Async XLA Ops:
  0.6 100.9 %copy-start = (bf16[1,512,1024]{2,1,0:T(8,128)(2,1)S(1)}, bf16[1,512,1024]{2,1,0:T(8,128)(2,1)}, u32[]{:S(2)}) copy-start(bf16[1,512,1024]{2,1,0:T(8,128)(2,1)} %param.20) | copy-start | bytes 3145732
  1.8 13.0 %copy-start.7 = (s32[1,128,2]{1,2,0:T(2,128)S(1)}, s32[1,128,2]{1,2,0:T(2,128)}, u32[]{:S(2)}) copy-start(s32[1,128,2]{1,2,0:T(2,128)} %param.16) | copy-start | bytes 3076
  2.8 13.2 %copy-start.8 = (f32[1,128,2]{1,2,0:T(2,128)S(1)}, f32[1,128,2]{1,2,0:T(2,128)}, u32[]{:S(2)}) copy-start(f32[1,128,2]{1,2,0:T(2,128)} %param.17) | copy-start | bytes 3076
  4.1 26.2 %copy-start.4 = (bf16[1,128,512]{2,1,0:T(8,128)(2,1)S(1)}, bf16[1,128,512]{2,1,0:T(8,128)(2,1)}, u32[]{:S(2)}) copy-start(bf16[1,128,512]{2,1,0:T(8,128)(2,1)} %param.18) | copy-start | bytes 393220
  5.3 23.7 %all-to-all-start = ((bf16[32,96,128]{2,1,0:T(8,128)(2,1)}), bf16[32,96,128]{2,1,0:T(8,128)(2,1)S(1)}, u32[]{:S(2)}, u32[]{:S(2)}) async-start(bf16[32,96,128]{2,1,0:T(8,128)(2,1)} %fusion.29), calls=%async_computation | async-start | bytes 1572864 | tf_op jit(solution)/shard_map/all_to_all | solution.py:84
  29.8 2.3 %collective-permute-start = (bf16[32,64,128]{2,1,0:T(8,128)(2,1)}, bf16[32,64,128]{2,1,0:T(8,128)(2,1)S(1)}, u32[]{:S(2)}, u32[]{:S(2)}) collective-permute-start(bf16[32,64,128]{2,1,0:T(8,128)(2,1)} %slice.36), channel_id=1, source_target_pairs={{0,1},{1,0},{2,3},{3,2},{4,5},{5,4},{6,7},{7,6},{8,9},{9,8},{10,11... | collective-permute-start | bytes 1572872 | tf_op jit(solution)/shard_map/ppermute | solution.py:85
  31.1 22.8 %copy-start.3 = (bf16[512,512]{1,0:T(8,128)(2,1)S(1)}, bf16[512,512]{1,0:T(8,128)(2,1)}, u32[]{:S(2)}) copy-start(bf16[512,512]{1,0:T(8,128)(2,1)} %param.15) | copy-start | bytes 1572868
  31.2 22.8 %copy-start.6 = (bf16[1,128,512]{2,1,0:T(8,128)(2,1)S(1)}, bf16[1,128,512]{2,1,0:T(8,128)(2,1)}, u32[]{:S(2)}) copy-start(bf16[1,128,512]{2,1,0:T(8,128)(2,1)} %param.11) | copy-start | bytes 393220
  41.7 11.6 %all-to-all-start.1 = ((bf16[32,2,1024]{2,1,0:T(2,128)(2,1)}), bf16[32,2,1024]{2,1,0:T(2,128)(2,1)S(1)}, u32[]{:S(2)}, u32[]{:S(2)}) async-start(bf16[32,2,1024]{2,1,0:T(2,128)(2,1)} %reshape.126), calls=%async_computation.1 | async-start | bytes 262144 | tf_op jit(solution)/shard_map/all_to_all | solution.py:126
  92.4 5.3 %copy-start.9 = (bf16[1,1024,512]{2,1,0:T(8,128)(2,1)S(1)}, bf16[1,1024,512]{2,1,0:T(8,128)(2,1)}, u32[]{:S(2)}) copy-start(bf16[1,1024,512]{2,1,0:T(8,128)(2,1)} %param.21) | copy-start | bytes 3145732
  93.3 4.3 %collective-permute-start.1 = (bf16[128,6,1024]{2,0,1:T(8,128)(2,1)S(1)}, bf16[128,6,1024]{2,0,1:T(8,128)(2,1)S(1)}, u32[]{:S(2)}, u32[]{:S(2)}) collective-permute-start(bf16[128,6,1024]{2,0,1:T(8,128)(2,1)S(1)} %get-tuple-element.6), channel_id=1, source_target_pairs={{0,1},{1,0},{2,3},{3,2},{4,5},{5,4},{6,7},{7,6},{8,9},{9,8},{10,11... | collective-permute-start | bytes 4718600 | tf_op jit(solution)/shard_map/ppermute | solution.py:40
  97.7 3.8 %copy-start.1 = (bf16[256,6,1024]{2,0,1:T(8,128)(2,1)}, bf16[256,6,1024]{2,0,1:T(8,128)(2,1)S(1)}, u32[]{:S(2)}) copy-start(bf16[256,6,1024]{2,0,1:T(8,128)(2,1)S(1)} %constant_dynamic-update-slice_fusion) | copy-start | bytes 9437188
  97.7 2.0 %copy-start.10 = (bf16[1,512,1024]{2,1,0:T(8,128)(2,1)S(1)}, bf16[1,512,1024]{2,1,0:T(8,128)(2,1)}, u32[]{:S(2)}) copy-start(bf16[1,512,1024]{2,1,0:T(8,128)(2,1)} %param.19) | copy-start | bytes 3145732
  106.7 6.0 %copy-start.13 = (bf16[256,6,1024]{2,0,1:T(8,128)(2,1)}, bf16[256,6,1024]{2,0,1:T(8,128)(2,1)S(1)}, u32[]{:S(2)}) copy-start(bf16[256,6,1024]{2,0,1:T(8,128)(2,1)S(1)} %get-tuple-element.8) | copy-start | bytes 9437188
  106.7 7.9 %copy-start.11 = (bf16[256,6,1024]{2,0,1:T(8,128)(2,1)}, bf16[256,6,1024]{2,0,1:T(8,128)(2,1)S(1)}, u32[]{:S(2)}) copy-start(bf16[256,6,1024]{2,0,1:T(8,128)(2,1)S(1)} %get-tuple-element.9) | copy-start | bytes 9437188
  116.8 3.5 %collective-permute-start.2 = (bf16[128,6,1024]{2,0,1:T(8,128)(2,1)S(1)}, bf16[128,6,1024]{2,0,1:T(8,128)(2,1)S(1)}, u32[]{:S(2)}, u32[]{:S(2)}) collective-permute-start(bf16[128,6,1024]{2,0,1:T(8,128)(2,1)S(1)} %pad_maximum_fusion), channel_id=1, source_target_pairs={{0,1},{1,0},{2,3},{3,2},{4,5},{5,4},{6,7},{7,6},{8,9},{9,8},{10,11... | collective-permute-start | bytes 4718600 | tf_op jit(solution)/shard_map/ppermute | solution.py:174
  123.1 34.4 %all-to-all-start.3 = ((bf16[128,6,1024]{2,1,0:T(8,128)(2,1)}), bf16[128,6,1024]{2,1,0:T(8,128)(2,1)S(1)}, u32[]{:S(2)}, u32[]{:S(2)}) async-start(bf16[128,6,1024]{2,1,0:T(8,128)(2,1)} %copy.57), calls=%async_computation.3 | async-start | bytes 4194304 | tf_op jit(solution)/shard_map/all_to_all | solution.py:30
  127.0 5.3 %copy-start.2 = (bf16[256,6,1024]{2,0,1:T(8,128)(2,1)S(1)}, bf16[256,6,1024]{2,0,1:T(8,128)(2,1)}, u32[]{:S(2)}) copy-start(bf16[256,6,1024]{2,0,1:T(8,128)(2,1)} %copy-done.1) | copy-start | bytes 9437188
  127.0 5.3 %copy-start.14 = (bf16[256,6,1024]{2,0,1:T(8,128)(2,1)S(1)}, bf16[256,6,1024]{2,0,1:T(8,128)(2,1)}, u32[]{:S(2)}) copy-start(bf16[256,6,1024]{2,0,1:T(8,128)(2,1)} %copy-done.13) | copy-start | bytes 9437188
  132.3 2.8 %copy-start.12 = (bf16[256,6,1024]{2,0,1:T(8,128)(2,1)S(1)}, bf16[256,6,1024]{2,0,1:T(8,128)(2,1)}, u32[]{:S(2)}) copy-start(bf16[256,6,1024]{2,0,1:T(8,128)(2,1)} %copy-done.11) | copy-start | bytes 9437188
  159.5 2.2 %copy-start.5 = (bf16[1,128,512]{2,1,0:T(8,128)(2,1)S(1)}, bf16[1,128,512]{2,1,0:T(8,128)(2,1)}, u32[]{:S(2)}) copy-start(bf16[1,128,512]{2,1,0:T(8,128)(2,1)} %param.18) | copy-start | bytes 393220

commit v6 on v4

--- a/solution.py
+++ b/solution.py
@@ -175,8 +175,10 @@
     theirs = lax.ppermute(other, "blk", partner_pairs())
     summed = (own.astype(jnp.float32) + theirs.astype(jnp.float32)).astype(jnp.bfloat16)
     back = to_anchor(summed)
-    picking = (slot_index[:, None, None] == slot_ids[None, :, :]).astype(jnp.bfloat16)
-    picked = jnp.einsum("rjc,jcw->rw", picking, back, preferred_element_type=jnp.float32)
+    picking = (slot_index[:, None] == slot_ids.reshape(1, -1)).astype(jnp.bfloat16)
+    picked = jnp.dot(
+        picking, back.reshape(EXPERTS * CAP, 2 * D), preferred_element_type=jnp.float32
+    )
     route_out = picked[:, :D]
     route_grad = picked[:, D:]
     grad_gate = (gate_a + gate_b).astype(jnp.bfloat16)[None]

time: 158 us -> 157 us (level)
  local copies, waits for them, and re-layouts: 13.1 us -> 14.7 us
    unnamed x50 -> x54, local copies, waits for them, and re-layouts: 5.36 us -> 5.51 us
  transfers between devices with their start and end apart: 6 -> 6, of which waited for: 5 -> 5; matrix products, arithmetic and copies ran while one was open for 13% -> 14% of each run, Pallas kernels for 0% -> 0%
where the time goes in v6:
time: 157 us
  waiting for transfers between devices  41.8 us (27%)
  blocking collectives  36.2 us (23%)
  matrix products  29.3 us (19%)
  starting transfers between devices  19.7 us (13%)
  local copies, waits for them, and re-layouts  14.7 us (9%)
  Pallas kernels  8.8 us (6%)
  other arithmetic  5.08 us (3%)
    all_to_all x1, blocking collectives, to_experts(): lax.all_to_all(buffer, ('table', 'blk'), split_axis=0, concat_axis=0, til...  36.2 us
    all_to_all x1, waiting for transfers between devices, to_anchor(): lax.all_to_all(buffer, ('table', 'blk'), split_axis=0, concat_axis=0, til...  19.4 us
    all_to_all x1, waiting for transfers between devices, attend_heads(): got = lax.all_to_all(parcel, 'blk', 0, 0, tiled=True)  12.7 us
    all_to_all x1, starting transfers between devices, attend_heads(): got = lax.all_to_all(parcel, 'blk', 0, 0, tiled=True)  9.55 us
    pallas_call x1, Pallas kernels, attend_heads(): pl.pallas_call(kernel, grid=(steps,), in_specs=[pl.BlockSpec(got.shape, l...  8.8 us
    all_to_all x1, waiting for transfers between devices, attend_heads(): back = lax.all_to_all(mixed, 'blk', 0, 0, tiled=True)  7.69 us
    unnamed x54, local copies, waits for them, and re-layouts  5.51 us
    dot_general x2, matrix products, piece_pass(): jnp.einsum('scd,scf->df', inputs, grad_pre_up, preferred_element_type=jnp...  4.77 us
  transfers between devices with their start and end apart: 6, of which 5 were waited for; matrix products, arithmetic and copies ran while one was open for 14% of the time, Pallas kernels for 0%

profile of v6, /device:TPU:1, one launch (start us, length us, event | category | flops | bytes accessed | tf_op | source)
XLA Modules:
  0.0 156.8 jit_solution(5601609287033229291)
XLA Ops:
  0.7 1.1 copy.56
  1.8 1.0 copy.57
  4.4 9.6 %all-to-all-start = ((bf16[32,96,128]{2,1,0:T(8,128)(2,1)}), bf16[32,96,128]{2,1,0:T(8,128)(2,1)S(1)}, u32[]{:S(2)}, u32[]{:S(2)}) async-start(bf16[32,96,128]{2,1,0:T(8,128)(2,1)} %fusion.29), calls=%async_computation | async-start | bytes 1572864 | tf_op jit(solution)/shard_map/all_to_all | solution.py:84
  15.5 12.7 %all-to-all-done.got_ref = bf16[32,96,128]{2,1,0:T(8,128)(2,1)S(1)} async-done(((bf16[32,96,128]{2,1,0:T(8,128)(2,1)}), bf16[32,96,128]{2,1,0:T(8,128)(2,1)S(1)}, u32[]{:S(2)}, u32[]{:S(2)}) %all-to-all-start) | async-done | bytes 786464 | tf_op jit(solution)/shard_map/all_to_all | solution.py:84
  31.3 8.8 %shard_map.146 = bf16[32,32,64]{2,1,0:T(8,128)(2,1)S(1)} custom-call(bf16[32,96,128]{2,1,0:T(8,128)(2,1)S(1)} %all-to-all-done.got_ref, bf16[32,64,128]{2,1,0:T(8,128)(2,1)S(1)} %collective-permute-done.other_ref), custom_call_target="tpu_custom_call" | custom-call | flops 2147483648 | bytes 1441792 | tf_op jit(solution)/shard_map/pallas_call | solution.py:110
  41.0 3.9 %all-to-all-start.1 = ((bf16[32,2,1024]{2,1,0:T(2,128)(2,1)}), bf16[32,2,1024]{2,1,0:T(2,128)(2,1)S(1)}, u32[]{:S(2)}, u32[]{:S(2)}) async-start(bf16[32,2,1024]{2,1,0:T(2,128)(2,1)} %reshape.122), calls=%async_computation.1 | async-start | bytes 262144 | tf_op jit(solution)/shard_map/all_to_all | solution.py:126
  44.9 7.7 %all-to-all-done.1 = bf16[32,2,1024]{2,1,0:T(2,128)(2,1)S(1)} async-done(((bf16[32,2,1024]{2,1,0:T(2,128)(2,1)}), bf16[32,2,1024]{2,1,0:T(2,128)(2,1)S(1)}, u32[]{:S(2)}, u32[]{:S(2)}) %all-to-all-start.1) | async-done | bytes 131104 | tf_op jit(solution)/shard_map/all_to_all | solution.py:126
  55.5 36.2 %all_to_all.20 = bf16[128,6,1024]{2,1,0:T(8,128)(2,1)S(1)} all-to-all(bf16[128,6,1024]{2,1,0:T(8,128)(2,1)S(1)} %copy.65), channel_id=1, replica_groups=mesh['table'=4,'blk'=32] {'table','blk'}, dimensions={0} | all-to-all | bytes 3145728 | tf_op jit(solution)/shard_map/all_to_all | solution.py:26
  92.5 1.2 collective-permute-start.1
  93.8 1.0 fusion.12
  94.8 1.0 fusion.27
  95.8 1.0 collective-permute-done.1
  96.8 1.0 fusion.9
  97.8 1.0 fusion.23
  98.8 2.1 %multiply_convert_fusion.2 = (bf16[128,6,1024]{2,0,1:T(8,128)(2,1)S(1)}, bf16[128,6,1024]{2,0,1:T(8,128)(2,1)S(1)}, bf16[128,6,1024]{2,0,1:T(8,128)(2,1)S(1)}) fusion(f32[128,6,1024]{2,0,1:T(8,128)S(1)} %fusion.23, f32[128,6,1024]{2,0,1:T(8,128)S(1)} %fusion.9, bf16[1,512,1024]{2,1,0:T(8,128)(2,1)S(1)} %copy-done, ...), kind=kOutput, calls=%fused_computation.3 | convolution fusion | flops 817102848 | bytes 12845056 | tf_op jit(solution)/shard_map/scd,df->scf/dot_general | solution.py:46
  102.6 1.0 fusion.21
  103.7 1.0 add_convert_fusion.1
  105.6 2.1 %multiply_convert_fusion.5 = (bf16[128,6,1024]{2,0,1:T(8,128)(2,1)S(1)}, bf16[128,6,1024]{2,0,1:T(8,128)(2,1)S(1)}, bf16[128,6,1024]{2,0,1:T(8,128)(2,1)S(1)}) fusion(f32[128,6,1024]{2,0,1:T(8,128)S(1)} %fusion.27, f32[128,6,1024]{2,0,1:T(8,128)S(1)} %fusion.12, bf16[1,512,1024]{2,1,0:T(8,128)(2,1)S(1)} %copy-done, bf16[128,6,1024]{2,0,1:T(8,128)(2,1)S(1)} %copy.66), kind=kOutput, calls=%fused_computation.8 | convolution fusion | flops 817102848 | bytes 12845056 | tf_op jit(solution)/shard_map/scd,df->scf/dot_general | solution.py:46
  107.7 1.0 convolution_convert_fusion.2
  108.9 1.0 fusion.25
  110.0 2.3 %fusion.34 = f32[1024,512,1]{1,0,2:T(8,128)} fusion(bf16[128,6,1024]{2,0,1:T(8,128)(2,1)S(1)} %get-tuple-element.5, bf16[128,6,1024]{2,0,1:T(8,128)(2,1)S(1)} %copy.66), kind=kOutput, calls=%fused_computation.55 | convolution fusion | flops 805306368 | bytes 4456448 | tf_op jit(solution)/shard_map/scf,scd->fd/dot_general | solution.py:59
  112.3 1.0 add_convert_fusion.2
  113.9 2.2 %copy.69 = bf16[128,6,1024]{2,1,0:T(8,128)(2,1)} copy(bf16[128,6,1024]{2,0,1:T(8,128)(2,1)S(1)} %add_convert_fusion) | data formatting | bytes 3145728 | tf_op jit(solution)/shard_map/convert_element_type | solution.py:176
  116.1 3.8 %all-to-all-start.3 = ((bf16[128,6,1024]{2,1,0:T(8,128)(2,1)}), bf16[128,6,1024]{2,1,0:T(8,128)(2,1)S(1)}, u32[]{:S(2)}, u32[]{:S(2)}) async-start(bf16[128,6,1024]{2,1,0:T(8,128)(2,1)} %copy.69), calls=%async_computation.3 | async-start | bytes 4194304 | tf_op jit(solution)/shard_map/all_to_all | solution.py:30
  120.0 2.8 %fusion.43 = f32[512,1024,1]{1,0,2:T(8,128)S(1)} fusion(bf16[128,6,1024]{2,0,1:T(8,128)(2,1)} %copy-done.23, bf16[128,6,1024]{2,0,1:T(8,128)(2,1)} %copy-done.1), kind=kOutput, calls=%fused_computation.67 | convolution fusion | flops 805306368 | bytes 4456448 | tf_op jit(solution)/shard_map/scd,scf->df/dot_general | solution.py:61
  122.8 1.0 fusion.45
  124.9 2.0 %fusion.8 = bf16[1,1024,512]{2,1,0:T(8,128)(2,1)} fusion(bf16[128,6,1024]{2,0,1:T(8,128)(2,1)S(1)} %copy-done.20, f32[1024,512,1]{1,0,2:T(8,128)S(1)} %copy-done.14, bf16[128,6,1024]{2,0,1:T(8,128)(2,1)S(1)} %copy-done.6), kind=kOutput, calls=%fused_computation.27 | convolution fusion | flops 806354944 | bytes 5505024 | tf_op jit(solution)/shard_map/scf,scd->fd/dot_general | solution.py:59
  126.9 2.0 %fusion.7 = bf16[1,512,1024]{2,1,0:T(8,128)(2,1)} fusion(bf16[128,6,1024]{2,0,1:T(8,128)(2,1)S(1)} %copy-done.18, f32[512,1024,1]{1,0,2:T(8,128)S(1)} %fusion.43, bf16[128,6,1024]{2,0,1:T(8,128)(2,1)S(1)} %copy-done.6), kind=kOutput, calls=%fused_computation.26 | convolution fusion | flops 806354944 | bytes 5505024 | tf_op jit(solution)/shard_map/scd,scf->df/dot_general | solution.py:61
  128.9 2.0 %fusion.6 = bf16[1,512,1024]{2,1,0:T(8,128)(2,1)} fusion(bf16[128,6,1024]{2,0,1:T(8,128)(2,1)S(1)} %copy-done.16, f32[512,1024,1]{1,0,2:T(8,128)S(1)} %fusion.45, bf16[128,6,1024]{2,0,1:T(8,128)(2,1)S(1)} %copy-done.6), kind=kOutput, calls=%fused_computation.25 | convolution fusion | flops 806354944 | bytes 5505024 | tf_op jit(solution)/shard_map/scd,scf->df/dot_general | solution.py:60
  130.9 19.4 %all-to-all-done.3 = bf16[128,6,1024]{2,1,0:T(8,128)(2,1)S(1)} async-done(((bf16[128,6,1024]{2,1,0:T(8,128)(2,1)}), bf16[128,6,1024]{2,1,0:T(8,128)(2,1)S(1)}, u32[]{:S(2)}, u32[]{:S(2)}) %all-to-all-start.3) | async-done | bytes 1572896 | tf_op jit(solution)/shard_map/all_to_all | solution.py:30
  150.3 1.5 reshape.106
  151.8 2.0 %fusion.30 = f32[256,1024]{1,0:T(8,128)S(1)} fusion(bf16[768,1024]{1,0:T(8,128)(2,1)} %reshape.106, s32[256]{0:T(256)S(1)} %multiply_add_fusion.1), kind=kOutput, calls=%fused_computation.51 | convolution fusion | flops 402849792 | bytes 2622464 | tf_op jit(solution)/shard_map/dot_general | solution.py:179
  (99 shorter events, 18.0 us)
Async XLA Ops:
  0.6 98.2 %copy-start = (bf16[1,512,1024]{2,1,0:T(8,128)(2,1)S(1)}, bf16[1,512,1024]{2,1,0:T(8,128)(2,1)}, u32[]{:S(2)}) copy-start(bf16[1,512,1024]{2,1,0:T(8,128)(2,1)} %param.20) | copy-start | bytes 3145732
  0.6 2.4 %copy-start.10 = (bf16[1,128,512]{2,1,0:T(8,128)(2,1)S(1)}, bf16[1,128,512]{2,1,0:T(8,128)(2,1)}, u32[]{:S(2)}) copy-start(bf16[1,128,512]{2,1,0:T(8,128)(2,1)} %param.12) | copy-start | bytes 393220
  3.4 10.6 %copy-start.12 = (s32[1,128,2]{1,2,0:T(2,128)S(1)}, s32[1,128,2]{1,2,0:T(2,128)}, u32[]{:S(2)}) copy-start(s32[1,128,2]{1,2,0:T(2,128)} %param.16) | copy-start | bytes 3076
  3.4 11.8 %copy-start.13 = (f32[1,128,2]{1,2,0:T(2,128)S(1)}, f32[1,128,2]{1,2,0:T(2,128)}, u32[]{:S(2)}) copy-start(f32[1,128,2]{1,2,0:T(2,128)} %param.17) | copy-start | bytes 3076
  4.4 25.2 %copy-start.8 = (bf16[1,128,512]{2,1,0:T(8,128)(2,1)S(1)}, bf16[1,128,512]{2,1,0:T(8,128)(2,1)}, u32[]{:S(2)}) copy-start(bf16[1,128,512]{2,1,0:T(8,128)(2,1)} %param.18) | copy-start | bytes 393220
  4.4 23.8 %all-to-all-start = ((bf16[32,96,128]{2,1,0:T(8,128)(2,1)}), bf16[32,96,128]{2,1,0:T(8,128)(2,1)S(1)}, u32[]{:S(2)}, u32[]{:S(2)}) async-start(bf16[32,96,128]{2,1,0:T(8,128)(2,1)} %fusion.29), calls=%async_computation | async-start | bytes 1572864 | tf_op jit(solution)/shard_map/all_to_all | solution.py:84
  29.1 2.3 %collective-permute-start = (bf16[32,64,128]{2,1,0:T(8,128)(2,1)}, bf16[32,64,128]{2,1,0:T(8,128)(2,1)S(1)}, u32[]{:S(2)}, u32[]{:S(2)}) collective-permute-start(bf16[32,64,128]{2,1,0:T(8,128)(2,1)} %slice.36), channel_id=1, source_target_pairs={{0,1},{1,0},{2,3},{3,2},{4,5},{5,4},{6,7},{7,6},{8,9},{9,8},{10,11... | collective-permute-start | bytes 1572872 | tf_op jit(solution)/shard_map/ppermute | solution.py:85
  40.1 13.1 %copy-start.7 = (bf16[512,512]{1,0:T(8,128)(2,1)S(1)}, bf16[512,512]{1,0:T(8,128)(2,1)}, u32[]{:S(2)}) copy-start(bf16[512,512]{1,0:T(8,128)(2,1)} %param.15) | copy-start | bytes 1572868
  40.1 13.1 %copy-start.11 = (bf16[1,128,512]{2,1,0:T(8,128)(2,1)S(1)}, bf16[1,128,512]{2,1,0:T(8,128)(2,1)}, u32[]{:S(2)}) copy-start(bf16[1,128,512]{2,1,0:T(8,128)(2,1)} %param.11) | copy-start | bytes 393220
  41.0 11.6 %all-to-all-start.1 = ((bf16[32,2,1024]{2,1,0:T(2,128)(2,1)}), bf16[32,2,1024]{2,1,0:T(2,128)(2,1)S(1)}, u32[]{:S(2)}, u32[]{:S(2)}) async-start(bf16[32,2,1024]{2,1,0:T(2,128)(2,1)} %reshape.122), calls=%async_computation.1 | async-start | bytes 262144 | tf_op jit(solution)/shard_map/all_to_all | solution.py:126
  91.6 2.1 %copy-start.3 = (bf16[1,1024,512]{2,1,0:T(8,128)(2,1)S(1)}, bf16[1,1024,512]{2,1,0:T(8,128)(2,1)}, u32[]{:S(2)}) copy-start(bf16[1,1024,512]{2,1,0:T(8,128)(2,1)} %param.21) | copy-start | bytes 3145732
  92.5 17.4 %copy-start.1 = (bf16[128,6,1024]{2,0,1:T(8,128)(2,1)}, bf16[128,6,1024]{2,0,1:T(8,128)(2,1)S(1)}, u32[]{:S(2)}) copy-start(bf16[128,6,1024]{2,0,1:T(8,128)(2,1)S(1)} %copy.66) | copy-start | bytes 4718596
  92.5 2.3 %copy-start.4 = (bf16[1,512,1024]{2,1,0:T(8,128)(2,1)S(1)}, bf16[1,512,1024]{2,1,0:T(8,128)(2,1)}, u32[]{:S(2)}) copy-start(bf16[1,512,1024]{2,1,0:T(8,128)(2,1)} %param.19) | copy-start | bytes 3145732
  92.5 4.3 %collective-permute-start.1 = (bf16[128,6,1024]{2,0,1:T(8,128)(2,1)S(1)}, bf16[128,6,1024]{2,0,1:T(8,128)(2,1)S(1)}, u32[]{:S(2)}, u32[]{:S(2)}) collective-permute-start(bf16[128,6,1024]{2,0,1:T(8,128)(2,1)S(1)} %copy.66), channel_id=1, source_target_pairs={{0,1},{1,0},{2,3},{3,2},{4,5},{5,4},{6,7},{7,6},{8,9},{9,8},{10,11... | collective-permute-start | bytes 4718600 | tf_op jit(solution)/shard_map/ppermute | solution.py:40
  96.8 2.0 %copy-start.5 = (bf16[128,6,1024]{2,0,1:T(8,128)(2,1)}, bf16[128,6,1024]{2,0,1:T(8,128)(2,1)S(1)}, u32[]{:S(2)}) copy-start(bf16[128,6,1024]{2,0,1:T(8,128)(2,1)S(1)} %collective-permute-done.1) | copy-start | bytes 4718596
  101.0 1.2 copy-start.19
  101.0 1.7 %copy-start.15 = (bf16[128,6,1024]{2,0,1:T(8,128)(2,1)}, bf16[128,6,1024]{2,0,1:T(8,128)(2,1)S(1)}, u32[]{:S(2)}) copy-start(bf16[128,6,1024]{2,0,1:T(8,128)(2,1)S(1)} %get-tuple-element.9) | copy-start | bytes 4718596
  101.0 2.7 %copy-start.17 = (bf16[128,6,1024]{2,0,1:T(8,128)(2,1)}, bf16[128,6,1024]{2,0,1:T(8,128)(2,1)S(1)}, u32[]{:S(2)}) copy-start(bf16[128,6,1024]{2,0,1:T(8,128)(2,1)S(1)} %get-tuple-element.10) | copy-start | bytes 4718596
  104.9 8.4 %collective-permute-start.2 = (bf16[128,6,1024]{2,0,1:T(8,128)(2,1)S(1)}, bf16[128,6,1024]{2,0,1:T(8,128)(2,1)S(1)}, u32[]{:S(2)}, u32[]{:S(2)}) collective-permute-start(bf16[128,6,1024]{2,0,1:T(8,128)(2,1)S(1)} %pad_maximum_fusion), channel_id=1, source_target_pairs={{0,1},{1,0},{2,3},{3,2},{4,5},{5,4},{6,7},{7,6},{8,9},{9,8},{10,11... | collective-permute-start | bytes 4718600 | tf_op jit(solution)/shard_map/ppermute | solution.py:175
  107.7 1.2 copy-start.21
  107.7 4.6 %copy-start.23 = (bf16[128,6,1024]{2,0,1:T(8,128)(2,1)}, bf16[128,6,1024]{2,0,1:T(8,128)(2,1)S(1)}, u32[]{:S(2)}) copy-start(bf16[128,6,1024]{2,0,1:T(8,128)(2,1)S(1)} %get-tuple-element.7) | copy-start | bytes 4718596
  116.1 34.2 %all-to-all-start.3 = ((bf16[128,6,1024]{2,1,0:T(8,128)(2,1)}), bf16[128,6,1024]{2,1,0:T(8,128)(2,1)S(1)}, u32[]{:S(2)}, u32[]{:S(2)}) async-start(bf16[128,6,1024]{2,1,0:T(8,128)(2,1)} %copy.69), calls=%async_computation.3 | async-start | bytes 4194304 | tf_op jit(solution)/shard_map/all_to_all | solution.py:30
  120.0 2.8 %copy-start.2 = (bf16[128,6,1024]{2,0,1:T(8,128)(2,1)S(1)}, bf16[128,6,1024]{2,0,1:T(8,128)(2,1)}, u32[]{:S(2)}) copy-start(bf16[128,6,1024]{2,0,1:T(8,128)(2,1)} %copy-done.1) | copy-start | bytes 4718596
  120.0 2.8 %copy-start.22 = (bf16[128,6,1024]{2,0,1:T(8,128)(2,1)S(1)}, bf16[128,6,1024]{2,0,1:T(8,128)(2,1)}, u32[]{:S(2)}) copy-start(bf16[128,6,1024]{2,0,1:T(8,128)(2,1)} %copy-done.21) | copy-start | bytes 4718596
  120.0 3.9 %copy-start.20 = (bf16[128,6,1024]{2,0,1:T(8,128)(2,1)S(1)}, bf16[128,6,1024]{2,0,1:T(8,128)(2,1)}, u32[]{:S(2)}) copy-start(bf16[128,6,1024]{2,0,1:T(8,128)(2,1)} %copy-done.19) | copy-start | bytes 4718596
  122.8 1.5 copy-start.6
  122.8 2.1 %copy-start.14 = (f32[1024,512,1]{1,0,2:T(8,128)S(1)}, f32[1024,512,1]{1,0,2:T(8,128)}, u32[]{:S(2)}) copy-start(f32[1024,512,1]{1,0,2:T(8,128)} %fusion.34) | copy-start | bytes 6291460
  124.9 2.0 %copy-start.18 = (bf16[128,6,1024]{2,0,1:T(8,128)(2,1)S(1)}, bf16[128,6,1024]{2,0,1:T(8,128)(2,1)}, u32[]{:S(2)}) copy-start(bf16[128,6,1024]{2,0,1:T(8,128)(2,1)} %copy-done.17) | copy-start | bytes 4718596
  126.9 2.0 %copy-start.16 = (bf16[128,6,1024]{2,0,1:T(8,128)(2,1)S(1)}, bf16[128,6,1024]{2,0,1:T(8,128)(2,1)}, u32[]{:S(2)}) copy-start(bf16[128,6,1024]{2,0,1:T(8,128)(2,1)} %copy-done.15) | copy-start | bytes 4718596
  154.2 1.8 %copy-start.9 = (bf16[1,128,512]{2,1,0:T(8,128)(2,1)S(1)}, bf16[1,128,512]{2,1,0:T(8,128)(2,1)}, u32[]{:S(2)}) copy-start(bf16[1,128,512]{2,1,0:T(8,128)(2,1)} %param.18) | copy-start | bytes 393220

commit v7 on v6

--- a/solution.py
+++ b/solution.py
@@ -70,26 +70,41 @@
     kept = rows // 2
     scale = 1.0 / math.sqrt(HEAD)
 
-    def by_head(block):
-        return jnp.transpose(block.reshape(rows, HEADS, HEAD), (1, 0, 2))
-
-    pairs = jnp.concatenate([by_head(key_rows), by_head(value_rows)], axis=-1)
-    pairs = pairs.reshape(HEADS, 1, 2, kept, 2 * HEAD)
-    pairs = jnp.broadcast_to(pairs, (HEADS, groups // 2, 2, kept, 2 * HEAD))
-    pairs = pairs.reshape(devices, kept, 2 * HEAD)
-    asked = jnp.transpose(query_rows.reshape(groups, part, HEADS, HEAD), (2, 0, 1, 3))
-    asked = asked.reshape(devices, part, HEAD)
-    asked = jnp.concatenate([asked, jnp.zeros_like(asked)], axis=-1)
-    parcel = jnp.concatenate([pairs, asked], axis=1)
+    def pack(key_ref, value_ref, query_ref, parcel_ref):
+        lane = lax.broadcasted_iota(jnp.int32, (rows, 2 * HEAD), 1)
+        low = lane < HEAD
+        for head in range(HEADS):
+            cols = pl.ds((head // 2) * 2 * HEAD, 2 * HEAD)
+            key_tile = key_ref[:, cols].astype(jnp.float32)
+            value_tile = value_ref[:, cols].astype(jnp.float32)
+            query_tile = query_ref[:, cols].astype(jnp.float32)
+            if head % 2 == 0:
+                both = jnp.where(low, key_tile, pltpu.roll(value_tile, HEAD, 1))
+                ask = jnp.where(low, query_tile, 0.0)
+            else:
+                both = jnp.where(low, pltpu.roll(key_tile, HEAD, 1), value_tile)
+                ask = jnp.where(low, pltpu.roll(query_tile, HEAD, 1), 0.0)
+            both = both.astype(jnp.bfloat16)
+            ask = ask.astype(jnp.bfloat16)
+            for group in range(groups):
+                dest = head * groups + group
+                side = group % 2
+                parcel_ref[dest, :kept, :] = both[side * kept : (side + 1) * kept]
+                parcel_ref[dest, kept:, :] = ask[group * part : (group + 1) * part]
+
+    parcel = pl.pallas_call(
+        pack,
+        out_shape=jax.ShapeDtypeStruct((devices, kept + part, 2 * HEAD), jnp.bfloat16),
+    )(key_rows, value_rows, query_rows)
     got = lax.all_to_all(parcel, "blk", 0, 0, tiled=True)
-    other = lax.ppermute(got[:, :kept, :], "blk", partner_pairs())
-    steps = 4
+    other = lax.ppermute(got, "blk", partner_pairs())
+    steps = 2
     chunk = devices // steps
 
     def kernel(got_ref, other_ref, out_ref):
         step = pl.program_id(0)
         near = got_ref[:, :kept, :].reshape(devices * kept, 2 * HEAD)
-        far = other_ref[...].reshape(devices * kept, 2 * HEAD)
+        far = other_ref[:, :kept, :].reshape(devices * kept, 2 * HEAD)
         asked_now = got_ref[pl.ds(step * chunk, chunk), kept:, :].reshape(chunk * part, 2 * HEAD)
         dims = (((1,), (1,)), ((), ()))
         near_scores = lax.dot_general(asked_now, near, dims, preferred_element_type=jnp.float32) * scale

time: 157 us -> 161 us (1.025)
  Pallas kernels: 8.8 us -> 14.5 us
  local copies, waits for them, and re-layouts: 14.7 us -> 13 us
    pallas_call x1, Pallas kernels: 8.8 us -> 12.3 us  [attend_heads(): pl.pallas_call(kernel, grid=(steps,), in_specs=[pl.BlockSpec(got.shape, l...]
    pallas_call x0 -> x1, Pallas kernels: none -> 2.19 us  [attend_heads(): pl.pallas_call(pack, out_shape=jax.ShapeDtypeStruct((devices, kept + part...]
    unnamed x54 -> x52, local copies, waits for them, and re-layouts: 5.51 us -> 3.36 us
  transfers between devices with their start and end apart: 6 -> 6, of which waited for: 5 -> 4; matrix products, arithmetic and copies ran while one was open for 14% -> 15% of each run, Pallas kernels for 0% -> 0%
where the time goes in v7:
time: 161 us; the launch traced here: 160 us
  waiting for transfers between devices  42 us (26%)
  blocking collectives  36.2 us (22%)
  matrix products  29.3 us (18%)
  starting transfers between devices  19.2 us (12%)
  Pallas kernels  14.5 us (9%)
  local copies, waits for them, and re-layouts  13 us (8%)
  other arithmetic  4.8 us (3%)
    all_to_all x1, blocking collectives, to_experts(): lax.all_to_all(buffer, ('table', 'blk'), split_axis=0, concat_axis=0, til...  36.2 us
    all_to_all x1, waiting for transfers between devices, to_anchor(): lax.all_to_all(buffer, ('table', 'blk'), split_axis=0, concat_axis=0, til...  19.4 us
    all_to_all x1, waiting for transfers between devices, attend_heads(): got = lax.all_to_all(parcel, 'blk', 0, 0, tiled=True)  14 us
    pallas_call x1, Pallas kernels, attend_heads(): pl.pallas_call(kernel, grid=(steps,), in_specs=[pl.BlockSpec(got.shape, l...  12.3 us
    all_to_all x1, starting transfers between devices, attend_heads(): got = lax.all_to_all(parcel, 'blk', 0, 0, tiled=True)  9.42 us
    all_to_all x1, waiting for transfers between devices, attend_heads(): back = lax.all_to_all(mixed, 'blk', 0, 0, tiled=True)  7.58 us
    dot_general x2, matrix products, piece_pass(): jnp.einsum('scd,scf->df', inputs, grad_pre_up, preferred_element_type=jnp...  4.77 us
    dot_general x2, matrix products, piece_pass(): jnp.einsum('scf,scd->fd', hidden, cots, preferred_element_type=jnp.float32)  4.31 us
  transfers between devices with their start and end apart: 6, of which 4 were waited for; matrix products, arithmetic and copies ran while one was open for 15% of the time, Pallas kernels for 0%

profile of v7, /device:TPU:1, one launch (start us, length us, event | category | flops | bytes accessed | tf_op | source)
XLA Modules:
  0.0 160.2 jit_solution(7592449971735209784)
XLA Ops:
  0.7 2.2 %shard_map.146 = bf16[32,96,128]{2,1,0:T(8,128)(2,1)} custom-call(bf16[128,512]{1,0:T(8,128)(2,1)} %bitcast.130, bf16[128,512]{1,0:T(8,128)(2,1)} %bitcast.131, bf16[128,512]{1,0:T(8,128)(2,1)} %bitcast.132), custom_call_target="tpu_custom_call" | custom-call | tf_op jit(solution)/shard_map/pallas_call | solution.py:95
  2.9 9.4 %all-to-all-start = ((bf16[32,96,128]{2,1,0:T(8,128)(2,1)}), bf16[32,96,128]{2,1,0:T(8,128)(2,1)S(1)}, u32[]{:S(2)}, u32[]{:S(2)}) async-start(bf16[32,96,128]{2,1,0:T(8,128)(2,1)} %shard_map.146), calls=%async_computation | async-start | bytes 1572864 | tf_op jit(solution)/shard_map/all_to_all | solution.py:99
  12.6 14.0 %all-to-all-done.got_ref = bf16[32,96,128]{2,1,0:T(8,128)(2,1)S(1)} async-done(((bf16[32,96,128]{2,1,0:T(8,128)(2,1)}), bf16[32,96,128]{2,1,0:T(8,128)(2,1)S(1)}, u32[]{:S(2)}, u32[]{:S(2)}) %all-to-all-start) | async-done | bytes 786464 | tf_op jit(solution)/shard_map/all_to_all | solution.py:99
  29.3 1.4 reshape.95
  31.6 12.3 %shard_map.147 = bf16[32,32,64]{2,1,0:T(8,128)(2,1)S(1)} custom-call(bf16[32,96,128]{2,1,0:T(8,128)(2,1)S(1)} %all-to-all-done.got_ref, bf16[32,96,128]{2,1,0:T(8,128)(2,1)S(1)} %collective-permute-done.other_ref), custom_call_target="tpu_custom_call" | custom-call | flops 2147483648 | bytes 1703936 | tf_op jit(solution)/shard_map/pallas_call | solution.py:125
  44.8 3.7 %all-to-all-start.1 = ((bf16[32,2,1024]{2,1,0:T(2,128)(2,1)}), bf16[32,2,1024]{2,1,0:T(2,128)(2,1)S(1)}, u32[]{:S(2)}, u32[]{:S(2)}) async-start(bf16[32,2,1024]{2,1,0:T(2,128)(2,1)} %reshape.112), calls=%async_computation.1 | async-start | bytes 262144 | tf_op jit(solution)/shard_map/all_to_all | solution.py:141
  48.6 7.6 %all-to-all-done.1 = bf16[32,2,1024]{2,1,0:T(2,128)(2,1)S(1)} async-done(((bf16[32,2,1024]{2,1,0:T(2,128)(2,1)}), bf16[32,2,1024]{2,1,0:T(2,128)(2,1)S(1)}, u32[]{:S(2)}, u32[]{:S(2)}) %all-to-all-start.1) | async-done | bytes 131104 | tf_op jit(solution)/shard_map/all_to_all | solution.py:141
  59.0 36.2 %all_to_all.20 = bf16[128,6,1024]{2,1,0:T(8,128)(2,1)S(1)} all-to-all(bf16[128,6,1024]{2,1,0:T(8,128)(2,1)S(1)} %copy.39), channel_id=1, replica_groups=mesh['table'=4,'blk'=32] {'table','blk'}, dimensions={0} | all-to-all | bytes 3145728 | tf_op jit(solution)/shard_map/all_to_all | solution.py:26
  96.1 1.0 collective-permute-start.1
  97.1 1.0 fusion.11
  98.2 1.0 fusion.26
  99.2 1.0 collective-permute-done.1
  100.2 1.0 fusion.8
  101.2 1.0 fusion.22
  102.2 2.1 %multiply_convert_fusion.2 = (bf16[128,6,1024]{2,0,1:T(8,128)(2,1)S(1)}, bf16[128,6,1024]{2,0,1:T(8,128)(2,1)S(1)}, bf16[128,6,1024]{2,0,1:T(8,128)(2,1)S(1)}) fusion(f32[128,6,1024]{2,0,1:T(8,128)S(1)} %fusion.22, f32[128,6,1024]{2,0,1:T(8,128)S(1)} %fusion.8, bf16[1,512,1024]{2,1,0:T(8,128)(2,1)S(1)} %copy-done, ...), kind=kOutput, calls=%fused_computation.3 | convolution fusion | flops 817102848 | bytes 12845056 | tf_op jit(solution)/shard_map/scd,df->scf/dot_general | solution.py:46
  106.0 1.0 fusion.20
  107.0 1.0 add_convert_fusion.1
  109.0 2.1 %multiply_convert_fusion.5 = (bf16[128,6,1024]{2,0,1:T(8,128)(2,1)S(1)}, bf16[128,6,1024]{2,0,1:T(8,128)(2,1)S(1)}, bf16[128,6,1024]{2,0,1:T(8,128)(2,1)S(1)}) fusion(f32[128,6,1024]{2,0,1:T(8,128)S(1)} %fusion.26, f32[128,6,1024]{2,0,1:T(8,128)S(1)} %fusion.11, bf16[1,512,1024]{2,1,0:T(8,128)(2,1)S(1)} %copy-done, bf16[128,6,1024]{2,0,1:T(8,128)(2,1)S(1)} %copy.40), kind=kOutput, calls=%fused_computation.8 | convolution fusion | flops 817102848 | bytes 12845056 | tf_op jit(solution)/shard_map/scd,df->scf/dot_general | solution.py:46
  111.1 1.0 convolution_convert_fusion.2
  112.3 1.0 fusion.24
  113.3 2.3 %fusion.32 = f32[1024,512,1]{1,0,2:T(8,128)} fusion(bf16[128,6,1024]{2,0,1:T(8,128)(2,1)S(1)} %get-tuple-element.5, bf16[128,6,1024]{2,0,1:T(8,128)(2,1)S(1)} %copy.40), kind=kOutput, calls=%fused_computation.52 | convolution fusion | flops 805306368 | bytes 4456448 | tf_op jit(solution)/shard_map/scf,scd->fd/dot_general | solution.py:59
  115.7 1.0 add_convert_fusion.2
  117.3 2.2 %copy.43 = bf16[128,6,1024]{2,1,0:T(8,128)(2,1)} copy(bf16[128,6,1024]{2,0,1:T(8,128)(2,1)S(1)} %add_convert_fusion) | data formatting | bytes 3145728 | tf_op jit(solution)/shard_map/convert_element_type | solution.py:191
  119.5 3.8 %all-to-all-start.3 = ((bf16[128,6,1024]{2,1,0:T(8,128)(2,1)}), bf16[128,6,1024]{2,1,0:T(8,128)(2,1)S(1)}, u32[]{:S(2)}, u32[]{:S(2)}) async-start(bf16[128,6,1024]{2,1,0:T(8,128)(2,1)} %copy.43), calls=%async_computation.3 | async-start | bytes 4194304 | tf_op jit(solution)/shard_map/all_to_all | solution.py:30
  123.4 2.8 %fusion.41 = f32[512,1024,1]{1,0,2:T(8,128)S(1)} fusion(bf16[128,6,1024]{2,0,1:T(8,128)(2,1)} %copy-done.23, bf16[128,6,1024]{2,0,1:T(8,128)(2,1)} %copy-done.1), kind=kOutput, calls=%fused_computation.64 | convolution fusion | flops 805306368 | bytes 4456448 | tf_op jit(solution)/shard_map/scd,scf->df/dot_general | solution.py:61
  126.2 1.0 fusion.43
  128.3 2.0 %fusion.7 = bf16[1,1024,512]{2,1,0:T(8,128)(2,1)} fusion(bf16[128,6,1024]{2,0,1:T(8,128)(2,1)S(1)} %copy-done.20, f32[1024,512,1]{1,0,2:T(8,128)S(1)} %copy-done.14, bf16[128,6,1024]{2,0,1:T(8,128)(2,1)S(1)} %copy-done.6), kind=kOutput, calls=%fused_computation.25 | convolution fusion | flops 806354944 | bytes 5505024 | tf_op jit(solution)/shard_map/scf,scd->fd/dot_general | solution.py:59
  130.3 2.0 %fusion.6 = bf16[1,512,1024]{2,1,0:T(8,128)(2,1)} fusion(bf16[128,6,1024]{2,0,1:T(8,128)(2,1)S(1)} %copy-done.18, f32[512,1024,1]{1,0,2:T(8,128)S(1)} %fusion.41, bf16[128,6,1024]{2,0,1:T(8,128)(2,1)S(1)} %copy-done.6), kind=kOutput, calls=%fused_computation.24 | convolution fusion | flops 806354944 | bytes 5505024 | tf_op jit(solution)/shard_map/scd,scf->df/dot_general | solution.py:61
  132.3 2.0 %fusion.5 = bf16[1,512,1024]{2,1,0:T(8,128)(2,1)} fusion(bf16[128,6,1024]{2,0,1:T(8,128)(2,1)S(1)} %copy-done.16, f32[512,1024,1]{1,0,2:T(8,128)S(1)} %fusion.43, bf16[128,6,1024]{2,0,1:T(8,128)(2,1)S(1)} %copy-done.6), kind=kOutput, calls=%fused_computation.23 | convolution fusion | flops 806354944 | bytes 5505024 | tf_op jit(solution)/shard_map/scd,scf->df/dot_general | solution.py:60
  134.3 19.4 %all-to-all-done.3 = bf16[128,6,1024]{2,1,0:T(8,128)(2,1)S(1)} async-done(((bf16[128,6,1024]{2,1,0:T(8,128)(2,1)}), bf16[128,6,1024]{2,1,0:T(8,128)(2,1)S(1)}, u32[]{:S(2)}, u32[]{:S(2)}) %all-to-all-start.3) | async-done | bytes 1572896 | tf_op jit(solution)/shard_map/all_to_all | solution.py:30
  153.7 1.5 reshape.96
  155.2 2.0 %fusion.28 = f32[256,1024]{1,0:T(8,128)S(1)} fusion(bf16[768,1024]{1,0:T(8,128)(2,1)} %reshape.96, s32[256]{0:T(256)S(1)} %multiply_add_fusion.1), kind=kOutput, calls=%fused_computation.48 | convolution fusion | flops 402849792 | bytes 2622464 | tf_op jit(solution)/shard_map/dot_general | solution.py:194
  (91 shorter events, 15.8 us)
Async XLA Ops:
  0.6 101.6 %copy-start = (bf16[1,512,1024]{2,1,0:T(8,128)(2,1)S(1)}, bf16[1,512,1024]{2,1,0:T(8,128)(2,1)}, u32[]{:S(2)}) copy-start(bf16[1,512,1024]{2,1,0:T(8,128)(2,1)} %param.20) | copy-start | bytes 3145732
  0.6 11.6 %copy-start.12 = (s32[1,128,2]{1,2,0:T(2,128)S(1)}, s32[1,128,2]{1,2,0:T(2,128)}, u32[]{:S(2)}) copy-start(s32[1,128,2]{1,2,0:T(2,128)} %param.16) | copy-start | bytes 3076
  0.7 27.4 %copy-start.13 = (f32[1,128,2]{1,2,0:T(2,128)S(1)}, f32[1,128,2]{1,2,0:T(2,128)}, u32[]{:S(2)}) copy-start(f32[1,128,2]{1,2,0:T(2,128)} %param.17) | copy-start | bytes 3076
  0.7 27.6 %copy-start.9 = (bf16[1,128,512]{2,1,0:T(8,128)(2,1)S(1)}, bf16[1,128,512]{2,1,0:T(8,128)(2,1)}, u32[]{:S(2)}) copy-start(bf16[1,128,512]{2,1,0:T(8,128)(2,1)} %param.18) | copy-start | bytes 393220
  2.9 23.7 %all-to-all-start = ((bf16[32,96,128]{2,1,0:T(8,128)(2,1)}), bf16[32,96,128]{2,1,0:T(8,128)(2,1)S(1)}, u32[]{:S(2)}, u32[]{:S(2)}) async-start(bf16[32,96,128]{2,1,0:T(8,128)(2,1)} %shard_map.146), calls=%async_computation | async-start | bytes 1572864 | tf_op jit(solution)/shard_map/all_to_all | solution.py:99
  26.5 5.1 %collective-permute-start = (bf16[32,96,128]{2,1,0:T(8,128)(2,1)S(1)}, bf16[32,96,128]{2,1,0:T(8,128)(2,1)S(1)}, u32[]{:S(2)}, u32[]{:S(2)}) collective-permute-start(bf16[32,96,128]{2,1,0:T(8,128)(2,1)S(1)} %all-to-all-done.got_ref), channel_id=1, source_target_pairs={{0,1},{1,0},{2,3},{3,2},{4,5},{5,4},{6,7},{7,6},{8,9},{9,8},{10,11... | collective-permute-start | bytes 2359304 | tf_op jit(solution)/shard_map/ppermute | solution.py:100
  44.0 12.8 %copy-start.8 = (bf16[512,512]{1,0:T(8,128)(2,1)S(1)}, bf16[512,512]{1,0:T(8,128)(2,1)}, u32[]{:S(2)}) copy-start(bf16[512,512]{1,0:T(8,128)(2,1)} %param.15) | copy-start | bytes 1572868
  44.0 12.8 %copy-start.11 = (bf16[1,128,512]{2,1,0:T(8,128)(2,1)S(1)}, bf16[1,128,512]{2,1,0:T(8,128)(2,1)}, u32[]{:S(2)}) copy-start(bf16[1,128,512]{2,1,0:T(8,128)(2,1)} %param.11) | copy-start | bytes 393220
  44.8 11.3 %all-to-all-start.1 = ((bf16[32,2,1024]{2,1,0:T(2,128)(2,1)}), bf16[32,2,1024]{2,1,0:T(2,128)(2,1)S(1)}, u32[]{:S(2)}, u32[]{:S(2)}) async-start(bf16[32,2,1024]{2,1,0:T(2,128)(2,1)} %reshape.112), calls=%async_computation.1 | async-start | bytes 262144 | tf_op jit(solution)/shard_map/all_to_all | solution.py:141
  56.4 1.1 copy-start.7
  95.2 1.9 %copy-start.3 = (bf16[1,1024,512]{2,1,0:T(8,128)(2,1)S(1)}, bf16[1,1024,512]{2,1,0:T(8,128)(2,1)}, u32[]{:S(2)}) copy-start(bf16[1,1024,512]{2,1,0:T(8,128)(2,1)} %param.21) | copy-start | bytes 3145732
  96.1 17.3 %copy-start.1 = (bf16[128,6,1024]{2,0,1:T(8,128)(2,1)}, bf16[128,6,1024]{2,0,1:T(8,128)(2,1)S(1)}, u32[]{:S(2)}) copy-start(bf16[128,6,1024]{2,0,1:T(8,128)(2,1)S(1)} %copy.40) | copy-start | bytes 4718596
  96.1 2.1 %copy-start.4 = (bf16[1,512,1024]{2,1,0:T(8,128)(2,1)S(1)}, bf16[1,512,1024]{2,1,0:T(8,128)(2,1)}, u32[]{:S(2)}) copy-start(bf16[1,512,1024]{2,1,0:T(8,128)(2,1)} %param.19) | copy-start | bytes 3145732
  96.1 4.1 %collective-permute-start.1 = (bf16[128,6,1024]{2,0,1:T(8,128)(2,1)S(1)}, bf16[128,6,1024]{2,0,1:T(8,128)(2,1)S(1)}, u32[]{:S(2)}, u32[]{:S(2)}) collective-permute-start(bf16[128,6,1024]{2,0,1:T(8,128)(2,1)S(1)} %copy.40), channel_id=1, source_target_pairs={{0,1},{1,0},{2,3},{3,2},{4,5},{5,4},{6,7},{7,6},{8,9},{9,8},{10,11... | collective-permute-start | bytes 4718600 | tf_op jit(solution)/shard_map/ppermute | solution.py:40
  100.2 2.0 %copy-start.5 = (bf16[128,6,1024]{2,0,1:T(8,128)(2,1)}, bf16[128,6,1024]{2,0,1:T(8,128)(2,1)S(1)}, u32[]{:S(2)}) copy-start(bf16[128,6,1024]{2,0,1:T(8,128)(2,1)S(1)} %collective-permute-done.1) | copy-start | bytes 4718596
  104.3 1.2 copy-start.19
  104.3 1.7 %copy-start.15 = (bf16[128,6,1024]{2,0,1:T(8,128)(2,1)}, bf16[128,6,1024]{2,0,1:T(8,128)(2,1)S(1)}, u32[]{:S(2)}) copy-start(bf16[128,6,1024]{2,0,1:T(8,128)(2,1)S(1)} %get-tuple-element.9) | copy-start | bytes 4718596
  104.4 2.7 %copy-start.17 = (bf16[128,6,1024]{2,0,1:T(8,128)(2,1)}, bf16[128,6,1024]{2,0,1:T(8,128)(2,1)S(1)}, u32[]{:S(2)}) copy-start(bf16[128,6,1024]{2,0,1:T(8,128)(2,1)S(1)} %get-tuple-element.10) | copy-start | bytes 4718596
  108.3 8.4 %collective-permute-start.2 = (bf16[128,6,1024]{2,0,1:T(8,128)(2,1)S(1)}, bf16[128,6,1024]{2,0,1:T(8,128)(2,1)S(1)}, u32[]{:S(2)}, u32[]{:S(2)}) collective-permute-start(bf16[128,6,1024]{2,0,1:T(8,128)(2,1)S(1)} %pad_maximum_fusion), channel_id=1, source_target_pairs={{0,1},{1,0},{2,3},{3,2},{4,5},{5,4},{6,7},{7,6},{8,9},{9,8},{10,11... | collective-permute-start | bytes 4718600 | tf_op jit(solution)/shard_map/ppermute | solution.py:190
  111.1 1.2 copy-start.21
  111.1 4.6 %copy-start.23 = (bf16[128,6,1024]{2,0,1:T(8,128)(2,1)}, bf16[128,6,1024]{2,0,1:T(8,128)(2,1)S(1)}, u32[]{:S(2)}) copy-start(bf16[128,6,1024]{2,0,1:T(8,128)(2,1)S(1)} %get-tuple-element.7) | copy-start | bytes 4718596
  119.5 34.2 %all-to-all-start.3 = ((bf16[128,6,1024]{2,1,0:T(8,128)(2,1)}), bf16[128,6,1024]{2,1,0:T(8,128)(2,1)S(1)}, u32[]{:S(2)}, u32[]{:S(2)}) async-start(bf16[128,6,1024]{2,1,0:T(8,128)(2,1)} %copy.43), calls=%async_computation.3 | async-start | bytes 4194304 | tf_op jit(solution)/shard_map/all_to_all | solution.py:30
  123.4 2.8 %copy-start.2 = (bf16[128,6,1024]{2,0,1:T(8,128)(2,1)S(1)}, bf16[128,6,1024]{2,0,1:T(8,128)(2,1)}, u32[]{:S(2)}) copy-start(bf16[128,6,1024]{2,0,1:T(8,128)(2,1)} %copy-done.1) | copy-start | bytes 4718596
  123.4 2.8 %copy-start.22 = (bf16[128,6,1024]{2,0,1:T(8,128)(2,1)S(1)}, bf16[128,6,1024]{2,0,1:T(8,128)(2,1)}, u32[]{:S(2)}) copy-start(bf16[128,6,1024]{2,0,1:T(8,128)(2,1)} %copy-done.21) | copy-start | bytes 4718596
  123.4 3.9 %copy-start.20 = (bf16[128,6,1024]{2,0,1:T(8,128)(2,1)S(1)}, bf16[128,6,1024]{2,0,1:T(8,128)(2,1)}, u32[]{:S(2)}) copy-start(bf16[128,6,1024]{2,0,1:T(8,128)(2,1)} %copy-done.19) | copy-start | bytes 4718596
  126.2 1.5 copy-start.6
  126.2 2.1 %copy-start.14 = (f32[1024,512,1]{1,0,2:T(8,128)S(1)}, f32[1024,512,1]{1,0,2:T(8,128)}, u32[]{:S(2)}) copy-start(f32[1024,512,1]{1,0,2:T(8,128)} %fusion.32) | copy-start | bytes 6291460
  128.3 2.0 %copy-start.18 = (bf16[128,6,1024]{2,0,1:T(8,128)(2,1)S(1)}, bf16[128,6,1024]{2,0,1:T(8,128)(2,1)}, u32[]{:S(2)}) copy-start(bf16[128,6,1024]{2,0,1:T(8,128)(2,1)} %copy-done.17) | copy-start | bytes 4718596
  130.3 2.0 %copy-start.16 = (bf16[128,6,1024]{2,0,1:T(8,128)(2,1)S(1)}, bf16[128,6,1024]{2,0,1:T(8,128)(2,1)}, u32[]{:S(2)}) copy-start(bf16[128,6,1024]{2,0,1:T(8,128)(2,1)} %copy-done.15) | copy-start | bytes 4718596
  157.6 1.8 %copy-start.10 = (bf16[1,128,512]{2,1,0:T(8,128)(2,1)S(1)}, bf16[1,128,512]{2,1,0:T(8,128)(2,1)}, u32[]{:S(2)}) copy-start(bf16[1,128,512]{2,1,0:T(8,128)(2,1)} %param.18) | copy-start | bytes 393220

commit v8 on v7

--- a/solution.py
+++ b/solution.py
@@ -97,14 +97,14 @@
         out_shape=jax.ShapeDtypeStruct((devices, kept + part, 2 * HEAD), jnp.bfloat16),
     )(key_rows, value_rows, query_rows)
     got = lax.all_to_all(parcel, "blk", 0, 0, tiled=True)
-    other = lax.ppermute(got, "blk", partner_pairs())
-    steps = 2
+    other = lax.ppermute(got[:, :kept, :], "blk", partner_pairs())
+    steps = 8
     chunk = devices // steps
 
     def kernel(got_ref, other_ref, out_ref):
         step = pl.program_id(0)
         near = got_ref[:, :kept, :].reshape(devices * kept, 2 * HEAD)
-        far = other_ref[:, :kept, :].reshape(devices * kept, 2 * HEAD)
+        far = other_ref[...].reshape(devices * kept, 2 * HEAD)
         asked_now = got_ref[pl.ds(step * chunk, chunk), kept:, :].reshape(chunk * part, 2 * HEAD)
         dims = (((1,), (1,)), ((), ()))
         near_scores = lax.dot_general(asked_now, near, dims, preferred_element_type=jnp.float32) * scale

time: 161 us -> 158 us (0.981)
  Pallas kernels: 14.5 us -> 12.8 us
    pallas_call x1, Pallas kernels: 12.3 us -> 10.6 us  [attend_heads(): pl.pallas_call(kernel, grid=(steps,), in_specs=[pl.BlockSpec(got.shape, l...]
    unnamed x52 -> x48, local copies, waits for them, and re-layouts: 3.36 us -> 3.32 us
where the time goes in v8:
time: 158 us
  waiting for transfers between devices  40.7 us (26%)
  blocking collectives  36.2 us (23%)
  matrix products  29.3 us (19%)
  starting transfers between devices  19.5 us (12%)
  local copies, waits for them, and re-layouts  13.8 us (9%)
  Pallas kernels  12.8 us (8%)
  other arithmetic  4.09 us (3%)
    all_to_all x1, blocking collectives, to_experts(): lax.all_to_all(buffer, ('table', 'blk'), split_axis=0, concat_axis=0, til...  36.2 us
    all_to_all x1, waiting for transfers between devices, to_anchor(): lax.all_to_all(buffer, ('table', 'blk'), split_axis=0, concat_axis=0, til...  19.4 us
    all_to_all x1, waiting for transfers between devices, attend_heads(): got = lax.all_to_all(parcel, 'blk', 0, 0, tiled=True)  12.7 us
    pallas_call x1, Pallas kernels, attend_heads(): pl.pallas_call(kernel, grid=(steps,), in_specs=[pl.BlockSpec(got.shape, l...  10.6 us
    all_to_all x1, starting transfers between devices, attend_heads(): got = lax.all_to_all(parcel, 'blk', 0, 0, tiled=True)  9.55 us
    all_to_all x1, waiting for transfers between devices, attend_heads(): back = lax.all_to_all(mixed, 'blk', 0, 0, tiled=True)  7.58 us
    dot_general x2, matrix products, piece_pass(): jnp.einsum('scd,scf->df', inputs, grad_pre_up, preferred_element_type=jnp...  4.77 us
    dot_general x2, matrix products, piece_pass(): jnp.einsum('scf,scd->fd', hidden, cots, preferred_element_type=jnp.float32)  4.31 us
  transfers between devices with their start and end apart: 6, of which 4 were waited for; matrix products, arithmetic and copies ran while one was open for 15% of the time, Pallas kernels for 0%

profile of v8, /device:TPU:1, one launch (start us, length us, event | category | flops | bytes accessed | tf_op | source)
XLA Modules:
  0.0 157.6 jit_solution(4686682780325908431)
XLA Ops:
  0.7 2.2 %shard_map.146 = bf16[32,96,128]{2,1,0:T(8,128)(2,1)} custom-call(bf16[128,512]{1,0:T(8,128)(2,1)} %bitcast.130, bf16[128,512]{1,0:T(8,128)(2,1)} %bitcast.131, bf16[128,512]{1,0:T(8,128)(2,1)} %bitcast.132), custom_call_target="tpu_custom_call" | custom-call | tf_op jit(solution)/shard_map/pallas_call | solution.py:95
  2.9 9.6 %all-to-all-start = ((bf16[32,96,128]{2,1,0:T(8,128)(2,1)}), bf16[32,96,128]{2,1,0:T(8,128)(2,1)S(1)}, u32[]{:S(2)}, u32[]{:S(2)}) async-start(bf16[32,96,128]{2,1,0:T(8,128)(2,1)} %shard_map.146), calls=%async_computation | async-start | bytes 1572864 | tf_op jit(solution)/shard_map/all_to_all | solution.py:99
  13.9 12.7 %all-to-all-done.got_ref = bf16[32,96,128]{2,1,0:T(8,128)(2,1)S(1)} async-done(((bf16[32,96,128]{2,1,0:T(8,128)(2,1)}), bf16[32,96,128]{2,1,0:T(8,128)(2,1)S(1)}, u32[]{:S(2)}, u32[]{:S(2)}) %all-to-all-start) | async-done | bytes 786464 | tf_op jit(solution)/shard_map/all_to_all | solution.py:99
  28.1 1.0 broadcast_in_dim.27
  29.0 1.4 reshape.95
  30.7 10.6 %shard_map.147 = bf16[32,32,64]{2,1,0:T(8,128)(2,1)S(1)} custom-call(bf16[32,96,128]{2,1,0:T(8,128)(2,1)S(1)} %all-to-all-done.got_ref, bf16[32,64,128]{2,1,0:T(8,128)(2,1)S(1)} %collective-permute-done.other_ref), custom_call_target="tpu_custom_call" | custom-call | flops 2147483648 | bytes 1441792 | tf_op jit(solution)/shard_map/pallas_call | solution.py:125
  42.2 3.7 %all-to-all-start.1 = ((bf16[32,2,1024]{2,1,0:T(2,128)(2,1)}), bf16[32,2,1024]{2,1,0:T(2,128)(2,1)S(1)}, u32[]{:S(2)}, u32[]{:S(2)}) async-start(bf16[32,2,1024]{2,1,0:T(2,128)(2,1)} %reshape.112), calls=%async_computation.1 | async-start | bytes 262144 | tf_op jit(solution)/shard_map/all_to_all | solution.py:141
  45.9 7.6 %all-to-all-done.1 = bf16[32,2,1024]{2,1,0:T(2,128)(2,1)S(1)} async-done(((bf16[32,2,1024]{2,1,0:T(2,128)(2,1)}), bf16[32,2,1024]{2,1,0:T(2,128)(2,1)S(1)}, u32[]{:S(2)}, u32[]{:S(2)}) %all-to-all-start.1) | async-done | bytes 131104 | tf_op jit(solution)/shard_map/all_to_all | solution.py:141
  56.3 36.2 %all_to_all.20 = bf16[128,6,1024]{2,1,0:T(8,128)(2,1)S(1)} all-to-all(bf16[128,6,1024]{2,1,0:T(8,128)(2,1)S(1)} %copy.39), channel_id=1, replica_groups=mesh['table'=4,'blk'=32] {'table','blk'}, dimensions={0} | all-to-all | bytes 3145728 | tf_op jit(solution)/shard_map/all_to_all | solution.py:26
  93.4 1.2 collective-permute-start.1
  94.6 1.0 fusion.11
  95.6 1.0 fusion.26
  96.6 1.0 collective-permute-done.1
  97.6 1.0 fusion.8
  98.7 1.0 fusion.22
  99.7 2.1 %multiply_convert_fusion.2 = (bf16[128,6,1024]{2,0,1:T(8,128)(2,1)S(1)}, bf16[128,6,1024]{2,0,1:T(8,128)(2,1)S(1)}, bf16[128,6,1024]{2,0,1:T(8,128)(2,1)S(1)}) fusion(f32[128,6,1024]{2,0,1:T(8,128)S(1)} %fusion.22, f32[128,6,1024]{2,0,1:T(8,128)S(1)} %fusion.8, bf16[1,512,1024]{2,1,0:T(8,128)(2,1)S(1)} %copy-done, ...), kind=kOutput, calls=%fused_computation.3 | convolution fusion | flops 817102848 | bytes 12845056 | tf_op jit(solution)/shard_map/scd,df->scf/dot_general | solution.py:46
  103.5 1.0 fusion.20
  104.5 1.0 add_convert_fusion.1
  106.4 2.1 %multiply_convert_fusion.5 = (bf16[128,6,1024]{2,0,1:T(8,128)(2,1)S(1)}, bf16[128,6,1024]{2,0,1:T(8,128)(2,1)S(1)}, bf16[128,6,1024]{2,0,1:T(8,128)(2,1)S(1)}) fusion(f32[128,6,1024]{2,0,1:T(8,128)S(1)} %fusion.26, f32[128,6,1024]{2,0,1:T(8,128)S(1)} %fusion.11, bf16[1,512,1024]{2,1,0:T(8,128)(2,1)S(1)} %copy-done, bf16[128,6,1024]{2,0,1:T(8,128)(2,1)S(1)} %copy.40), kind=kOutput, calls=%fused_computation.8 | convolution fusion | flops 817102848 | bytes 12845056 | tf_op jit(solution)/shard_map/scd,df->scf/dot_general | solution.py:46
  109.8 1.0 fusion.24
  110.8 2.3 %fusion.32 = f32[1024,512,1]{1,0,2:T(8,128)} fusion(bf16[128,6,1024]{2,0,1:T(8,128)(2,1)S(1)} %get-tuple-element.5, bf16[128,6,1024]{2,0,1:T(8,128)(2,1)S(1)} %copy.40), kind=kOutput, calls=%fused_computation.52 | convolution fusion | flops 805306368 | bytes 4456448 | tf_op jit(solution)/shard_map/scf,scd->fd/dot_general | solution.py:59
  113.1 1.0 add_convert_fusion.2
  114.7 2.2 %copy.43 = bf16[128,6,1024]{2,1,0:T(8,128)(2,1)} copy(bf16[128,6,1024]{2,0,1:T(8,128)(2,1)S(1)} %add_convert_fusion) | data formatting | bytes 3145728 | tf_op jit(solution)/shard_map/convert_element_type | solution.py:191
  116.9 3.8 %all-to-all-start.3 = ((bf16[128,6,1024]{2,1,0:T(8,128)(2,1)}), bf16[128,6,1024]{2,1,0:T(8,128)(2,1)S(1)}, u32[]{:S(2)}, u32[]{:S(2)}) async-start(bf16[128,6,1024]{2,1,0:T(8,128)(2,1)} %copy.43), calls=%async_computation.3 | async-start | bytes 4194304 | tf_op jit(solution)/shard_map/all_to_all | solution.py:30
  120.8 2.8 %fusion.41 = f32[512,1024,1]{1,0,2:T(8,128)S(1)} fusion(bf16[128,6,1024]{2,0,1:T(8,128)(2,1)} %copy-done.21, bf16[128,6,1024]{2,0,1:T(8,128)(2,1)} %copy-done.1), kind=kOutput, calls=%fused_computation.64 | convolution fusion | flops 805306368 | bytes 4456448 | tf_op jit(solution)/shard_map/scd,scf->df/dot_general | solution.py:61
  123.6 1.0 fusion.43
  125.7 2.0 %fusion.7 = bf16[1,1024,512]{2,1,0:T(8,128)(2,1)} fusion(bf16[128,6,1024]{2,0,1:T(8,128)(2,1)S(1)} %copy-done.18, f32[1024,512,1]{1,0,2:T(8,128)S(1)} %copy-done.12, bf16[128,6,1024]{2,0,1:T(8,128)(2,1)S(1)} %copy-done.6), kind=kOutput, calls=%fused_computation.25 | convolution fusion | flops 806354944 | bytes 5505024 | tf_op jit(solution)/shard_map/scf,scd->fd/dot_general | solution.py:59
  127.7 2.0 %fusion.6 = bf16[1,512,1024]{2,1,0:T(8,128)(2,1)} fusion(bf16[128,6,1024]{2,0,1:T(8,128)(2,1)S(1)} %copy-done.16, f32[512,1024,1]{1,0,2:T(8,128)S(1)} %fusion.41, bf16[128,6,1024]{2,0,1:T(8,128)(2,1)S(1)} %copy-done.6), kind=kOutput, calls=%fused_computation.24 | convolution fusion | flops 806354944 | bytes 5505024 | tf_op jit(solution)/shard_map/scd,scf->df/dot_general | solution.py:61
  129.7 2.0 %fusion.5 = bf16[1,512,1024]{2,1,0:T(8,128)(2,1)} fusion(bf16[128,6,1024]{2,0,1:T(8,128)(2,1)S(1)} %copy-done.14, f32[512,1024,1]{1,0,2:T(8,128)S(1)} %fusion.43, bf16[128,6,1024]{2,0,1:T(8,128)(2,1)S(1)} %copy-done.6), kind=kOutput, calls=%fused_computation.23 | convolution fusion | flops 806354944 | bytes 5505024 | tf_op jit(solution)/shard_map/scd,scf->df/dot_general | solution.py:60
  131.7 19.4 %all-to-all-done.3 = bf16[128,6,1024]{2,1,0:T(8,128)(2,1)S(1)} async-done(((bf16[128,6,1024]{2,1,0:T(8,128)(2,1)}), bf16[128,6,1024]{2,1,0:T(8,128)(2,1)S(1)}, u32[]{:S(2)}, u32[]{:S(2)}) %all-to-all-start.3) | async-done | bytes 1572896 | tf_op jit(solution)/shard_map/all_to_all | solution.py:30
  151.1 1.4 reshape.96
  152.5 2.0 %fusion.28 = f32[256,1024]{1,0:T(8,128)S(1)} fusion(bf16[768,1024]{1,0:T(8,128)(2,1)} %reshape.96, s32[256]{0:T(256)S(1)} %multiply_add_fusion.1), kind=kOutput, calls=%fused_computation.48 | convolution fusion | flops 402849792 | bytes 2622464 | tf_op jit(solution)/shard_map/dot_general | solution.py:194
  (88 shorter events, 16.0 us)
Async XLA Ops:
  0.6 99.0 %copy-start = (bf16[1,512,1024]{2,1,0:T(8,128)(2,1)S(1)}, bf16[1,512,1024]{2,1,0:T(8,128)(2,1)}, u32[]{:S(2)}) copy-start(bf16[1,512,1024]{2,1,0:T(8,128)(2,1)} %param.20) | copy-start | bytes 3145732
  0.6 11.8 %copy-start.10 = (s32[1,128,2]{1,2,0:T(2,128)S(1)}, s32[1,128,2]{1,2,0:T(2,128)}, u32[]{:S(2)}) copy-start(s32[1,128,2]{1,2,0:T(2,128)} %param.16) | copy-start | bytes 3076
  0.7 13.0 %copy-start.11 = (f32[1,128,2]{1,2,0:T(2,128)S(1)}, f32[1,128,2]{1,2,0:T(2,128)}, u32[]{:S(2)}) copy-start(f32[1,128,2]{1,2,0:T(2,128)} %param.17) | copy-start | bytes 3076
  2.8 25.2 %copy-start.8 = (bf16[1,128,512]{2,1,0:T(8,128)(2,1)S(1)}, bf16[1,128,512]{2,1,0:T(8,128)(2,1)}, u32[]{:S(2)}) copy-start(bf16[1,128,512]{2,1,0:T(8,128)(2,1)} %param.18) | copy-start | bytes 393220
  2.9 23.8 %all-to-all-start = ((bf16[32,96,128]{2,1,0:T(8,128)(2,1)}), bf16[32,96,128]{2,1,0:T(8,128)(2,1)S(1)}, u32[]{:S(2)}, u32[]{:S(2)}) async-start(bf16[32,96,128]{2,1,0:T(8,128)(2,1)} %shard_map.146), calls=%async_computation | async-start | bytes 1572864 | tf_op jit(solution)/shard_map/all_to_all | solution.py:99
  27.5 3.1 %collective-permute-start = (bf16[32,64,128]{2,1,0:T(8,128)(2,1)}, bf16[32,64,128]{2,1,0:T(8,128)(2,1)S(1)}, u32[]{:S(2)}, u32[]{:S(2)}) collective-permute-start(bf16[32,64,128]{2,1,0:T(8,128)(2,1)} %slice.36), channel_id=1, source_target_pairs={{0,1},{1,0},{2,3},{3,2},{4,5},{5,4},{6,7},{7,6},{8,9},{9,8},{10,11... | collective-permute-start | bytes 1572872 | tf_op jit(solution)/shard_map/ppermute | solution.py:100
  41.3 12.8 %copy-start.7 = (bf16[512,512]{1,0:T(8,128)(2,1)S(1)}, bf16[512,512]{1,0:T(8,128)(2,1)}, u32[]{:S(2)}) copy-start(bf16[512,512]{1,0:T(8,128)(2,1)} %param.15) | copy-start | bytes 1572868
  41.3 12.8 %copy-start.9 = (bf16[1,128,512]{2,1,0:T(8,128)(2,1)S(1)}, bf16[1,128,512]{2,1,0:T(8,128)(2,1)}, u32[]{:S(2)}) copy-start(bf16[1,128,512]{2,1,0:T(8,128)(2,1)} %param.11) | copy-start | bytes 393220
  42.2 11.3 %all-to-all-start.1 = ((bf16[32,2,1024]{2,1,0:T(2,128)(2,1)}), bf16[32,2,1024]{2,1,0:T(2,128)(2,1)S(1)}, u32[]{:S(2)}, u32[]{:S(2)}) async-start(bf16[32,2,1024]{2,1,0:T(2,128)(2,1)} %reshape.112), calls=%async_computation.1 | async-start | bytes 262144 | tf_op jit(solution)/shard_map/all_to_all | solution.py:141
  92.5 2.1 %copy-start.3 = (bf16[1,1024,512]{2,1,0:T(8,128)(2,1)S(1)}, bf16[1,1024,512]{2,1,0:T(8,128)(2,1)}, u32[]{:S(2)}) copy-start(bf16[1,1024,512]{2,1,0:T(8,128)(2,1)} %param.21) | copy-start | bytes 3145732
  93.4 17.4 %copy-start.1 = (bf16[128,6,1024]{2,0,1:T(8,128)(2,1)}, bf16[128,6,1024]{2,0,1:T(8,128)(2,1)S(1)}, u32[]{:S(2)}) copy-start(bf16[128,6,1024]{2,0,1:T(8,128)(2,1)S(1)} %copy.40) | copy-start | bytes 4718596
  93.4 2.3 %copy-start.4 = (bf16[1,512,1024]{2,1,0:T(8,128)(2,1)S(1)}, bf16[1,512,1024]{2,1,0:T(8,128)(2,1)}, u32[]{:S(2)}) copy-start(bf16[1,512,1024]{2,1,0:T(8,128)(2,1)} %param.19) | copy-start | bytes 3145732
  93.4 4.3 %collective-permute-start.1 = (bf16[128,6,1024]{2,0,1:T(8,128)(2,1)S(1)}, bf16[128,6,1024]{2,0,1:T(8,128)(2,1)S(1)}, u32[]{:S(2)}, u32[]{:S(2)}) collective-permute-start(bf16[128,6,1024]{2,0,1:T(8,128)(2,1)S(1)} %copy.40), channel_id=1, source_target_pairs={{0,1},{1,0},{2,3},{3,2},{4,5},{5,4},{6,7},{7,6},{8,9},{9,8},{10,11... | collective-permute-start | bytes 4718600 | tf_op jit(solution)/shard_map/ppermute | solution.py:40
  97.6 2.0 %copy-start.5 = (bf16[128,6,1024]{2,0,1:T(8,128)(2,1)}, bf16[128,6,1024]{2,0,1:T(8,128)(2,1)S(1)}, u32[]{:S(2)}) copy-start(bf16[128,6,1024]{2,0,1:T(8,128)(2,1)S(1)} %collective-permute-done.1) | copy-start | bytes 4718596
  101.8 1.2 copy-start.17
  101.8 1.6 %copy-start.13 = (bf16[128,6,1024]{2,0,1:T(8,128)(2,1)}, bf16[128,6,1024]{2,0,1:T(8,128)(2,1)S(1)}, u32[]{:S(2)}) copy-start(bf16[128,6,1024]{2,0,1:T(8,128)(2,1)S(1)} %get-tuple-element.9) | copy-start | bytes 4718596
  101.8 2.6 %copy-start.15 = (bf16[128,6,1024]{2,0,1:T(8,128)(2,1)}, bf16[128,6,1024]{2,0,1:T(8,128)(2,1)S(1)}, u32[]{:S(2)}) copy-start(bf16[128,6,1024]{2,0,1:T(8,128)(2,1)S(1)} %get-tuple-element.10) | copy-start | bytes 4718596
  105.7 8.4 %collective-permute-start.2 = (bf16[128,6,1024]{2,0,1:T(8,128)(2,1)S(1)}, bf16[128,6,1024]{2,0,1:T(8,128)(2,1)S(1)}, u32[]{:S(2)}, u32[]{:S(2)}) collective-permute-start(bf16[128,6,1024]{2,0,1:T(8,128)(2,1)S(1)} %pad_maximum_fusion), channel_id=1, source_target_pairs={{0,1},{1,0},{2,3},{3,2},{4,5},{5,4},{6,7},{7,6},{8,9},{9,8},{10,11... | collective-permute-start | bytes 4718600 | tf_op jit(solution)/shard_map/ppermute | solution.py:190
  108.5 1.2 copy-start.19
  108.5 4.6 %copy-start.21 = (bf16[128,6,1024]{2,0,1:T(8,128)(2,1)}, bf16[128,6,1024]{2,0,1:T(8,128)(2,1)S(1)}, u32[]{:S(2)}) copy-start(bf16[128,6,1024]{2,0,1:T(8,128)(2,1)S(1)} %get-tuple-element.7) | copy-start | bytes 4718596
  116.9 34.2 %all-to-all-start.3 = ((bf16[128,6,1024]{2,1,0:T(8,128)(2,1)}), bf16[128,6,1024]{2,1,0:T(8,128)(2,1)S(1)}, u32[]{:S(2)}, u32[]{:S(2)}) async-start(bf16[128,6,1024]{2,1,0:T(8,128)(2,1)} %copy.43), calls=%async_computation.3 | async-start | bytes 4194304 | tf_op jit(solution)/shard_map/all_to_all | solution.py:30
  120.8 2.8 %copy-start.2 = (bf16[128,6,1024]{2,0,1:T(8,128)(2,1)S(1)}, bf16[128,6,1024]{2,0,1:T(8,128)(2,1)}, u32[]{:S(2)}) copy-start(bf16[128,6,1024]{2,0,1:T(8,128)(2,1)} %copy-done.1) | copy-start | bytes 4718596
  120.8 2.8 %copy-start.20 = (bf16[128,6,1024]{2,0,1:T(8,128)(2,1)S(1)}, bf16[128,6,1024]{2,0,1:T(8,128)(2,1)}, u32[]{:S(2)}) copy-start(bf16[128,6,1024]{2,0,1:T(8,128)(2,1)} %copy-done.19) | copy-start | bytes 4718596
  120.8 3.9 %copy-start.18 = (bf16[128,6,1024]{2,0,1:T(8,128)(2,1)S(1)}, bf16[128,6,1024]{2,0,1:T(8,128)(2,1)}, u32[]{:S(2)}) copy-start(bf16[128,6,1024]{2,0,1:T(8,128)(2,1)} %copy-done.17) | copy-start | bytes 4718596
  123.6 1.5 copy-start.6
  123.6 2.1 %copy-start.12 = (f32[1024,512,1]{1,0,2:T(8,128)S(1)}, f32[1024,512,1]{1,0,2:T(8,128)}, u32[]{:S(2)}) copy-start(f32[1024,512,1]{1,0,2:T(8,128)} %fusion.32) | copy-start | bytes 6291460
  125.7 2.0 %copy-start.16 = (bf16[128,6,1024]{2,0,1:T(8,128)(2,1)S(1)}, bf16[128,6,1024]{2,0,1:T(8,128)(2,1)}, u32[]{:S(2)}) copy-start(bf16[128,6,1024]{2,0,1:T(8,128)(2,1)} %copy-done.15) | copy-start | bytes 4718596
  127.7 2.0 %copy-start.14 = (bf16[128,6,1024]{2,0,1:T(8,128)(2,1)S(1)}, bf16[128,6,1024]{2,0,1:T(8,128)(2,1)}, u32[]{:S(2)}) copy-start(bf16[128,6,1024]{2,0,1:T(8,128)(2,1)} %copy-done.13) | copy-start | bytes 4718596

commit v9 on v8

--- a/solution.py
+++ b/solution.py
@@ -75,15 +75,15 @@
         low = lane < HEAD
         for head in range(HEADS):
             cols = pl.ds((head // 2) * 2 * HEAD, 2 * HEAD)
-            key_tile = key_ref[:, cols].astype(jnp.float32)
-            value_tile = value_ref[:, cols].astype(jnp.float32)
+            key_tile = key_ref[:, cols]
+            value_tile = value_ref[:, cols]
             query_tile = query_ref[:, cols].astype(jnp.float32)
             if head % 2 == 0:
                 both = jnp.where(low, key_tile, pltpu.roll(value_tile, HEAD, 1))
-                ask = jnp.where(low, query_tile, 0.0)
+                ask = jnp.where(low, query_tile * scale, 0.0)
             else:
                 both = jnp.where(low, pltpu.roll(key_tile, HEAD, 1), value_tile)
-                ask = jnp.where(low, pltpu.roll(query_tile, HEAD, 1), 0.0)
+                ask = jnp.where(low, pltpu.roll(query_tile * scale, HEAD, 1), 0.0)
             both = both.astype(jnp.bfloat16)
             ask = ask.astype(jnp.bfloat16)
             for group in range(groups):
@@ -98,7 +98,7 @@
     )(key_rows, value_rows, query_rows)
     got = lax.all_to_all(parcel, "blk", 0, 0, tiled=True)
     other = lax.ppermute(got[:, :kept, :], "blk", partner_pairs())
-    steps = 8
+    steps = 4
     chunk = devices // steps
 
     def kernel(got_ref, other_ref, out_ref):
@@ -107,8 +107,8 @@
         far = other_ref[...].reshape(devices * kept, 2 * HEAD)
         asked_now = got_ref[pl.ds(step * chunk, chunk), kept:, :].reshape(chunk * part, 2 * HEAD)
         dims = (((1,), (1,)), ((), ()))
-        near_scores = lax.dot_general(asked_now, near, dims, preferred_element_type=jnp.float32) * scale
-        far_scores = lax.dot_general(asked_now, far, dims, preferred_element_type=jnp.float32) * scale
+        near_scores = lax.dot_general(asked_now, near, dims, preferred_element_type=jnp.float32)
+        far_scores = lax.dot_general(asked_now, far, dims, preferred_element_type=jnp.float32)
         highest = jnp.maximum(
             jnp.max(near_scores, axis=-1, keepdims=True), jnp.max(far_scores, axis=-1, keepdims=True)
         )

time: 158 us -> 156 us (0.987)
  Pallas kernels: 12.8 us -> 10.3 us
    pallas_call x1, Pallas kernels: 10.6 us -> 8.16 us  [attend_heads(): pl.pallas_call(kernel, grid=(steps,), in_specs=[pl.BlockSpec(got.shape, l...]
where the time goes in v9:
time: 156 us; the launch traced here: 155 us
  waiting for transfers between devices  40.7 us (26%)
  blocking collectives  36.2 us (23%)
  matrix products  29.3 us (19%)
  starting transfers between devices  19.5 us (12%)
  local copies, waits for them, and re-layouts  13.8 us (9%)
  Pallas kernels  10.3 us (7%)
  other arithmetic  4.09 us (3%)
    all_to_all x1, blocking collectives, to_experts(): lax.all_to_all(buffer, ('table', 'blk'), split_axis=0, concat_axis=0, til...  36.2 us
    all_to_all x1, waiting for transfers between devices, to_anchor(): lax.all_to_all(buffer, ('table', 'blk'), split_axis=0, concat_axis=0, til...  19.4 us
    all_to_all x1, waiting for transfers between devices, attend_heads(): got = lax.all_to_all(parcel, 'blk', 0, 0, tiled=True)  12.7 us
    all_to_all x1, starting transfers between devices, attend_heads(): got = lax.all_to_all(parcel, 'blk', 0, 0, tiled=True)  9.55 us
    pallas_call x1, Pallas kernels, attend_heads(): pl.pallas_call(kernel, grid=(steps,), in_specs=[pl.BlockSpec(got.shape, l...  8.16 us
    all_to_all x1, waiting for transfers between devices, attend_heads(): back = lax.all_to_all(mixed, 'blk', 0, 0, tiled=True)  7.58 us
    dot_general x2, matrix products, piece_pass(): jnp.einsum('scd,scf->df', inputs, grad_pre_up, preferred_element_type=jnp...  4.77 us
    dot_general x2, matrix products, piece_pass(): jnp.einsum('scf,scd->fd', hidden, cots, preferred_element_type=jnp.float32)  4.31 us
  transfers between devices with their start and end apart: 6, of which 4 were waited for; matrix products, arithmetic and copies ran while one was open for 15% of the time, Pallas kernels for 0%

profile of v9, /device:TPU:1, one launch (start us, length us, event | category | flops | bytes accessed | tf_op | source)
XLA Modules:
  0.0 155.1 jit_solution(3219578532940086613)
XLA Ops:
  0.7 2.2 %shard_map.146 = bf16[32,96,128]{2,1,0:T(8,128)(2,1)} custom-call(bf16[128,512]{1,0:T(8,128)(2,1)} %bitcast.130, bf16[128,512]{1,0:T(8,128)(2,1)} %bitcast.131, bf16[128,512]{1,0:T(8,128)(2,1)} %bitcast.132), custom_call_target="tpu_custom_call" | custom-call | tf_op jit(solution)/shard_map/pallas_call | solution.py:95
  2.8 9.6 %all-to-all-start = ((bf16[32,96,128]{2,1,0:T(8,128)(2,1)}), bf16[32,96,128]{2,1,0:T(8,128)(2,1)S(1)}, u32[]{:S(2)}, u32[]{:S(2)}) async-start(bf16[32,96,128]{2,1,0:T(8,128)(2,1)} %shard_map.146), calls=%async_computation | async-start | bytes 1572864 | tf_op jit(solution)/shard_map/all_to_all | solution.py:99
  13.9 12.7 %all-to-all-done.got_ref = bf16[32,96,128]{2,1,0:T(8,128)(2,1)S(1)} async-done(((bf16[32,96,128]{2,1,0:T(8,128)(2,1)}), bf16[32,96,128]{2,1,0:T(8,128)(2,1)S(1)}, u32[]{:S(2)}, u32[]{:S(2)}) %all-to-all-start) | async-done | bytes 786464 | tf_op jit(solution)/shard_map/all_to_all | solution.py:99
  28.0 1.0 broadcast_in_dim.27
  29.0 1.4 reshape.95
  30.6 8.2 %shard_map.147 = bf16[32,32,64]{2,1,0:T(8,128)(2,1)S(1)} custom-call(bf16[32,96,128]{2,1,0:T(8,128)(2,1)S(1)} %all-to-all-done.got_ref, bf16[32,64,128]{2,1,0:T(8,128)(2,1)S(1)} %collective-permute-done.other_ref), custom_call_target="tpu_custom_call" | custom-call | flops 2147483648 | bytes 1441792 | tf_op jit(solution)/shard_map/pallas_call | solution.py:125
  39.7 3.7 %all-to-all-start.1 = ((bf16[32,2,1024]{2,1,0:T(2,128)(2,1)}), bf16[32,2,1024]{2,1,0:T(2,128)(2,1)S(1)}, u32[]{:S(2)}, u32[]{:S(2)}) async-start(bf16[32,2,1024]{2,1,0:T(2,128)(2,1)} %reshape.112), calls=%async_computation.1 | async-start | bytes 262144 | tf_op jit(solution)/shard_map/all_to_all | solution.py:141
  43.4 7.6 %all-to-all-done.1 = bf16[32,2,1024]{2,1,0:T(2,128)(2,1)S(1)} async-done(((bf16[32,2,1024]{2,1,0:T(2,128)(2,1)}), bf16[32,2,1024]{2,1,0:T(2,128)(2,1)S(1)}, u32[]{:S(2)}, u32[]{:S(2)}) %all-to-all-start.1) | async-done | bytes 131104 | tf_op jit(solution)/shard_map/all_to_all | solution.py:141
  53.8 36.2 %all_to_all.20 = bf16[128,6,1024]{2,1,0:T(8,128)(2,1)S(1)} all-to-all(bf16[128,6,1024]{2,1,0:T(8,128)(2,1)S(1)} %copy.39), channel_id=1, replica_groups=mesh['table'=4,'blk'=32] {'table','blk'}, dimensions={0} | all-to-all | bytes 3145728 | tf_op jit(solution)/shard_map/all_to_all | solution.py:26
  90.9 1.2 collective-permute-start.1
  92.1 1.0 fusion.11
  93.2 1.0 fusion.26
  94.1 1.0 collective-permute-done.1
  95.2 1.0 fusion.8
  96.2 1.0 fusion.22
  97.2 2.1 %multiply_convert_fusion.2 = (bf16[128,6,1024]{2,0,1:T(8,128)(2,1)S(1)}, bf16[128,6,1024]{2,0,1:T(8,128)(2,1)S(1)}, bf16[128,6,1024]{2,0,1:T(8,128)(2,1)S(1)}) fusion(f32[128,6,1024]{2,0,1:T(8,128)S(1)} %fusion.22, f32[128,6,1024]{2,0,1:T(8,128)S(1)} %fusion.8, bf16[1,512,1024]{2,1,0:T(8,128)(2,1)S(1)} %copy-done, ...), kind=kOutput, calls=%fused_computation.3 | convolution fusion | flops 817102848 | bytes 12845056 | tf_op jit(solution)/shard_map/scd,df->scf/dot_general | solution.py:46
  101.0 1.0 fusion.20
  102.0 1.0 add_convert_fusion.1
  103.9 2.1 %multiply_convert_fusion.5 = (bf16[128,6,1024]{2,0,1:T(8,128)(2,1)S(1)}, bf16[128,6,1024]{2,0,1:T(8,128)(2,1)S(1)}, bf16[128,6,1024]{2,0,1:T(8,128)(2,1)S(1)}) fusion(f32[128,6,1024]{2,0,1:T(8,128)S(1)} %fusion.26, f32[128,6,1024]{2,0,1:T(8,128)S(1)} %fusion.11, bf16[1,512,1024]{2,1,0:T(8,128)(2,1)S(1)} %copy-done, bf16[128,6,1024]{2,0,1:T(8,128)(2,1)S(1)} %copy.40), kind=kOutput, calls=%fused_computation.8 | convolution fusion | flops 817102848 | bytes 12845056 | tf_op jit(solution)/shard_map/scd,df->scf/dot_general | solution.py:46
  107.3 1.0 fusion.24
  108.3 2.3 %fusion.32 = f32[1024,512,1]{1,0,2:T(8,128)} fusion(bf16[128,6,1024]{2,0,1:T(8,128)(2,1)S(1)} %get-tuple-element.5, bf16[128,6,1024]{2,0,1:T(8,128)(2,1)S(1)} %copy.40), kind=kOutput, calls=%fused_computation.52 | convolution fusion | flops 805306368 | bytes 4456448 | tf_op jit(solution)/shard_map/scf,scd->fd/dot_general | solution.py:59
  110.6 1.0 add_convert_fusion.2
  112.2 2.2 %copy.43 = bf16[128,6,1024]{2,1,0:T(8,128)(2,1)} copy(bf16[128,6,1024]{2,0,1:T(8,128)(2,1)S(1)} %add_convert_fusion) | data formatting | bytes 3145728 | tf_op jit(solution)/shard_map/convert_element_type | solution.py:191
  114.5 3.8 %all-to-all-start.3 = ((bf16[128,6,1024]{2,1,0:T(8,128)(2,1)}), bf16[128,6,1024]{2,1,0:T(8,128)(2,1)S(1)}, u32[]{:S(2)}, u32[]{:S(2)}) async-start(bf16[128,6,1024]{2,1,0:T(8,128)(2,1)} %copy.43), calls=%async_computation.3 | async-start | bytes 4194304 | tf_op jit(solution)/shard_map/all_to_all | solution.py:30
  118.3 2.8 %fusion.41 = f32[512,1024,1]{1,0,2:T(8,128)S(1)} fusion(bf16[128,6,1024]{2,0,1:T(8,128)(2,1)} %copy-done.21, bf16[128,6,1024]{2,0,1:T(8,128)(2,1)} %copy-done.1), kind=kOutput, calls=%fused_computation.64 | convolution fusion | flops 805306368 | bytes 4456448 | tf_op jit(solution)/shard_map/scd,scf->df/dot_general | solution.py:61
  121.2 1.0 fusion.43
  123.3 2.0 %fusion.7 = bf16[1,1024,512]{2,1,0:T(8,128)(2,1)} fusion(bf16[128,6,1024]{2,0,1:T(8,128)(2,1)S(1)} %copy-done.18, f32[1024,512,1]{1,0,2:T(8,128)S(1)} %copy-done.12, bf16[128,6,1024]{2,0,1:T(8,128)(2,1)S(1)} %copy-done.6), kind=kOutput, calls=%fused_computation.25 | convolution fusion | flops 806354944 | bytes 5505024 | tf_op jit(solution)/shard_map/scf,scd->fd/dot_general | solution.py:59
  125.3 2.0 %fusion.6 = bf16[1,512,1024]{2,1,0:T(8,128)(2,1)} fusion(bf16[128,6,1024]{2,0,1:T(8,128)(2,1)S(1)} %copy-done.16, f32[512,1024,1]{1,0,2:T(8,128)S(1)} %fusion.41, bf16[128,6,1024]{2,0,1:T(8,128)(2,1)S(1)} %copy-done.6), kind=kOutput, calls=%fused_computation.24 | convolution fusion | flops 806354944 | bytes 5505024 | tf_op jit(solution)/shard_map/scd,scf->df/dot_general | solution.py:61
  127.2 2.0 %fusion.5 = bf16[1,512,1024]{2,1,0:T(8,128)(2,1)} fusion(bf16[128,6,1024]{2,0,1:T(8,128)(2,1)S(1)} %copy-done.14, f32[512,1024,1]{1,0,2:T(8,128)S(1)} %fusion.43, bf16[128,6,1024]{2,0,1:T(8,128)(2,1)S(1)} %copy-done.6), kind=kOutput, calls=%fused_computation.23 | convolution fusion | flops 806354944 | bytes 5505024 | tf_op jit(solution)/shard_map/scd,scf->df/dot_general | solution.py:60
  129.2 19.4 %all-to-all-done.3 = bf16[128,6,1024]{2,1,0:T(8,128)(2,1)S(1)} async-done(((bf16[128,6,1024]{2,1,0:T(8,128)(2,1)}), bf16[128,6,1024]{2,1,0:T(8,128)(2,1)S(1)}, u32[]{:S(2)}, u32[]{:S(2)}) %all-to-all-start.3) | async-done | bytes 1572896 | tf_op jit(solution)/shard_map/all_to_all | solution.py:30
  148.6 1.4 reshape.96
  150.1 2.0 %fusion.28 = f32[256,1024]{1,0:T(8,128)S(1)} fusion(bf16[768,1024]{1,0:T(8,128)(2,1)} %reshape.96, s32[256]{0:T(256)S(1)} %multiply_add_fusion.1), kind=kOutput, calls=%fused_computation.48 | convolution fusion | flops 402849792 | bytes 2622464 | tf_op jit(solution)/shard_map/dot_general | solution.py:194
  (88 shorter events, 16.0 us)
Async XLA Ops:
  0.6 96.5 %copy-start = (bf16[1,512,1024]{2,1,0:T(8,128)(2,1)S(1)}, bf16[1,512,1024]{2,1,0:T(8,128)(2,1)}, u32[]{:S(2)}) copy-start(bf16[1,512,1024]{2,1,0:T(8,128)(2,1)} %param.20) | copy-start | bytes 3145732
  0.6 11.8 %copy-start.10 = (s32[1,128,2]{1,2,0:T(2,128)S(1)}, s32[1,128,2]{1,2,0:T(2,128)}, u32[]{:S(2)}) copy-start(s32[1,128,2]{1,2,0:T(2,128)} %param.16) | copy-start | bytes 3076
  0.7 13.0 %copy-start.11 = (f32[1,128,2]{1,2,0:T(2,128)S(1)}, f32[1,128,2]{1,2,0:T(2,128)}, u32[]{:S(2)}) copy-start(f32[1,128,2]{1,2,0:T(2,128)} %param.17) | copy-start | bytes 3076
  2.8 25.2 %copy-start.8 = (bf16[1,128,512]{2,1,0:T(8,128)(2,1)S(1)}, bf16[1,128,512]{2,1,0:T(8,128)(2,1)}, u32[]{:S(2)}) copy-start(bf16[1,128,512]{2,1,0:T(8,128)(2,1)} %param.18) | copy-start | bytes 393220
  2.8 23.8 %all-to-all-start = ((bf16[32,96,128]{2,1,0:T(8,128)(2,1)}), bf16[32,96,128]{2,1,0:T(8,128)(2,1)S(1)}, u32[]{:S(2)}, u32[]{:S(2)}) async-start(bf16[32,96,128]{2,1,0:T(8,128)(2,1)} %shard_map.146), calls=%async_computation | async-start | bytes 1572864 | tf_op jit(solution)/shard_map/all_to_all | solution.py:99
  27.5 3.1 %collective-permute-start = (bf16[32,64,128]{2,1,0:T(8,128)(2,1)}, bf16[32,64,128]{2,1,0:T(8,128)(2,1)S(1)}, u32[]{:S(2)}, u32[]{:S(2)}) collective-permute-start(bf16[32,64,128]{2,1,0:T(8,128)(2,1)} %slice.36), channel_id=1, source_target_pairs={{0,1},{1,0},{2,3},{3,2},{4,5},{5,4},{6,7},{7,6},{8,9},{9,8},{10,11... | collective-permute-start | bytes 1572872 | tf_op jit(solution)/shard_map/ppermute | solution.py:100
  38.8 12.8 %copy-start.7 = (bf16[512,512]{1,0:T(8,128)(2,1)S(1)}, bf16[512,512]{1,0:T(8,128)(2,1)}, u32[]{:S(2)}) copy-start(bf16[512,512]{1,0:T(8,128)(2,1)} %param.15) | copy-start | bytes 1572868
  38.8 12.8 %copy-start.9 = (bf16[1,128,512]{2,1,0:T(8,128)(2,1)S(1)}, bf16[1,128,512]{2,1,0:T(8,128)(2,1)}, u32[]{:S(2)}) copy-start(bf16[1,128,512]{2,1,0:T(8,128)(2,1)} %param.11) | copy-start | bytes 393220
  39.7 11.3 %all-to-all-start.1 = ((bf16[32,2,1024]{2,1,0:T(2,128)(2,1)}), bf16[32,2,1024]{2,1,0:T(2,128)(2,1)S(1)}, u32[]{:S(2)}, u32[]{:S(2)}) async-start(bf16[32,2,1024]{2,1,0:T(2,128)(2,1)} %reshape.112), calls=%async_computation.1 | async-start | bytes 262144 | tf_op jit(solution)/shard_map/all_to_all | solution.py:141
  90.0 2.1 %copy-start.3 = (bf16[1,1024,512]{2,1,0:T(8,128)(2,1)S(1)}, bf16[1,1024,512]{2,1,0:T(8,128)(2,1)}, u32[]{:S(2)}) copy-start(bf16[1,1024,512]{2,1,0:T(8,128)(2,1)} %param.21) | copy-start | bytes 3145732
  90.9 17.4 %copy-start.1 = (bf16[128,6,1024]{2,0,1:T(8,128)(2,1)}, bf16[128,6,1024]{2,0,1:T(8,128)(2,1)S(1)}, u32[]{:S(2)}) copy-start(bf16[128,6,1024]{2,0,1:T(8,128)(2,1)S(1)} %copy.40) | copy-start | bytes 4718596
  90.9 2.3 %copy-start.4 = (bf16[1,512,1024]{2,1,0:T(8,128)(2,1)S(1)}, bf16[1,512,1024]{2,1,0:T(8,128)(2,1)}, u32[]{:S(2)}) copy-start(bf16[1,512,1024]{2,1,0:T(8,128)(2,1)} %param.19) | copy-start | bytes 3145732
  90.9 4.3 %collective-permute-start.1 = (bf16[128,6,1024]{2,0,1:T(8,128)(2,1)S(1)}, bf16[128,6,1024]{2,0,1:T(8,128)(2,1)S(1)}, u32[]{:S(2)}, u32[]{:S(2)}) collective-permute-start(bf16[128,6,1024]{2,0,1:T(8,128)(2,1)S(1)} %copy.40), channel_id=1, source_target_pairs={{0,1},{1,0},{2,3},{3,2},{4,5},{5,4},{6,7},{7,6},{8,9},{9,8},{10,11... | collective-permute-start | bytes 4718600 | tf_op jit(solution)/shard_map/ppermute | solution.py:40
  95.2 2.0 %copy-start.5 = (bf16[128,6,1024]{2,0,1:T(8,128)(2,1)}, bf16[128,6,1024]{2,0,1:T(8,128)(2,1)S(1)}, u32[]{:S(2)}) copy-start(bf16[128,6,1024]{2,0,1:T(8,128)(2,1)S(1)} %collective-permute-done.1) | copy-start | bytes 4718596
  99.3 1.2 copy-start.17
  99.3 1.6 %copy-start.13 = (bf16[128,6,1024]{2,0,1:T(8,128)(2,1)}, bf16[128,6,1024]{2,0,1:T(8,128)(2,1)S(1)}, u32[]{:S(2)}) copy-start(bf16[128,6,1024]{2,0,1:T(8,128)(2,1)S(1)} %get-tuple-element.9) | copy-start | bytes 4718596
  99.3 2.6 %copy-start.15 = (bf16[128,6,1024]{2,0,1:T(8,128)(2,1)}, bf16[128,6,1024]{2,0,1:T(8,128)(2,1)S(1)}, u32[]{:S(2)}) copy-start(bf16[128,6,1024]{2,0,1:T(8,128)(2,1)S(1)} %get-tuple-element.10) | copy-start | bytes 4718596
  103.2 8.4 %collective-permute-start.2 = (bf16[128,6,1024]{2,0,1:T(8,128)(2,1)S(1)}, bf16[128,6,1024]{2,0,1:T(8,128)(2,1)S(1)}, u32[]{:S(2)}, u32[]{:S(2)}) collective-permute-start(bf16[128,6,1024]{2,0,1:T(8,128)(2,1)S(1)} %pad_maximum_fusion), channel_id=1, source_target_pairs={{0,1},{1,0},{2,3},{3,2},{4,5},{5,4},{6,7},{7,6},{8,9},{9,8},{10,11... | collective-permute-start | bytes 4718600 | tf_op jit(solution)/shard_map/ppermute | solution.py:190
  106.0 1.2 copy-start.19
  106.0 4.6 %copy-start.21 = (bf16[128,6,1024]{2,0,1:T(8,128)(2,1)}, bf16[128,6,1024]{2,0,1:T(8,128)(2,1)S(1)}, u32[]{:S(2)}) copy-start(bf16[128,6,1024]{2,0,1:T(8,128)(2,1)S(1)} %get-tuple-element.7) | copy-start | bytes 4718596
  114.5 34.2 %all-to-all-start.3 = ((bf16[128,6,1024]{2,1,0:T(8,128)(2,1)}), bf16[128,6,1024]{2,1,0:T(8,128)(2,1)S(1)}, u32[]{:S(2)}, u32[]{:S(2)}) async-start(bf16[128,6,1024]{2,1,0:T(8,128)(2,1)} %copy.43), calls=%async_computation.3 | async-start | bytes 4194304 | tf_op jit(solution)/shard_map/all_to_all | solution.py:30
  118.3 2.8 %copy-start.2 = (bf16[128,6,1024]{2,0,1:T(8,128)(2,1)S(1)}, bf16[128,6,1024]{2,0,1:T(8,128)(2,1)}, u32[]{:S(2)}) copy-start(bf16[128,6,1024]{2,0,1:T(8,128)(2,1)} %copy-done.1) | copy-start | bytes 4718596
  118.3 2.8 %copy-start.20 = (bf16[128,6,1024]{2,0,1:T(8,128)(2,1)S(1)}, bf16[128,6,1024]{2,0,1:T(8,128)(2,1)}, u32[]{:S(2)}) copy-start(bf16[128,6,1024]{2,0,1:T(8,128)(2,1)} %copy-done.19) | copy-start | bytes 4718596
  118.3 3.9 %copy-start.18 = (bf16[128,6,1024]{2,0,1:T(8,128)(2,1)S(1)}, bf16[128,6,1024]{2,0,1:T(8,128)(2,1)}, u32[]{:S(2)}) copy-start(bf16[128,6,1024]{2,0,1:T(8,128)(2,1)} %copy-done.17) | copy-start | bytes 4718596
  121.1 1.5 copy-start.6
  121.2 2.1 %copy-start.12 = (f32[1024,512,1]{1,0,2:T(8,128)S(1)}, f32[1024,512,1]{1,0,2:T(8,128)}, u32[]{:S(2)}) copy-start(f32[1024,512,1]{1,0,2:T(8,128)} %fusion.32) | copy-start | bytes 6291460
  123.3 2.0 %copy-start.16 = (bf16[128,6,1024]{2,0,1:T(8,128)(2,1)S(1)}, bf16[128,6,1024]{2,0,1:T(8,128)(2,1)}, u32[]{:S(2)}) copy-start(bf16[128,6,1024]{2,0,1:T(8,128)(2,1)} %copy-done.15) | copy-start | bytes 4718596
  125.3 2.0 %copy-start.14 = (bf16[128,6,1024]{2,0,1:T(8,128)(2,1)S(1)}, bf16[128,6,1024]{2,0,1:T(8,128)(2,1)}, u32[]{:S(2)}) copy-start(bf16[128,6,1024]{2,0,1:T(8,128)(2,1)} %copy-done.13) | copy-start | bytes 4718596
